TPU v7x, 256 devices: a whole 4x4x8 slice. The times are simulated.
256 devices in a mesh: row: 8 (over z), col: 32 (over y, x, core).
Axes of the slice: x: 4, y: 4, z: 8, core: 2. Of those that a mesh axis runs over, the one named last changes fastest.
Arguments:
- features: bfloat16 [32768, 128], P(('row', 'col')), may hold values from -6 to 6
- first_weight: bfloat16 [128, 512], replicated, may hold values from -0.5 to 0.5
- second_weight: bfloat16 [512, 128], replicated, may hold values from -0.25 to 0.25
- tile_rows: int32 [8, 32, 80], P('row', 'col'), may hold values from 0 to 31
- tile_cols: int32 [8, 32, 80], P('row', 'col'), may hold values from 0 to 7
- tile_live: int32 [8, 32], P('row', 'col'), may hold values from 1 to 80, as said below
- column_mask: int32 [8, 32, 80, 128], P('row', 'col'), may hold values 0 or 1
- edge_weight: bfloat16 [8, 32, 80, 128, 128], P('row', 'col'), may hold values from 0.049804688 to 1
- cotangent: bfloat16 [32768, 128], P(('row', 'col')), may hold values from -6 to 6
Outputs:
- output: bfloat16 [32768, 128], P(('row', 'col'))
- first_grad: float32 [128, 512], replicated
- second_grad: float32 [512, 128], replicated
Inputs may be any that keep to these rules, and one draw needn't show every extreme that they name: `tile_live`: slots at or past a device's count are unused; every device of the last column group of the grid uses all 80.
All inputs are finite; a program needn't handle non-finite values. No bound on the sum of `column_mask` on one device may be relied on, other than what follows from the above.
Results may differ from a plain program's by a relative error of at most 0.014.
Values may be sent and summed in bfloat16 or wider, within the bound.
No kernel may reach another device: no remote copies, remote signals or barrier semaphores. Data moves between devices by JAX's collectives and lax.ppermute only.
A program may use at most 128 MiB of HBM per device.

v0:
```python
import math

import jax
import jax.numpy as jnp
from jax import lax
from jax.sharding import PartitionSpec as P

BLOCK = 128


gelu_coef = math.sqrt(2.0 / math.pi)


def gelu_tanh(value):
    return 0.5 * value * (1.0 + jnp.tanh(gelu_coef * (value + 0.044715 * value * value * value)))


def gelu_slope(value):
    tanh_value = jnp.tanh(gelu_coef * (value + 0.044715 * value * value * value))
    return 0.5 * (1.0 + tanh_value) + 0.5 * value * (1.0 - tanh_value * tanh_value) * gelu_coef * (
        1.0 + 3.0 * 0.044715 * value * value
    )


def slot_batches(tile_values, target_index, source_index):
    slot_count = tile_values.shape[0]
    group_size = 16
    batches = slot_count // group_size
    return (
        tile_values.reshape(batches, group_size, BLOCK, BLOCK),
        target_index.reshape(batches, group_size),
        source_index.reshape(batches, group_size),
    )


def forward_part(tile_values, row_index, col_index, panel, target_blocks):
    feature_width = panel.shape[1]
    source_blocks = panel.reshape(-1, BLOCK, feature_width)

    def forward_accumulate(running, slot_piece):
        values_here, rows_here, cols_here = slot_piece
        contrib = jnp.einsum(
            "sij,sjf->sif",
            values_here,
            source_blocks[cols_here],
            preferred_element_type=jnp.float32,
        )
        return (running.at[rows_here].add(contrib), None)

    start = jnp.zeros((target_blocks, BLOCK, feature_width), jnp.float32)
    running, _ = lax.scan(
        forward_accumulate, start, slot_batches(tile_values, row_index, col_index)
    )
    return running.reshape(-1, feature_width)


def backward_part(tile_values, col_index, row_index, panel, target_blocks):
    feature_width = panel.shape[1]
    source_blocks = panel.reshape(-1, BLOCK, feature_width)

    def backward_accumulate(running, slot_piece):
        values_here, cols_here, rows_here = slot_piece
        contrib = jnp.einsum(
            "sij,sif->sjf",
            values_here,
            source_blocks[rows_here],
            preferred_element_type=jnp.float32,
        )
        return (running.at[cols_here].add(contrib), None)

    start = jnp.zeros((target_blocks, BLOCK, feature_width), jnp.float32)
    running, _ = lax.scan(
        backward_accumulate, start, slot_batches(tile_values, col_index, row_index)
    )
    return running.reshape(-1, feature_width)


def local(
    features,
    first_weight,
    second_weight,
    tile_rows,
    tile_cols,
    tile_live,
    column_mask,
    edge_weight,
    cotangent,
):
    slot_count = edge_weight.shape[2]
    node_count = features.shape[0]
    live_slots = (jnp.arange(slot_count, dtype=jnp.int32) < tile_live[0, 0]).astype(jnp.bfloat16)
    tile_values = (
        edge_weight[0, 0]
        * column_mask[0, 0].astype(jnp.bfloat16)[:, None, :]
        * live_slots[:, None, None]
    )
    row_index = tile_rows[0, 0]
    col_index = tile_cols[0, 0]
    row_groups = lax.axis_size("col") * node_count // BLOCK
    col_groups = lax.axis_size("row") * node_count // BLOCK
    row_sums = jnp.sum(tile_values.astype(jnp.float32), axis=2)
    degree_part = (
        jnp.zeros((row_groups, BLOCK), jnp.float32).at[row_index].add(row_sums).reshape(-1)
    )
    panel_in = lax.all_gather(features, "row", axis=0, tiled=True)
    partial_in = forward_part(tile_values, row_index, col_index, panel_in, row_groups)
    degree = lax.psum_scatter(degree_part, "col", scatter_dimension=0, tiled=True)
    summed_in = lax.psum_scatter(
        partial_in.astype(jnp.bfloat16), "col", scatter_dimension=0, tiled=True
    ).astype(jnp.float32)
    row_scale = (1.0 / jnp.sqrt(1.0 + degree))[:, None]
    first_mix = (features.astype(jnp.float32) + row_scale * summed_in).astype(jnp.bfloat16)
    first_pre = jnp.dot(first_mix, first_weight, preferred_element_type=jnp.float32)
    hidden = gelu_tanh(first_pre).astype(jnp.bfloat16)
    panel_hidden = lax.all_gather(hidden, "row", axis=0, tiled=True)
    partial_hidden = forward_part(tile_values, row_index, col_index, panel_hidden, row_groups)
    summed_hidden = lax.psum_scatter(
        partial_hidden.astype(jnp.bfloat16), "col", scatter_dimension=0, tiled=True
    ).astype(jnp.float32)
    second_mix = (hidden.astype(jnp.float32) + row_scale * summed_hidden).astype(jnp.bfloat16)
    output = jnp.dot(second_mix, second_weight, preferred_element_type=jnp.float32).astype(
        jnp.bfloat16
    )
    mix_grad = jnp.einsum("no,ho->nh", cotangent, second_weight, preferred_element_type=jnp.float32)
    scaled_grad = (row_scale * mix_grad).astype(jnp.bfloat16)
    grad_rows = lax.all_gather(scaled_grad, "col", axis=0, tiled=True)
    returned = lax.psum_scatter(
        backward_part(tile_values, col_index, row_index, grad_rows, col_groups).astype(
            jnp.bfloat16
        ),
        "row",
        scatter_dimension=0,
        tiled=True,
    ).astype(jnp.float32)
    hidden_grad = mix_grad + returned
    second_term = jnp.einsum("nh,no->ho", second_mix, cotangent, preferred_element_type=jnp.float32)
    pre_grad = (hidden_grad * gelu_slope(first_pre)).astype(jnp.bfloat16)
    first_term = jnp.einsum("ni,nh->ih", first_mix, pre_grad, preferred_element_type=jnp.float32)
    node_scale = 1.0 / math.sqrt(node_count * lax.axis_size("row") * lax.axis_size("col"))
    first_grad, second_grad = lax.psum(
        (first_term * node_scale, second_term * node_scale), ("row", "col")
    )
    return (output, first_grad, second_grad)


def solution(mesh):
    return jax.shard_map(
        local,
        mesh=mesh,
        in_specs=(
            P(("row", "col"), None),
            P(),
            P(),
            P("row", "col", None),
            P("row", "col", None),
            P("row", "col"),
            P("row", "col", None, None),
            P("row", "col", None, None, None),
            P(("row", "col"), None),
        ),
        out_specs=(P(("row", "col"), None), P(), P()),
        check_vma=False,
    )
```

profile of v0, /device:TPU:1, one launch (start us, length us, event | category | flops | bytes accessed | tf_op | source)
XLA Modules:
  0.0 727.7 jit_solution(3400894786560194901)
XLA Ops:
  8.4 1.3 reduce.7
  9.7 1.3 reduce.6
  11.2 0.8 convert_element_type.79
  12.0 23.5 %all_gather.9 = bf16[1024,128]{1,0:T(8,128)(2,1)S(1)} all-gather(bf16[128,128]{1,0:T(8,128)(2,1)} %param.15), channel_id=1, replica_groups=mesh['row'=8,'col'=32] {'row'}, dimensions={0}, use_global_device_ids=true | all-gather | bytes 294912 | tf_op jit(solution)/shard_map/all_gather | solution.py:105
  35.5 4.4 copy.15
  39.8 4.0 multiply_multiply_fusion
  43.8 4.4 copy.16
  48.2 1.6 broadcast_in_dim.11
  49.8 26.7 %while.30 = (s32[]{:T(128)}, f32[32,128,128]{2,1,0:T(8,128)}, s32[5,16]{1,0:T(8,128)S(1)}, bf16[5,16,128,128]{3,2,1,0:T(8,128)(2,1)}, s32[5,16]{1,0:T(8,128)S(1)}, /*index=5*/bf16[8,128,128]{2,1,0:T(8,128)(2,1)S(1)}, s32[]{:T(128)}) while((s32[]{:T(128)}, f32[32,128,128]{2,1,0:T(8,128)}, s32[5,16]{1,0:T(8,128)S(1)}, ...), condition=%wide.region_5.6_spmd, body=%wide.region_3.0_spmd.sunk | while | flops 67372128 | bytes 6296093 | solution.py:51
  50.4 1.3 fusion.67
  51.8 3.3 scatter_fusion
  55.8 1.3 fusion.67
  57.1 3.3 scatter_fusion
  61.1 1.3 fusion.67
  62.5 3.3 scatter_fusion
  66.5 1.3 fusion.67
  67.8 3.3 scatter_fusion
  71.8 1.3 fusion.67
  73.1 3.3 scatter_fusion
  76.5 2.9 convert_element_type.85
  80.8 1.8 convert_reduce_fusion
  82.6 0.8 scatter_custom_fusion.3
  83.4 125.2 %all-reduce = f32[4096]{0:T(1024)S(1)} all-reduce(f32[4096]{0:T(1024)S(1)} %bitcast.122), channel_id=2, replica_groups=mesh['row'=8,'col'=32] {'col'}, use_global_device_ids=true, to_apply=%region_2.3.clone | all-reduce | flops 4096 | bytes 32768
  208.7 1.7 multiply_convert_fusion.1
  210.5 0.9 multiply_convert_fusion
  211.5 31.6 %all-gather.3.cloned.1.call-done = bf16[1024,512]{1,0:T(8,128)(2,1)} async-done(((bf16[128,512]{1,0:T(8,128)(2,1)}), bf16[1024,512]{1,0:T(8,128)(2,1)}) %all-gather.3.cloned.1.call-update) | async-done | bytes 1048592 | tf_op jit(solution)/shard_map/all_gather | solution.py:115
  243.1 4.3 broadcast_in_dim.12
  247.4 69.8 %while.31 = (s32[]{:T(128)}, f32[32,128,512]{2,1,0:T(8,128)}, s32[5,16]{1,0:T(8,128)S(1)}, bf16[5,16,128,128]{3,2,1,0:T(8,128)(2,1)}, s32[5,16]{1,0:T(8,128)S(1)}, /*index=5*/bf16[8,128,512]{2,1,0:T(8,128)(2,1)S(1)}, s32[]{:T(128)}) while((s32[]{:T(128)}, f32[32,128,512]{2,1,0:T(8,128)}, s32[5,16]{1,0:T(8,128)S(1)}, ...), condition=%wide.region_9.10_spmd, body=%wide.region_7.9_spmd.sunk | while | flops 269485152 | bytes 23597596 | solution.py:51
  248.1 3.7 fusion.71
  251.8 9.7 %scatter_fusion.1 = f32[32,128,512]{2,1,0:T(8,128)} fusion(f32[32,128,512]{2,1,0:T(8,128)} %get-tuple-element.326, s32[16]{0:T(128)S(1)} %get-tuple-element.287, f32[16,128,512]{2,1,0:T(8,128)} %fusion.71), kind=kCustom, calls=%fused_computation.4.clone.1 | custom fusion | flops 1048576 | bytes 12582976 | tf_op jit(solution)/shard_map/while/body/eval_jaxpr/scatter-add | solution.py:48
  262.1 3.7 fusion.71
  265.8 9.6 %scatter_fusion.1 = f32[32,128,512]{2,1,0:T(8,128)} fusion(f32[32,128,512]{2,1,0:T(8,128)} %get-tuple-element.326, s32[16]{0:T(128)S(1)} %get-tuple-element.287, f32[16,128,512]{2,1,0:T(8,128)} %fusion.71), kind=kCustom, calls=%fused_computation.4.clone.1 | custom fusion | flops 1048576 | bytes 12582976 | tf_op jit(solution)/shard_map/while/body/eval_jaxpr/scatter-add | solution.py:48
  276.1 3.7 fusion.71
  279.8 9.5 %scatter_fusion.1 = f32[32,128,512]{2,1,0:T(8,128)} fusion(f32[32,128,512]{2,1,0:T(8,128)} %get-tuple-element.326, s32[16]{0:T(128)S(1)} %get-tuple-element.287, f32[16,128,512]{2,1,0:T(8,128)} %fusion.71), kind=kCustom, calls=%fused_computation.4.clone.1 | custom fusion | flops 1048576 | bytes 12582976 | tf_op jit(solution)/shard_map/while/body/eval_jaxpr/scatter-add | solution.py:48
  290.0 3.7 fusion.71
  293.7 9.5 %scatter_fusion.1 = f32[32,128,512]{2,1,0:T(8,128)} fusion(f32[32,128,512]{2,1,0:T(8,128)} %get-tuple-element.326, s32[16]{0:T(128)S(1)} %get-tuple-element.287, f32[16,128,512]{2,1,0:T(8,128)} %fusion.71), kind=kCustom, calls=%fused_computation.4.clone.1 | custom fusion | flops 1048576 | bytes 12582976 | tf_op jit(solution)/shard_map/while/body/eval_jaxpr/scatter-add | solution.py:48
  303.9 3.7 fusion.71
  307.6 9.6 %scatter_fusion.1 = f32[32,128,512]{2,1,0:T(8,128)} fusion(f32[32,128,512]{2,1,0:T(8,128)} %get-tuple-element.326, s32[16]{0:T(128)S(1)} %get-tuple-element.287, f32[16,128,512]{2,1,0:T(8,128)} %fusion.71), kind=kCustom, calls=%fused_computation.4.clone.1 | custom fusion | flops 1048576 | bytes 12582976 | tf_op jit(solution)/shard_map/while/body/eval_jaxpr/scatter-add | solution.py:48
  317.1 5.9 convert_element_type.91
  323.4 74.4 %while.32 = (s32[]{:T(128)}, f32[8,128,512]{2,1,0:T(8,128)S(1)}, s32[5,16]{1,0:T(8,128)S(1)}, bf16[5,16,128,128]{2,3,1,0:T(8,128)(2,1)}, s32[5,16]{1,0:T(8,128)S(1)}, /*index=5*/bf16[32,128,512]{2,1,0:T(8,128)(2,1)}, s32[]{:T(128)}) while((s32[]{:T(128)}, f32[8,128,512]{2,1,0:T(8,128)S(1)}, s32[5,16]{1,0:T(8,128)S(1)}, ...), condition=%wide.region_13.14_spmd, body=%wide.region_11.13_spmd.sunk | while | flops 269485152 | bytes 23597596 | solution.py:72
  323.5 4.2 gather_fusion.2
  327.7 4.4 fusion.75
  332.1 6.1 scatter_fusion.2
  338.2 4.2 gather_fusion.2
  342.4 4.5 fusion.75
  346.9 6.2 scatter_fusion.2
  353.2 4.3 gather_fusion.2
  357.5 4.5 fusion.75
  361.9 6.2 scatter_fusion.2
  368.2 4.2 gather_fusion.2
  372.4 4.4 fusion.75
  376.8 6.1 scatter_fusion.2
  382.9 4.3 gather_fusion.2
  387.2 4.5 fusion.75
  391.7 6.2 scatter_fusion.2
  397.9 1.1 convert_element_type.97
  399.1 16.7 %reduce-scatter.6.cloned.1.call-done = bf16[128,512]{1,0:T(8,128)(2,1)} async-done(((bf16[4096,512]{1,0:T(8,128)(2,1)}), bf16[128,512]{1,0:T(8,128)(2,1)}) %reduce-scatter.6.cloned.1.call-update) | async-done | bytes 131088 | tf_op jit(solution)/shard_map/reduce_scatter | solution.py:117
  415.8 2.0 convolution_multiply_fusion
  417.8 35.6 %reduce-scatter.8.cloned.1.call-done = bf16[128,512]{1,0:T(8,128)(2,1)} async-done(((bf16[1024,512]{1,0:T(8,128)(2,1)}), bf16[128,512]{1,0:T(8,128)(2,1)}) %reduce-scatter.8.cloned.1.call-update) | async-done | bytes 131088 | tf_op jit(solution)/shard_map/reduce_scatter | solution.py:127
  453.4 2.0 convolution_multiply_fusion.1
  455.4 0.9 convolution_convert_fusion
  456.3 261.2 %all-reduce.4.cloned.1.call-done = (f32[128,512]{1,0:T(8,128)}, f32[512,128]{1,0:T(8,128)}) async-done(((f32[128,512]{1,0:T(8,128)}, f32[512,128]{1,0:T(8,128)}), (f32[128,512]{1,0:T(8,128)}, f32[512,128]{1,0:T(8,128)})) %all-reduce.4.cloned.1.call-update) | async-done | bytes 524304 | tf_op jit(solution)/shard_map/psum | solution.py:140
  717.5 1.7 copy.43
  719.2 1.7 copy.44
  (98 shorter events, 8.9 us)
Async XLA Ops:
  7.2 203.4 %copy-start = (bf16[512,128]{1,0:T(8,128)(2,1)S(1)}, bf16[512,128]{1,0:T(8,128)(2,1)}, u32[]{:S(2)}) copy-start(bf16[512,128]{1,0:T(8,128)(2,1)} %param.17) | copy-start | bytes 393220
  7.2 201.5 %reduce-scatter.4.cloned.1.call-start = ((), (), s32[]{:S(2)}) async-start(), calls=%async_computation.3 | async-start | bytes 1081344 | tf_op jit(solution)/shard_map/reduce_scatter | solution.py:108
  76.5 3.0 copy-start.15
  76.5 4.2 copy-start.14
  76.5 4.3 copy-start.5
  76.5 4.3 copy-start.2
  79.4 129.3 %copy-start.8 = (bf16[128,128]{1,0:T(8,128)(2,1)S(1)}, bf16[128,128]{1,0:T(8,128)(2,1)}, u32[]{:S(2)}) copy-start(bf16[128,128]{1,0:T(8,128)(2,1)} %param.15) | copy-start | bytes 98308
  79.4 129.3 %copy-start.12 = (bf16[128,512]{1,0:T(8,128)(2,1)S(1)}, bf16[128,512]{1,0:T(8,128)(2,1)}, u32[]{:S(2)}) copy-start(bf16[128,512]{1,0:T(8,128)(2,1)} %param.16) | copy-start | bytes 393220
  79.4 131.2 %copy-start.6 = (bf16[128,128]{1,0:T(8,128)(2,1)S(1)}, bf16[128,128]{1,0:T(8,128)(2,1)}, u32[]{:S(2)}) copy-start(bf16[128,128]{1,0:T(8,128)(2,1)} %param.23) | copy-start | bytes 98308
  79.4 163.7 %all-gather.3.cloned.1.call-start = ((), (), s32[]{:S(2)}) async-start(), calls=%async_computation.4 | async-start | bytes 1179648 | tf_op jit(solution)/shard_map/all_gather | solution.py:115
  208.7 38.7 %copy-start.10 = (f32[128]{0:T(128)}, f32[128]{0:T(128)S(1)}, u32[]{:S(2)}) copy-start(f32[128]{0:T(128)S(1)} %fusion.37) | copy-start | bytes 1540
  210.5 112.7 %all-gather.5.cloned.1.call-start = ((), (), s32[]{:S(2)}) async-start(), calls=%async_computation.6 | async-start | bytes 4325376 | tf_op jit(solution)/shard_map/all_gather | solution.py:126
  211.4 204.4 %reduce-scatter.6.cloned.1.call-start = ((), (), s32[]{:S(2)}) async-start(), calls=%async_computation.5 | async-start | bytes 4325376 | tf_op jit(solution)/shard_map/reduce_scatter | solution.py:117
  243.1 4.3 copy-start.1
  323.1 130.3 %reduce-scatter.8.cloned.1.call-start = ((), (), s32[]{:S(2)}) async-start(), calls=%async_computation.7 | async-start | bytes 1179648 | tf_op jit(solution)/shard_map/reduce_scatter | solution.py:127
  397.9 17.9 %copy-start.3 = (bf16[128,512]{1,0:T(8,128)(2,1)S(1)}, bf16[128,512]{1,0:T(8,128)(2,1)}, u32[]{:S(2)}) copy-start(bf16[128,512]{1,0:T(8,128)(2,1)} %get-tuple-element.170) | copy-start | bytes 393220
  397.9 17.9 %copy-start.7 = (bf16[128,128]{1,0:T(8,128)(2,1)S(1)}, bf16[128,128]{1,0:T(8,128)(2,1)}, u32[]{:S(2)}) copy-start(bf16[128,128]{1,0:T(8,128)(2,1)} %param.23) | copy-start | bytes 98308
  397.9 17.9 %copy-start.11 = (f32[128]{0:T(128)S(1)}, f32[128]{0:T(128)}, u32[]{:S(2)}) copy-start(f32[128]{0:T(128)} %copy-done.10) | copy-start | bytes 1540
  397.9 55.5 %copy-start.9 = (bf16[128,128]{1,0:T(8,128)(2,1)S(1)}, bf16[128,128]{1,0:T(8,128)(2,1)}, u32[]{:S(2)}) copy-start(bf16[128,128]{1,0:T(8,128)(2,1)} %param.15) | copy-start | bytes 98308
  397.9 55.5 %copy-start.13 = (bf16[128,128]{1,0:T(8,128)(2,1)S(1)}, bf16[128,128]{1,0:T(8,128)(2,1)}, u32[]{:S(2)}) copy-start(bf16[128,128]{1,0:T(8,128)(2,1)} %reduce-scatter.4.cloned.1.call-done) | copy-start | bytes 98308
  397.9 55.5 %copy-start.16 = (f32[128,512]{1,0:T(8,128)S(1)}, f32[128,512]{1,0:T(8,128)}, u32[]{:S(2)}) copy-start(f32[128,512]{1,0:T(8,128)} %get-tuple-element.171) | copy-start | bytes 786436
  399.1 318.4 %all-reduce.4.cloned.1.call-start = ((), (), s32[]{:S(2)}) async-start(), calls=%async_computation.8 | async-start | bytes 1048576 | tf_op jit(solution)/shard_map/psum | solution.py:140
  415.8 39.6 %copy-start.4 = (bf16[128,512]{1,0:T(8,128)(2,1)S(1)}, bf16[128,512]{1,0:T(8,128)(2,1)}, u32[]{:S(2)}) copy-start(bf16[128,512]{1,0:T(8,128)(2,1)} %reduce-scatter.6.cloned.1.call-done) | copy-start | bytes 393220
Sparse Core Ops, SparseCore 0:
  79.5 89.1 reduce-scatter.3
  210.6 32.4 all-gather.2
  245.6 54.8 all-gather.4
  323.2 92.5 reduce-scatter.5
  418.2 35.1 reduce-scatter.7
  459.4 258.0 all-reduce.3
where the time goes:
time: 731 us; the launch traced here: 728 us
  waiting for transfers between devices  345 us (47%)
  blocking collectives  149 us (20%)
  other arithmetic  116 us (16%)
  matrix products  54.7 us (7%)
  local copies, waits for them, and re-layouts  47.3 us (6%)
  between operations  15.6 us (2%)
    psum x1, waiting for transfers between devices, local(): lax.psum((first_term * node_scale, second_term * node_scale), ('row', 'co...  261 us
    unnamed x1, blocking collectives  125 us
    scatter-add x10, other arithmetic, forward_accumulate(): return (running.at[rows_here].add(contrib), None)  64.5 us
    reduce_scatter x1, waiting for transfers between devices, local(): lax.psum_scatter(backward_part(tile_values, col_index, row_index, grad_ro...  35.6 us
    all_gather x1, waiting for transfers between devices, local(): panel_hidden = lax.all_gather(hidden, 'row', axis=0, tiled=True)  31.6 us
    scatter-add x5, other arithmetic, backward_accumulate(): return (running.at[cols_here].add(contrib), None)  30.8 us
    dot_general x10, matrix products, forward_accumulate(): jnp.einsum('sij,sjf->sif', values_here, source_blocks[cols_here], preferr...  25 us
    all_gather x1, blocking collectives, local(): panel_in = lax.all_gather(features, 'row', axis=0, tiled=True)  23.5 us
  transfers between devices with their start and end apart: 6, of which 4 were waited for; matrix products, arithmetic and copies ran while one was open for 22% of the time, Pallas kernels for 0%

commit v1 on v0

v1 whole, which is shorter than its diff:
```python
import functools
import math

import jax
import jax.numpy as jnp
from jax import lax
from jax.experimental import pallas as pl
from jax.experimental.pallas import tpu as pltpu
from jax.sharding import PartitionSpec as P

BLOCK = 128


gelu_coef = math.sqrt(2.0 / math.pi)


def gelu_tanh(value):
    return 0.5 * value * (1.0 + jnp.tanh(gelu_coef * (value + 0.044715 * value * value * value)))


def gelu_slope(value):
    tanh_value = jnp.tanh(gelu_coef * (value + 0.044715 * value * value * value))
    return 0.5 * (1.0 + tanh_value) + 0.5 * value * (1.0 - tanh_value * tanh_value) * gelu_coef * (
        1.0 + 3.0 * 0.044715 * value * value
    )


def _masked_tile(tiles_ref, mask_ref, s):
    return (tiles_ref[s].astype(jnp.float32) * mask_ref[s]).astype(jnp.bfloat16)


def _forward_kernel(with_degree, live_ref, rows_ref, cols_ref, tiles_ref, mask_ref, src_ref, *rest):
    if with_degree:
        out_ref, deg_ref, acc_ref, dacc_ref = rest
    else:
        out_ref, acc_ref = rest
    slots = tiles_ref.shape[0]
    n_dst = acc_ref.shape[0]
    n_src = src_ref.shape[0]
    acc_ref[...] = jnp.zeros_like(acc_ref)
    if with_degree:
        dacc_ref[...] = jnp.zeros_like(dacc_ref)
    ones = jnp.ones((8, BLOCK), jnp.bfloat16)

    def body(s, carry):
        r = jnp.clip(rows_ref[s], 0, n_dst - 1)
        c = jnp.clip(cols_ref[s], 0, n_src - 1)
        tile = _masked_tile(tiles_ref, mask_ref, s)
        acc_ref[r] += jnp.dot(tile, src_ref[c], preferred_element_type=jnp.float32)
        if with_degree:
            dacc_ref[r] += lax.dot_general(
                ones, tile, (((1,), (1,)), ((), ())), preferred_element_type=jnp.float32
            )
        return carry

    lax.fori_loop(0, jnp.clip(live_ref[0], 0, slots), body, 0)
    out_ref[...] = acc_ref[...].astype(out_ref.dtype)
    if with_degree:
        deg_ref[...] = dacc_ref[...]


def _transpose_kernel(live_ref, rows_ref, cols_ref, tiles_ref, mask_ref, src_ref, out_ref, acc_ref):
    slots = tiles_ref.shape[0]
    n_dst = acc_ref.shape[0]
    n_src = src_ref.shape[0]
    acc_ref[...] = jnp.zeros_like(acc_ref)

    def body(s, carry):
        r = jnp.clip(rows_ref[s], 0, n_src - 1)
        c = jnp.clip(cols_ref[s], 0, n_dst - 1)
        tile = _masked_tile(tiles_ref, mask_ref, s)
        acc_ref[c] += jnp.dot(src_ref[r], tile, preferred_element_type=jnp.float32)
        return carry

    lax.fori_loop(0, jnp.clip(live_ref[0], 0, slots), body, 0)
    out_ref[...] = acc_ref[...].astype(out_ref.dtype)


_SMEM = pl.BlockSpec(memory_space=pltpu.SMEM)
_VMEM = pl.BlockSpec(memory_space=pltpu.VMEM)


def forward_aggregate(live, rows, cols, tiles, mask, src, n_dst, with_degree):
    width = src.shape[-1]
    slots = tiles.shape[0]
    out_shape = [jax.ShapeDtypeStruct((n_dst, BLOCK, width), jnp.bfloat16)]
    scratch = [pltpu.VMEM((n_dst, BLOCK, width), jnp.float32)]
    if with_degree:
        out_shape.append(jax.ShapeDtypeStruct((n_dst, 8, BLOCK), jnp.float32))
        scratch.append(pltpu.VMEM((n_dst, 8, BLOCK), jnp.float32))
    flops = 2 * slots * BLOCK * BLOCK * (width + (8 if with_degree else 0))
    bytes_accessed = tiles.size * 2 + src.size * 2 + n_dst * BLOCK * width * 2
    return pl.pallas_call(
        functools.partial(_forward_kernel, with_degree),
        out_shape=tuple(out_shape),
        in_specs=[_SMEM, _SMEM, _SMEM, _VMEM, _VMEM, _VMEM],
        out_specs=tuple([_VMEM] * len(out_shape)),
        scratch_shapes=scratch,
        cost_estimate=pl.CostEstimate(flops=flops, bytes_accessed=bytes_accessed, transcendentals=0),
    )(live, rows, cols, tiles, mask, src)


def transpose_aggregate(live, rows, cols, tiles, mask, src_t, n_dst):
    width = src_t.shape[1]
    slots = tiles.shape[0]
    flops = 2 * slots * BLOCK * BLOCK * width
    bytes_accessed = tiles.size * 2 + src_t.size * 2 + n_dst * BLOCK * width * 2
    return pl.pallas_call(
        _transpose_kernel,
        out_shape=jax.ShapeDtypeStruct((n_dst, width, BLOCK), jnp.bfloat16),
        in_specs=[_SMEM, _SMEM, _SMEM, _VMEM, _VMEM, _VMEM],
        out_specs=_VMEM,
        scratch_shapes=[pltpu.VMEM((n_dst, width, BLOCK), jnp.float32)],
        cost_estimate=pl.CostEstimate(flops=flops, bytes_accessed=bytes_accessed, transcendentals=0),
    )(live, rows, cols, tiles, mask, src_t)


def gather_blocks(block, axis):
    n = lax.axis_size(axis)
    return lax.all_to_all(jnp.broadcast_to(block[None], (n,) + block.shape), axis, 0, 0, tiled=False)


def scatter_blocks(blocks, axis):
    return lax.all_to_all(blocks, axis, 0, 0, tiled=False)


def split_hi_lo(value):
    hi = value.astype(jnp.bfloat16)
    lo = (value - hi.astype(jnp.float32)).astype(jnp.bfloat16)
    return hi, lo


def local(
    features,
    first_weight,
    second_weight,
    tile_rows,
    tile_cols,
    tile_live,
    column_mask,
    edge_weight,
    cotangent,
):
    f32 = jnp.float32
    bf16 = jnp.bfloat16
    n_rows_axis = lax.axis_size("row")
    n_cols_axis = lax.axis_size("col")
    node_count = features.shape[0]
    row_groups = n_cols_axis * node_count // BLOCK
    col_groups = n_rows_axis * node_count // BLOCK

    live = tile_live.reshape(1)
    rows = tile_rows[0, 0]
    cols = tile_cols[0, 0]
    tiles = edge_weight[0, 0]
    mask = column_mask[0, 0].astype(f32)[:, None, :]

    x_panel = gather_blocks(features, "row")
    partial_in, partial_deg = forward_aggregate(
        live, rows, cols, tiles, mask, x_panel, row_groups, with_degree=True
    )
    deg_hi, deg_lo = split_hi_lo(partial_deg[:, 0, :])
    pad = jnp.zeros((row_groups, 14, BLOCK), bf16)
    packed = jnp.concatenate([partial_in, deg_hi[:, None, :], deg_lo[:, None, :], pad], axis=1)
    arrived = scatter_blocks(packed, "col").astype(f32)
    summed = jnp.sum(arrived, axis=0)
    summed_in = summed[:BLOCK]
    degree = summed[BLOCK] + summed[BLOCK + 1]
    row_scale = (1.0 / jnp.sqrt(1.0 + degree))[:, None]

    first_mix = (features.astype(f32) + row_scale * summed_in).astype(bf16)
    first_pre = jnp.dot(first_mix, first_weight, preferred_element_type=f32)
    hidden = gelu_tanh(first_pre).astype(bf16)
    projected = jnp.dot(hidden, second_weight, preferred_element_type=f32)

    scaled_t = (row_scale * cotangent.astype(f32)).astype(bf16).T
    grad_panel_t = gather_blocks(scaled_t, "col")
    partial_back_t = transpose_aggregate(live, rows, cols, tiles, mask, grad_panel_t, col_groups)
    returned_t = jnp.sum(scatter_blocks(partial_back_t, "row").astype(f32), axis=0)

    y_panel = gather_blocks(projected.astype(bf16), "row")
    (partial_y,) = forward_aggregate(live, rows, cols, tiles, mask, y_panel, row_groups, with_degree=False)
    summed_y = jnp.sum(scatter_blocks(partial_y, "col").astype(f32), axis=0)
    output = (projected + row_scale * summed_y).astype(bf16)

    hp = lax.Precision.HIGHEST
    combined = cotangent.astype(f32) + returned_t.T
    hidden_grad = jnp.dot(combined, second_weight.astype(f32).T, precision=hp, preferred_element_type=f32)
    pre_grad = (hidden_grad * gelu_slope(first_pre)).astype(bf16)
    first_term = jnp.dot(first_mix.T, pre_grad, preferred_element_type=f32)
    second_term = jnp.dot(hidden.astype(f32).T, combined, precision=hp, preferred_element_type=f32)

    node_scale = 1.0 / math.sqrt(node_count * n_rows_axis * n_cols_axis)
    n_dev = n_rows_axis * n_cols_axis
    flat = jnp.concatenate([first_term.reshape(-1), second_term.reshape(-1)]) * node_scale
    pieces = scatter_blocks(flat.reshape(n_dev, -1), ("row", "col"))
    reduced = jnp.sum(pieces, axis=0)
    everything = gather_blocks(reduced, ("row", "col")).reshape(-1)
    split = first_term.size
    first_grad = everything[:split].reshape(first_term.shape)
    second_grad = everything[split:].reshape(second_term.shape)
    return (output, first_grad, second_grad)


def solution(mesh):
    return jax.shard_map(
        local,
        mesh=mesh,
        in_specs=(
            P(("row", "col"), None),
            P(),
            P(),
            P("row", "col", None),
            P("row", "col", None),
            P("row", "col"),
            P("row", "col", None, None),
            P("row", "col", None, None, None),
            P(("row", "col"), None),
        ),
        out_specs=(P(("row", "col"), None), P(), P()),
        check_vma=False,
    )
```

time: 731 us -> 225 us (0.31)
  waiting for transfers between devices: 345 us -> 8.38 us
  other arithmetic: 116 us -> 5.41 us
  matrix products: 54.7 us -> 1.3 us
  local copies, waits for them, and re-layouts: 47.3 us -> 6.37 us
  blocking collectives: 149 us -> 176 us
  Pallas kernels: 0 us -> 16.3 us
  between operations: 15.6 us -> 1.45 us
  starting transfers between devices: 0.24 us -> 9 us
    psum x1 -> x0, waiting for transfers between devices: 261 us -> none  [local(): lax.psum((first_term * node_scale, second_term * node_scale), ('row', 'co...]
    all_to_all x0 -> x7, blocking collectives: none -> 176 us  [the longest x4 114 us: scatter_blocks(): return lax.all_to_all(blocks, axis, 0, 0, tiled=False)]
    unnamed x1 -> x0, blocking collectives: 125 us -> none
    scatter-add x16 -> x0, other arithmetic: 96.1 us -> none  [the longest x10 64.5 us: forward_accumulate(): return (running.at[rows_here].add(contrib), None)]
    dot_general x20 -> x5, matrix products: 54.7 us -> 1.3 us  [the longest x1 0.36 us: local(): jnp.dot(combined, second_weight.astype(f32).T, precision=hp, preferred_el...]
    reduce_scatter x3 -> x0, waiting for transfers between devices: 52.3 us -> none  [the longest x1 35.6 us: local(): lax.psum_scatter(backward_part(tile_values, col_index, row_index, grad_ro...]
    all_gather x2 -> x0, waiting for transfers between devices: 31.6 us -> none  [the longest x1 31.6 us: local(): panel_hidden = lax.all_gather(hidden, 'row', axis=0, tiled=True)]
    gather x15 -> x0, local copies, waits for them, and re-layouts: 27.8 us -> none  [the longest x5 21.1 us: backward_accumulate(): source_blocks[rows_here]]
  transfers between devices with their start and end apart: 6 -> 1, of which waited for: 4 -> 1; matrix products, arithmetic and copies ran while one was open for 22% -> 1% of each run, Pallas kernels for 0% -> 0%
where the time goes in v1:
time: 225 us
  blocking collectives  176 us (78%)
  Pallas kernels  16.3 us (7%)
  starting transfers between devices  9 us (4%)
  waiting for transfers between devices  8.38 us (4%)
  local copies, waits for them, and re-layouts  6.37 us (3%)
  other arithmetic  5.41 us (2%)
    all_to_all x4, blocking collectives, scatter_blocks(): return lax.all_to_all(blocks, axis, 0, 0, tiled=False)  114 us
    all_to_all x3, blocking collectives, gather_blocks(): lax.all_to_all(jnp.broadcast_to(block[None], (n,) + block.shape), axis, 0...  62.1 us
    pallas_call x2, Pallas kernels, forward_aggregate(): pl.pallas_call(functools.partial(_forward_kernel, with_degree), out_shape...  11.1 us
    all_to_all x1, starting transfers between devices, gather_blocks(): lax.all_to_all(jnp.broadcast_to(block[None], (n,) + block.shape), axis, 0...  9 us
    all_to_all x1, waiting for transfers between devices, gather_blocks(): lax.all_to_all(jnp.broadcast_to(block[None], (n,) + block.shape), axis, 0...  8.38 us
    pallas_call x1, Pallas kernels, transpose_aggregate(): pl.pallas_call(_transpose_kernel, out_shape=jax.ShapeDtypeStruct((n_dst,...  5.23 us
  transfers between devices with their start and end apart: 1, of which 1 were waited for; matrix products, arithmetic and copies ran while one was open for 1% of the time, Pallas kernels for 0%

profile of v1, /device:TPU:1, one launch (start us, length us, event | category | flops | bytes accessed | tf_op | source)
XLA Modules:
  0.0 224.6 jit_solution(6227846254774734901)
XLA Ops:
  0.6 0.0 copy-start
  0.6 1.5 broadcast_in_dim.10
  2.2 9.0 %all-to-all-start = ((bf16[8,128,128]{2,1,0:T(8,128)(2,1)}), bf16[8,128,128]{2,1,0:T(8,128)(2,1)S(1)}, u32[]{:S(2)}, u32[]{:S(2)}) async-start(bf16[8,128,128]{2,1,0:T(8,128)(2,1)} %broadcast_in_dim.10), calls=%async_computation | async-start | bytes 524288 | tf_op jit(solution)/shard_map/all_to_all | solution.py:120
  11.8 1.4 convert_element_type.63
  13.2 0.1 pad.5.clone
  13.3 8.4 %all-to-all-done.src_ref = bf16[8,128,128]{2,1,0:T(8,128)(2,1)S(1)} async-done(((bf16[8,128,128]{2,1,0:T(8,128)(2,1)}), bf16[8,128,128]{2,1,0:T(8,128)(2,1)S(1)}, u32[]{:S(2)}, u32[]{:S(2)}) %all-to-all-start) | async-done | bytes 262176 | tf_op jit(solution)/shard_map/all_to_all | solution.py:120
  21.7 0.0 copy-start.1
  21.7 0.7 copy-done.1
  22.4 5.6 %shard_map.112 = (bf16[32,128,128]{2,1,0:T(8,128)(2,1)}, f32[32,8,128]{2,1,0:T(8,128)}) custom-call(s32[1]{0:T(128)} %bitcast.25.live_ref, s32[80]{0:T(128)} %bitcast.36, s32[80]{0:T(128)} %bitcast.39, bf16[80,128,128]{2,1,0:T(8,128)(2,1)} %bitcast.28, f32[80,1,128]{2,1,0:T(1,128)} %bitcast.31, bf16[8,128,128]{2,1,0:T(8,128)(2,1)} %copy-done.1), custom_call_target="tpu_custom_call" | custom-call | flops 356515840 | bytes 3932160 | tf_op jit(solution)/shard_map/pallas_call | solution.py:93
  28.0 0.9 subtract_convert_fusion
  28.9 0.9 slice.53
  29.9 1.6 maximum_maximum_fusion
  31.4 0.0 copy-start.3
  31.4 0.0 copy-start.2
  31.4 36.6 %all_to_all.42 = bf16[32,144,128]{2,1,0:T(8,128)(2,1)S(1)} all-to-all(bf16[32,144,128]{2,1,0:T(8,128)(2,1)S(1)} %maximum_maximum_fusion), channel_id=1, replica_groups=mesh['row'=8,'col'=32] {'col'}, dimensions={0} | all-to-all | bytes 2359296 | tf_op jit(solution)/shard_map/all_to_all | solution.py:124
  68.1 0.2 convert_reduce_fusion
  68.3 0.0 copy-done.3
  68.3 0.1 fusion.8
  68.4 0.0 copy-done.2
  68.4 0.2 fusion.15
  68.5 0.0 copy-done
  68.6 0.2 fusion.14
  68.8 15.3 %all_to_all.43.src_ref = bf16[8,128,128]{2,1,0:T(8,128)(2,1)} all-to-all(bf16[8,128,128]{2,1,0:T(8,128)(2,1)S(1)} %broadcast_in_dim.12), channel_id=1, replica_groups=mesh['row'=8,'col'=32] {'row'}, dimensions={0} | all-to-all | bytes 524288 | tf_op jit(solution)/shard_map/all_to_all | solution.py:120
  84.2 5.5 %shard_map.113 = bf16[32,128,128]{2,1,0:T(8,128)(2,1)} custom-call(s32[1]{0:T(128)} %bitcast.26.live_ref, s32[80]{0:T(128)} %bitcast.37, s32[80]{0:T(128)} %bitcast.40, bf16[80,128,128]{2,1,0:T(8,128)(2,1)} %bitcast.29, f32[80,1,128]{2,1,0:T(1,128)} %bitcast.32, bf16[8,128,128]{2,1,0:T(8,128)(2,1)} %all_to_all.43.src_ref), custom_call_target="tpu_custom_call" | custom-call | flops 335544320 | bytes 3932160 | tf_op jit(solution)/shard_map/pallas_call | solution.py:93
  89.6 0.0 copy-start.4
  89.6 29.7 %all_to_all.44 = bf16[32,128,128]{2,1,0:T(8,128)(2,1)S(1)} all-to-all(bf16[32,128,128]{2,1,0:T(8,128)(2,1)} %shard_map.113), channel_id=1, replica_groups=mesh['row'=8,'col'=32] {'col'}, dimensions={0} | all-to-all | bytes 2097152 | tf_op jit(solution)/shard_map/all_to_all | solution.py:124
  119.3 0.2 convert_reduce_fusion.1
  119.5 0.0 copy-done.4
  119.5 0.7 fusion.10
  120.2 0.1 copy.13
  120.3 0.2 broadcast_in_dim.13
  120.5 20.9 %all_to_all.45.src_ref = bf16[32,128,128]{2,1,0:T(8,128)(2,1)} all-to-all(bf16[32,128,128]{2,1,0:T(8,128)(2,1)S(1)} %broadcast_in_dim.13), channel_id=1, replica_groups=mesh['row'=8,'col'=32] {'col'}, dimensions={0} | all-to-all | bytes 2097152 | tf_op jit(solution)/shard_map/all_to_all | solution.py:120
  141.4 5.2 %shard_map.114 = bf16[8,128,128]{2,1,0:T(8,128)(2,1)} custom-call(s32[1]{0:T(128)} %bitcast.27.live_ref, s32[80]{0:T(128)} %bitcast.38, s32[80]{0:T(128)} %bitcast.41, bf16[80,128,128]{2,1,0:T(8,128)(2,1)} %bitcast.30, f32[80,1,128]{2,1,0:T(1,128)} %bitcast.33, bf16[32,128,128]{2,1,0:T(8,128)(2,1)} %all_to_all.45.src_ref), custom_call_target="tpu_custom_call" | custom-call | flops 335544320 | bytes 3932160 | tf_op jit(solution)/shard_map/pallas_call | solution.py:108
  146.6 15.7 %all_to_all.46 = bf16[8,128,128]{2,1,0:T(8,128)(2,1)S(1)} all-to-all(bf16[8,128,128]{2,1,0:T(8,128)(2,1)} %shard_map.114), channel_id=1, replica_groups=mesh['row'=8,'col'=32] {'row'}, dimensions={0} | all-to-all | bytes 524288 | tf_op jit(solution)/shard_map/all_to_all | solution.py:124
  162.4 0.1 copy.14
  162.5 0.4 fusion
  162.9 0.4 fusion.9
  163.3 0.2 convolution_bitcast_fusion
  163.5 0.1 maximum_multiply_fusion
  163.6 0.5 copy.15
  164.1 32.2 %all_to_all.47 = f32[256,1,512]{2,1,0:T(1,128)S(1)} all-to-all(f32[256,1,512]{2,1,0:T(1,128)S(1)} %copy.15), channel_id=1, replica_groups=mesh['row'=8,'col'=32] {'row','col'}, dimensions={0} | all-to-all | bytes 1048576 | tf_op jit(solution)/shard_map/all_to_all | solution.py:124
  196.3 0.3 reduce_sum.39
  196.6 0.3 broadcast_in_dim.14
  196.9 25.9 %all_to_all.48 = f32[256,1,512]{2,1,0:T(1,128)S(1)} all-to-all(f32[256,1,512]{2,1,0:T(1,128)S(1)} %broadcast_in_dim.14), channel_id=1, replica_groups=mesh['row'=8,'col'=32] {'row','col'}, dimensions={0} | all-to-all | bytes 1048576 | tf_op jit(solution)/shard_map/all_to_all | solution.py:120
  222.8 1.1 fusion.13
  223.9 0.7 copy.18
  (5 shorter events, 0.1 us)
Async XLA Ops:
  0.6 67.9 %copy-start = (bf16[512,128]{1,0:T(8,128)(2,1)S(1)}, bf16[512,128]{1,0:T(8,128)(2,1)}, u32[]{:S(2)}) copy-start(bf16[512,128]{1,0:T(8,128)(2,1)} %param.11) | copy-start | bytes 393220
  2.2 19.5 %all-to-all-start = ((bf16[8,128,128]{2,1,0:T(8,128)(2,1)}), bf16[8,128,128]{2,1,0:T(8,128)(2,1)S(1)}, u32[]{:S(2)}, u32[]{:S(2)}) async-start(bf16[8,128,128]{2,1,0:T(8,128)(2,1)} %broadcast_in_dim.10), calls=%async_computation | async-start | bytes 524288 | tf_op jit(solution)/shard_map/all_to_all | solution.py:120
  21.7 0.7 copy-start.1
  31.4 36.8 %copy-start.3 = (bf16[128,128]{1,0:T(8,128)(2,1)S(1)}, bf16[128,128]{1,0:T(8,128)(2,1)}, u32[]{:S(2)}) copy-start(bf16[128,128]{1,0:T(8,128)(2,1)} %param.9) | copy-start | bytes 98308
  31.4 36.9 %copy-start.2 = (bf16[128,512]{1,0:T(8,128)(2,1)S(1)}, bf16[128,512]{1,0:T(8,128)(2,1)}, u32[]{:S(2)}) copy-start(bf16[128,512]{1,0:T(8,128)(2,1)} %param.10) | copy-start | bytes 393220
  89.6 29.9 %copy-start.4 = (bf16[128,128]{1,0:T(8,128)(2,1)S(1)}, bf16[128,128]{1,0:T(8,128)(2,1)}, u32[]{:S(2)}) copy-start(bf16[128,128]{1,0:T(8,128)(2,1)} %param.17) | copy-start | bytes 98308

commit v2 on v1

--- a/solution.py
+++ b/solution.py
@@ -160,28 +160,37 @@
         live, rows, cols, tiles, mask, x_panel, row_groups, with_degree=True
     )
     deg_hi, deg_lo = split_hi_lo(partial_deg[:, 0, :])
-    pad = jnp.zeros((row_groups, 14, BLOCK), bf16)
-    packed = jnp.concatenate([partial_in, deg_hi[:, None, :], deg_lo[:, None, :], pad], axis=1)
-    arrived = scatter_blocks(packed, "col").astype(f32)
-    summed = jnp.sum(arrived, axis=0)
-    summed_in = summed[:BLOCK]
-    degree = summed[BLOCK] + summed[BLOCK + 1]
-    row_scale = (1.0 / jnp.sqrt(1.0 + degree))[:, None]
+    shared = jnp.concatenate([deg_hi, deg_lo, cotangent], axis=0)
+    packed = jnp.concatenate(
+        [partial_in, jnp.broadcast_to(shared[None], (row_groups,) + shared.shape)], axis=1
+    )
+    arrived = scatter_blocks(packed, "col")
+    summed_in = jnp.sum(arrived[:, :BLOCK].astype(f32), axis=0)
+    degrees = jnp.sum(arrived[:, BLOCK : BLOCK + 2 * row_groups].astype(f32), axis=0)
+    degrees = degrees[:row_groups] + degrees[row_groups:]
+    group_cot = arrived[:, BLOCK + 2 * row_groups :]
+    group_scale = 1.0 / jnp.sqrt(1.0 + degrees)
+    me = lax.axis_index("col")
+    row_scale = lax.dynamic_index_in_dim(group_scale, me, axis=0, keepdims=False)[:, None]
 
     first_mix = (features.astype(f32) + row_scale * summed_in).astype(bf16)
     first_pre = jnp.dot(first_mix, first_weight, preferred_element_type=f32)
     hidden = gelu_tanh(first_pre).astype(bf16)
     projected = jnp.dot(hidden, second_weight, preferred_element_type=f32)
 
-    scaled_t = (row_scale * cotangent.astype(f32)).astype(bf16).T
-    grad_panel_t = gather_blocks(scaled_t, "col")
+    grad_panel_t = jnp.swapaxes(
+        (group_scale[:, :, None] * group_cot.astype(f32)).astype(bf16), 1, 2
+    )
     partial_back_t = transpose_aggregate(live, rows, cols, tiles, mask, grad_panel_t, col_groups)
-    returned_t = jnp.sum(scatter_blocks(partial_back_t, "row").astype(f32), axis=0)
-
-    y_panel = gather_blocks(projected.astype(bf16), "row")
+
+    packed = jnp.concatenate(
+        [jnp.broadcast_to(projected.astype(bf16)[None], (col_groups, BLOCK, BLOCK)), partial_back_t],
+        axis=1,
+    )
+    arrived = scatter_blocks(packed, "row")
+    y_panel = arrived[:, :BLOCK]
+    returned_t = jnp.sum(arrived[:, BLOCK:].astype(f32), axis=0)
     (partial_y,) = forward_aggregate(live, rows, cols, tiles, mask, y_panel, row_groups, with_degree=False)
-    summed_y = jnp.sum(scatter_blocks(partial_y, "col").astype(f32), axis=0)
-    output = (projected + row_scale * summed_y).astype(bf16)
 
     hp = lax.Precision.HIGHEST
     combined = cotangent.astype(f32) + returned_t.T
@@ -189,13 +198,21 @@
     pre_grad = (hidden_grad * gelu_slope(first_pre)).astype(bf16)
     first_term = jnp.dot(first_mix.T, pre_grad, preferred_element_type=f32)
     second_term = jnp.dot(hidden.astype(f32).T, combined, precision=hp, preferred_element_type=f32)
-
     node_scale = 1.0 / math.sqrt(node_count * n_rows_axis * n_cols_axis)
-    n_dev = n_rows_axis * n_cols_axis
     flat = jnp.concatenate([first_term.reshape(-1), second_term.reshape(-1)]) * node_scale
-    pieces = scatter_blocks(flat.reshape(n_dev, -1), ("row", "col"))
-    reduced = jnp.sum(pieces, axis=0)
-    everything = gather_blocks(reduced, ("row", "col")).reshape(-1)
+    slices = flat.reshape(row_groups, -1, BLOCK)
+    slice_rows = slices.shape[1]
+    grad_hi, grad_lo = split_hi_lo(slices)
+
+    packed = jnp.concatenate([partial_y, grad_hi, grad_lo], axis=1)
+    arrived = scatter_blocks(packed, "col").astype(f32)
+    summed_y = jnp.sum(arrived[:, :BLOCK], axis=0)
+    output = (projected + row_scale * summed_y).astype(bf16)
+    part = jnp.sum(arrived[:, BLOCK:], axis=0)
+    part = part[:slice_rows] + part[slice_rows:]
+
+    total = jnp.sum(gather_blocks(part, "row"), axis=0)
+    everything = gather_blocks(total, "col").reshape(-1)
     split = first_term.size
     first_grad = everything[:split].reshape(first_term.shape)
     second_grad = everything[split:].reshape(second_term.shape)

time: 225 us -> 205 us (0.911)
  blocking collectives: 176 us -> 54.2 us
  waiting for transfers between devices: 8.38 us -> 69.8 us
  starting transfers between devices: 9 us -> 36.1 us
  local copies, waits for them, and re-layouts: 6.37 us -> 11.9 us
  other arithmetic: 5.41 us -> 10.8 us
    all_to_all x4 -> x1, blocking collectives: 114 us -> 43.5 us  [scatter_blocks(): return lax.all_to_all(blocks, axis, 0, 0, tiled=False)]
    all_to_all x3 -> x1, blocking collectives: 62.1 us -> 10.7 us  [gather_blocks(): lax.all_to_all(jnp.broadcast_to(block[None], (n,) + block.shape), axis, 0...]
    all_to_all x0 -> x2, waiting for transfers between devices: none -> 50.6 us  [scatter_blocks(): return lax.all_to_all(blocks, axis, 0, 0, tiled=False)]
    all_to_all x0 -> x2, starting transfers between devices: none -> 21.2 us  [scatter_blocks(): return lax.all_to_all(blocks, axis, 0, 0, tiled=False)]
    all_to_all x1 -> x2, waiting for transfers between devices: 8.38 us -> 19.2 us  [gather_blocks(): lax.all_to_all(jnp.broadcast_to(block[None], (n,) + block.shape), axis, 0...]
    all_to_all x1 -> x2, starting transfers between devices: 9 us -> 14.9 us  [gather_blocks(): lax.all_to_all(jnp.broadcast_to(block[None], (n,) + block.shape), axis, 0...]
    concatenate x1 -> x4, other arithmetic: 1.56 us -> 5.13 us  [the longest x1 2.93 us: local(): jnp.concatenate([partial_in, jnp.broadcast_to(shared[None], (row_groups,)...]
  transfers between devices with their start and end apart: 1 -> 4, of which waited for: 1 -> 4; matrix products, arithmetic and copies ran while one was open for 1% -> 1% of each run, Pallas kernels for 0% -> 0%
where the time goes in v2:
time: 205 us; the launch traced here: 203 us
  waiting for transfers between devices  69.8 us (34%)
  blocking collectives  54.2 us (26%)
  starting transfers between devices  36.1 us (18%)
  Pallas kernels  17.7 us (9%)
  local copies, waits for them, and re-layouts  11.9 us (6%)
  other arithmetic  10.8 us (5%)
    all_to_all x2, waiting for transfers between devices, scatter_blocks(): return lax.all_to_all(blocks, axis, 0, 0, tiled=False)  50.6 us
    all_to_all x1, blocking collectives, scatter_blocks(): return lax.all_to_all(blocks, axis, 0, 0, tiled=False)  43.5 us
    all_to_all x2, starting transfers between devices, scatter_blocks(): return lax.all_to_all(blocks, axis, 0, 0, tiled=False)  21.2 us
    all_to_all x2, waiting for transfers between devices, gather_blocks(): lax.all_to_all(jnp.broadcast_to(block[None], (n,) + block.shape), axis, 0...  19.2 us
    all_to_all x2, starting transfers between devices, gather_blocks(): lax.all_to_all(jnp.broadcast_to(block[None], (n,) + block.shape), axis, 0...  14.9 us
    pallas_call x2, Pallas kernels, forward_aggregate(): pl.pallas_call(functools.partial(_forward_kernel, with_degree), out_shape...  12 us
    all_to_all x1, blocking collectives, gather_blocks(): lax.all_to_all(jnp.broadcast_to(block[None], (n,) + block.shape), axis, 0...  10.7 us
    pallas_call x1, Pallas kernels, transpose_aggregate(): pl.pallas_call(_transpose_kernel, out_shape=jax.ShapeDtypeStruct((n_dst,...  5.69 us
  transfers between devices with their start and end apart: 4, of which 4 were waited for; matrix products, arithmetic and copies ran while one was open for 1% of the time, Pallas kernels for 0%

profile of v2, /device:TPU:1, one launch (start us, length us, event | category | flops | bytes accessed | tf_op | source)
XLA Modules:
  0.0 203.3 jit_solution(15595372732156014124)
XLA Ops:
  0.6 0.0 copy-start
  0.6 0.0 copy-start.3
  0.7 1.5 broadcast_in_dim.10
  2.2 9.0 %all-to-all-start = ((bf16[8,128,128]{2,1,0:T(8,128)(2,1)}), bf16[8,128,128]{2,1,0:T(8,128)(2,1)S(1)}, u32[]{:S(2)}, u32[]{:S(2)}) async-start(bf16[8,128,128]{2,1,0:T(8,128)(2,1)} %broadcast_in_dim.10), calls=%async_computation | async-start | bytes 524288 | tf_op jit(solution)/shard_map/all_to_all | solution.py:120
  11.2 1.4 convert_element_type.73
  13.2 8.4 %all-to-all-done.src_ref = bf16[8,128,128]{2,1,0:T(8,128)(2,1)S(1)} async-done(((bf16[8,128,128]{2,1,0:T(8,128)(2,1)}), bf16[8,128,128]{2,1,0:T(8,128)(2,1)S(1)}, u32[]{:S(2)}, u32[]{:S(2)}) %all-to-all-start) | async-done | bytes 262176 | tf_op jit(solution)/shard_map/all_to_all | solution.py:120
  21.7 0.0 copy-start.1
  21.7 0.7 copy-done.1
  22.4 6.1 %shard_map.112 = (bf16[32,128,128]{2,1,0:T(8,128)(2,1)}, f32[32,8,128]{2,1,0:T(8,128)}) custom-call(s32[1]{0:T(128)} %bitcast.20.live_ref, s32[80]{0:T(128)} %bitcast.32, s32[80]{0:T(128)} %bitcast.35, bf16[80,128,128]{2,1,0:T(8,128)(2,1)} %bitcast.23, f32[80,1,128]{2,1,0:T(1,128)} %bitcast.26, bf16[8,128,128]{2,1,0:T(8,128)(2,1)} %copy-done.1), custom_call_target="tpu_custom_call" | custom-call | flops 356515840 | bytes 3932160 | tf_op jit(solution)/shard_map/pallas_call | solution.py:93
  28.5 0.9 slice.44
  29.4 0.0 copy-done.3
  29.4 0.3 broadcast_in_dim.11
  29.8 2.9 %pad_maximum_fusion = bf16[32,320,128]{2,1,0:T(8,128)(2,1)} fusion(bf16[32,192,128]{2,1,0:T(8,128)(2,1)S(1)} %broadcast_in_dim.11, bf16[32,128,128]{2,1,0:T(8,128)(2,1)} %get-tuple-element.5), kind=kLoop, calls=%fused_computation | loop fusion | flops 5242880 | bytes 5242880 | tf_op jit(solution)/shard_map/concatenate | solution.py:164
  32.7 17.7 %all-to-all-start.1 = ((bf16[32,320,128]{2,1,0:T(8,128)(2,1)}), bf16[32,320,128]{2,1,0:T(8,128)(2,1)S(1)}, u32[]{:S(2)}, u32[]{:S(2)}) async-start(bf16[32,320,128]{2,1,0:T(8,128)(2,1)} %pad_maximum_fusion), calls=%async_computation.1 | async-start | bytes 5242880 | tf_op jit(solution)/shard_map/all_to_all | solution.py:124
  50.4 33.9 %all-to-all-done.1 = bf16[32,320,128]{2,1,0:T(8,128)(2,1)S(1)} async-done(((bf16[32,320,128]{2,1,0:T(8,128)(2,1)}), bf16[32,320,128]{2,1,0:T(8,128)(2,1)S(1)}, u32[]{:S(2)}, u32[]{:S(2)}) %all-to-all-start.1) | async-done | bytes 2621472 | tf_op jit(solution)/shard_map/all_to_all | solution.py:124
  84.4 0.1 convert_reduce_fusion.1
  84.5 0.1 copy.34
  84.6 0.1 copy.35
  84.7 0.1 copy.29
  84.7 1.1 slice.62
  85.8 2.3 %copy.36 = bf16[32,128,128]{1,2,0:T(8,128)(2,1)} copy(bf16[32,128,128]{2,1,0:T(8,128)(2,1)} %slice.62) | data formatting | bytes 2097152
  88.1 0.2 dynamic-slice_reduce_fusion
  88.3 2.6 %fusion.1.src_ref = bf16[32,128,128]{2,1,0:T(8,128)(2,1)} fusion(bf16[32,128,128]{1,2,0:T(8,128)(2,1)} %copy.36, f32[32,128]{1,0:T(8,128)S(1)} %copy.29), kind=kLoop, calls=%fused_computation.7 | loop fusion | flops 1572864 | bytes 2113536 | tf_op jit(solution)/shard_map/transpose | solution.py:181
  90.9 0.0 copy-start.5
  90.9 0.0 copy-start.4
  90.9 5.7 %shard_map.113 = bf16[8,128,128]{2,1,0:T(8,128)(2,1)} custom-call(s32[1]{0:T(128)} %bitcast.21.live_ref, s32[80]{0:T(128)} %bitcast.33, s32[80]{0:T(128)} %bitcast.36, bf16[80,128,128]{2,1,0:T(8,128)(2,1)} %bitcast.24, f32[80,1,128]{2,1,0:T(1,128)} %bitcast.27, bf16[32,128,128]{2,1,0:T(8,128)(2,1)} %fusion.1.src_ref), custom_call_target="tpu_custom_call" | custom-call | flops 335544320 | bytes 3932160 | tf_op jit(solution)/shard_map/pallas_call | solution.py:108
  96.6 0.0 copy-start.2
  96.6 0.2 convert_reduce_fusion
  96.7 0.0 copy-done.5
  96.7 0.1 add_convert_fusion.1
  96.8 0.0 copy-done.4
  96.8 0.2 fusion.13
  97.0 0.0 copy-done
  97.0 0.2 fusion.12
  97.3 0.3 copy-done.2
  97.5 0.8 pad_maximum_fusion.2
  98.4 3.5 %all-to-all-start.2 = ((bf16[8,256,128]{2,1,0:T(8,128)(2,1)}), bf16[8,256,128]{2,1,0:T(8,128)(2,1)S(1)}, u32[]{:S(2)}, u32[]{:S(2)}) async-start(bf16[8,256,128]{2,1,0:T(8,128)(2,1)} %pad_maximum_fusion.2), calls=%async_computation.2 | async-start | bytes 1048576 | tf_op jit(solution)/shard_map/all_to_all | solution.py:124
  101.9 0.1 copy.31
  102.0 16.6 %all-to-all-done.2 = bf16[8,256,128]{2,1,0:T(8,128)(2,1)S(1)} async-done(((bf16[8,256,128]{2,1,0:T(8,128)(2,1)}), bf16[8,256,128]{2,1,0:T(8,128)(2,1)S(1)}, u32[]{:S(2)}, u32[]{:S(2)}) %all-to-all-start.2) | async-done | bytes 524320 | tf_op jit(solution)/shard_map/all_to_all | solution.py:124
  118.7 0.4 fusion
  119.1 0.4 fusion.8
  119.4 0.2 fusion.14
  119.7 0.1 fusion.2
  119.8 0.7 slice.63.src_ref
  120.5 5.9 %shard_map.114 = bf16[32,128,128]{2,1,0:T(8,128)(2,1)} custom-call(s32[1]{0:T(128)} %bitcast.22.live_ref, s32[80]{0:T(128)} %bitcast.34, s32[80]{0:T(128)} %bitcast.37, bf16[80,128,128]{2,1,0:T(8,128)(2,1)} %bitcast.25, f32[80,1,128]{2,1,0:T(1,128)} %bitcast.28, bf16[8,128,128]{2,1,0:T(8,128)(2,1)} %slice.63.src_ref), custom_call_target="tpu_custom_call" | custom-call | flops 335544320 | bytes 3932160 | tf_op jit(solution)/shard_map/pallas_call | solution.py:93
  126.4 1.4 pad_maximum_fusion.1
  127.8 43.5 %all_to_all.30 = bf16[32,192,128]{2,1,0:T(8,128)(2,1)S(1)} all-to-all(bf16[32,192,128]{2,1,0:T(8,128)(2,1)S(1)} %pad_maximum_fusion.1), channel_id=1, replica_groups=mesh['row'=8,'col'=32] {'col'}, dimensions={0} | all-to-all | bytes 3145728 | tf_op jit(solution)/shard_map/all_to_all | solution.py:124
  171.2 0.3 convert_element_type.91
  171.6 0.1 slice_reduce_fusion.1
  171.7 10.7 %all_to_all.31 = f32[8,32,128]{2,1,0:T(8,128)S(1)} all-to-all(f32[8,32,128]{2,1,0:T(8,128)S(1)} %broadcast_in_dim.13), channel_id=1, replica_groups=mesh['row'=8,'col'=32] {'row'}, dimensions={0} | all-to-all | bytes 262144 | tf_op jit(solution)/shard_map/all_to_all | solution.py:120
  182.4 0.9 broadcast_in_dim.14
  183.3 5.9 %all-to-all-start.5 = ((f32[32,32,128]{2,1,0:T(8,128)}), f32[32,32,128]{2,1,0:T(8,128)}, u32[]{:S(2)}, u32[]{:S(2)}) async-start(f32[32,32,128]{2,1,0:T(8,128)} %broadcast_in_dim.14), calls=%async_computation.5 | async-start | bytes 1048576 | tf_op jit(solution)/shard_map/all_to_all | solution.py:120
  189.2 0.1 slice_reduce_fusion
  189.3 0.7 add_convert_fusion
  190.0 10.8 %all-to-all-done.5 = f32[32,32,128]{2,1,0:T(8,128)} async-done(((f32[32,32,128]{2,1,0:T(8,128)}), f32[32,32,128]{2,1,0:T(8,128)}, u32[]{:S(2)}, u32[]{:S(2)}) %all-to-all-start.5) | async-done | bytes 524320 | tf_op jit(solution)/shard_map/all_to_all | solution.py:120
  200.8 1.8 fusion.10
  202.5 0.7 reshape.47
  (10 shorter events, 0.2 us)
Async XLA Ops:
  0.6 96.4 %copy-start = (bf16[512,128]{1,0:T(8,128)(2,1)S(1)}, bf16[512,128]{1,0:T(8,128)(2,1)}, u32[]{:S(2)}) copy-start(bf16[512,128]{1,0:T(8,128)(2,1)} %param.11) | copy-start | bytes 393220
  0.6 28.8 %copy-start.3 = (bf16[128,128]{1,0:T(8,128)(2,1)S(1)}, bf16[128,128]{1,0:T(8,128)(2,1)}, u32[]{:S(2)}) copy-start(bf16[128,128]{1,0:T(8,128)(2,1)} %param.17) | copy-start | bytes 98308
  2.2 19.5 %all-to-all-start = ((bf16[8,128,128]{2,1,0:T(8,128)(2,1)}), bf16[8,128,128]{2,1,0:T(8,128)(2,1)S(1)}, u32[]{:S(2)}, u32[]{:S(2)}) async-start(bf16[8,128,128]{2,1,0:T(8,128)(2,1)} %broadcast_in_dim.10), calls=%async_computation | async-start | bytes 524288 | tf_op jit(solution)/shard_map/all_to_all | solution.py:120
  21.7 0.7 copy-start.1
  32.7 51.6 %all-to-all-start.1 = ((bf16[32,320,128]{2,1,0:T(8,128)(2,1)}), bf16[32,320,128]{2,1,0:T(8,128)(2,1)S(1)}, u32[]{:S(2)}, u32[]{:S(2)}) async-start(bf16[32,320,128]{2,1,0:T(8,128)(2,1)} %pad_maximum_fusion), calls=%async_computation.1 | async-start | bytes 5242880 | tf_op jit(solution)/shard_map/all_to_all | solution.py:124
  90.9 5.8 %copy-start.5 = (bf16[128,128]{1,0:T(8,128)(2,1)S(1)}, bf16[128,128]{1,0:T(8,128)(2,1)}, u32[]{:S(2)}) copy-start(bf16[128,128]{1,0:T(8,128)(2,1)} %param.9) | copy-start | bytes 98308
  90.9 5.9 %copy-start.4 = (bf16[128,512]{1,0:T(8,128)(2,1)S(1)}, bf16[128,512]{1,0:T(8,128)(2,1)}, u32[]{:S(2)}) copy-start(bf16[128,512]{1,0:T(8,128)(2,1)} %param.10) | copy-start | bytes 393220
  96.6 0.9 copy-start.2
  98.4 20.3 %all-to-all-start.2 = ((bf16[8,256,128]{2,1,0:T(8,128)(2,1)}), bf16[8,256,128]{2,1,0:T(8,128)(2,1)S(1)}, u32[]{:S(2)}, u32[]{:S(2)}) async-start(bf16[8,256,128]{2,1,0:T(8,128)(2,1)} %pad_maximum_fusion.2), calls=%async_computation.2 | async-start | bytes 1048576 | tf_op jit(solution)/shard_map/all_to_all | solution.py:124
  183.3 17.5 %all-to-all-start.5 = ((f32[32,32,128]{2,1,0:T(8,128)}), f32[32,32,128]{2,1,0:T(8,128)}, u32[]{:S(2)}, u32[]{:S(2)}) async-start(f32[32,32,128]{2,1,0:T(8,128)} %broadcast_in_dim.14), calls=%async_computation.5 | async-start | bytes 1048576 | tf_op jit(solution)/shard_map/all_to_all | solution.py:120

commit v3 on v2

--- a/solution.py
+++ b/solution.py
@@ -25,8 +25,16 @@
     )
 
 
-def _masked_tile(tiles_ref, mask_ref, s):
-    return (tiles_ref[s].astype(jnp.float32) * mask_ref[s]).astype(jnp.bfloat16)
+UNROLL = 8
+
+
+def _slot(k, u, n_live, slots):
+    index = k * UNROLL + u
+    return jnp.minimum(index, slots - 1), (index < n_live).astype(jnp.float32)
+
+
+def _masked_tile(tiles_ref, mask_ref, s, keep):
+    return (tiles_ref[s].astype(jnp.float32) * (mask_ref[s] * keep)).astype(jnp.bfloat16)
 
 
 def _forward_kernel(with_degree, live_ref, rows_ref, cols_ref, tiles_ref, mask_ref, src_ref, *rest):
@@ -41,19 +49,22 @@
     if with_degree:
         dacc_ref[...] = jnp.zeros_like(dacc_ref)
     ones = jnp.ones((8, BLOCK), jnp.bfloat16)
-
-    def body(s, carry):
-        r = jnp.clip(rows_ref[s], 0, n_dst - 1)
-        c = jnp.clip(cols_ref[s], 0, n_src - 1)
-        tile = _masked_tile(tiles_ref, mask_ref, s)
-        acc_ref[r] += jnp.dot(tile, src_ref[c], preferred_element_type=jnp.float32)
-        if with_degree:
-            dacc_ref[r] += lax.dot_general(
-                ones, tile, (((1,), (1,)), ((), ())), preferred_element_type=jnp.float32
-            )
+    n_live = jnp.clip(live_ref[0], 0, slots)
+
+    def body(k, carry):
+        for u in range(UNROLL):
+            s, keep = _slot(k, u, n_live, slots)
+            r = jnp.clip(rows_ref[s], 0, n_dst - 1)
+            c = jnp.clip(cols_ref[s], 0, n_src - 1)
+            tile = _masked_tile(tiles_ref, mask_ref, s, keep)
+            acc_ref[r] += jnp.dot(tile, src_ref[c], preferred_element_type=jnp.float32)
+            if with_degree:
+                dacc_ref[r] += lax.dot_general(
+                    ones, tile, (((1,), (1,)), ((), ())), preferred_element_type=jnp.float32
+                )
         return carry
 
-    lax.fori_loop(0, jnp.clip(live_ref[0], 0, slots), body, 0)
+    lax.fori_loop(0, (n_live + UNROLL - 1) // UNROLL, body, 0)
     out_ref[...] = acc_ref[...].astype(out_ref.dtype)
     if with_degree:
         deg_ref[...] = dacc_ref[...]
@@ -64,15 +75,18 @@
     n_dst = acc_ref.shape[0]
     n_src = src_ref.shape[0]
     acc_ref[...] = jnp.zeros_like(acc_ref)
-
-    def body(s, carry):
-        r = jnp.clip(rows_ref[s], 0, n_src - 1)
-        c = jnp.clip(cols_ref[s], 0, n_dst - 1)
-        tile = _masked_tile(tiles_ref, mask_ref, s)
-        acc_ref[c] += jnp.dot(src_ref[r], tile, preferred_element_type=jnp.float32)
+    n_live = jnp.clip(live_ref[0], 0, slots)
+
+    def body(k, carry):
+        for u in range(UNROLL):
+            s, keep = _slot(k, u, n_live, slots)
+            r = jnp.clip(rows_ref[s], 0, n_src - 1)
+            c = jnp.clip(cols_ref[s], 0, n_dst - 1)
+            tile = _masked_tile(tiles_ref, mask_ref, s, keep)
+            acc_ref[c] += jnp.dot(src_ref[r], tile, preferred_element_type=jnp.float32)
         return carry
 
-    lax.fori_loop(0, jnp.clip(live_ref[0], 0, slots), body, 0)
+    lax.fori_loop(0, (n_live + UNROLL - 1) // UNROLL, body, 0)
     out_ref[...] = acc_ref[...].astype(out_ref.dtype)
 
 

time: 205 us -> 180 us (0.88)
  blocking collectives: 54.2 us -> 44.2 us
  Pallas kernels: 17.7 us -> 11.5 us
  starting transfers between devices: 36.1 us -> 30.3 us
    all_to_all x1, blocking collectives: 43.5 us -> 33.5 us  [scatter_blocks(): return lax.all_to_all(blocks, axis, 0, 0, tiled=False)]
    all_to_all x2, starting transfers between devices: 21.2 us -> 15.4 us  [scatter_blocks(): return lax.all_to_all(blocks, axis, 0, 0, tiled=False)]
    pallas_call x2, Pallas kernels: 12 us -> 7.9 us  [forward_aggregate(): pl.pallas_call(functools.partial(_forward_kernel, with_degree), out_shape...]
    pallas_call x1, Pallas kernels: 5.69 us -> 3.56 us  [transpose_aggregate(): pl.pallas_call(_transpose_kernel, out_shape=jax.ShapeDtypeStruct((n_dst,...]
where the time goes in v3:
time: 180 us
  waiting for transfers between devices  68.1 us (38%)
  blocking collectives  44.2 us (25%)
  starting transfers between devices  30.3 us (17%)
  local copies, waits for them, and re-layouts  11.9 us (7%)
  Pallas kernels  11.5 us (6%)
  other arithmetic  10.8 us (6%)
    all_to_all x2, waiting for transfers between devices, scatter_blocks(): return lax.all_to_all(blocks, axis, 0, 0, tiled=False)  48.9 us
    all_to_all x1, blocking collectives, scatter_blocks(): return lax.all_to_all(blocks, axis, 0, 0, tiled=False)  33.5 us
    all_to_all x2, waiting for transfers between devices, gather_blocks(): lax.all_to_all(jnp.broadcast_to(block[None], (n,) + block.shape), axis, 0...  19.2 us
    all_to_all x2, starting transfers between devices, scatter_blocks(): return lax.all_to_all(blocks, axis, 0, 0, tiled=False)  15.4 us
    all_to_all x2, starting transfers between devices, gather_blocks(): lax.all_to_all(jnp.broadcast_to(block[None], (n,) + block.shape), axis, 0...  14.9 us
    all_to_all x1, blocking collectives, gather_blocks(): lax.all_to_all(jnp.broadcast_to(block[None], (n,) + block.shape), axis, 0...  10.7 us
    pallas_call x2, Pallas kernels, forward_aggregate(): pl.pallas_call(functools.partial(_forward_kernel, with_degree), out_shape...  7.9 us
  transfers between devices with their start and end apart: 4, of which 4 were waited for; matrix products, arithmetic and copies ran while one was open for 1% of the time, Pallas kernels for 0%

profile of v3, /device:TPU:1, one launch (start us, length us, event | category | flops | bytes accessed | tf_op | source)
XLA Modules:
  0.0 179.6 jit_solution(16121671268331456867)
XLA Ops:
  0.6 0.0 copy-start
  0.6 0.0 copy-start.3
  0.7 1.5 broadcast_in_dim.10
  2.2 9.0 %all-to-all-start = ((bf16[8,128,128]{2,1,0:T(8,128)(2,1)}), bf16[8,128,128]{2,1,0:T(8,128)(2,1)S(1)}, u32[]{:S(2)}, u32[]{:S(2)}) async-start(bf16[8,128,128]{2,1,0:T(8,128)(2,1)} %broadcast_in_dim.10), calls=%async_computation | async-start | bytes 524288 | tf_op jit(solution)/shard_map/all_to_all | solution.py:134
  11.2 1.4 convert_element_type.73
  13.2 8.4 %all-to-all-done.src_ref = bf16[8,128,128]{2,1,0:T(8,128)(2,1)S(1)} async-done(((bf16[8,128,128]{2,1,0:T(8,128)(2,1)}), bf16[8,128,128]{2,1,0:T(8,128)(2,1)S(1)}, u32[]{:S(2)}, u32[]{:S(2)}) %all-to-all-start) | async-done | bytes 262176 | tf_op jit(solution)/shard_map/all_to_all | solution.py:134
  21.7 0.0 copy-start.1
  21.7 0.7 copy-done.1
  22.4 4.2 %shard_map.112 = (bf16[32,128,128]{2,1,0:T(8,128)(2,1)}, f32[32,8,128]{2,1,0:T(8,128)}) custom-call(s32[1]{0:T(128)} %bitcast.20.live_ref, s32[80]{0:T(128)} %bitcast.32, s32[80]{0:T(128)} %bitcast.35, bf16[80,128,128]{2,1,0:T(8,128)(2,1)} %bitcast.23, f32[80,1,128]{2,1,0:T(1,128)} %bitcast.26, bf16[8,128,128]{2,1,0:T(8,128)(2,1)} %copy-done.1), custom_call_target="tpu_custom_call" | custom-call | flops 356515840 | bytes 3932160 | tf_op jit(solution)/shard_map/pallas_call | solution.py:107
  26.6 0.9 slice.44
  27.5 0.0 copy-done.3
  27.5 0.3 broadcast_in_dim.11
  27.9 2.9 %pad_maximum_fusion = bf16[32,320,128]{2,1,0:T(8,128)(2,1)} fusion(bf16[32,192,128]{2,1,0:T(8,128)(2,1)S(1)} %broadcast_in_dim.11, bf16[32,128,128]{2,1,0:T(8,128)(2,1)} %get-tuple-element.5), kind=kLoop, calls=%fused_computation | loop fusion | flops 5242880 | bytes 5242880 | tf_op jit(solution)/shard_map/concatenate | solution.py:178
  30.8 11.9 %all-to-all-start.1 = ((bf16[32,320,128]{2,1,0:T(8,128)(2,1)}), bf16[32,320,128]{2,1,0:T(8,128)(2,1)S(1)}, u32[]{:S(2)}, u32[]{:S(2)}) async-start(bf16[32,320,128]{2,1,0:T(8,128)(2,1)} %pad_maximum_fusion), calls=%async_computation.1 | async-start | bytes 5242880 | tf_op jit(solution)/shard_map/all_to_all | solution.py:138
  42.7 33.9 %all-to-all-done.1 = bf16[32,320,128]{2,1,0:T(8,128)(2,1)S(1)} async-done(((bf16[32,320,128]{2,1,0:T(8,128)(2,1)}), bf16[32,320,128]{2,1,0:T(8,128)(2,1)S(1)}, u32[]{:S(2)}, u32[]{:S(2)}) %all-to-all-start.1) | async-done | bytes 2621472 | tf_op jit(solution)/shard_map/all_to_all | solution.py:138
  76.7 0.1 convert_reduce_fusion.1
  76.8 0.1 copy.34
  76.9 0.1 copy.35
  77.0 0.1 copy.29
  77.1 1.1 slice.62
  78.2 2.3 %copy.36 = bf16[32,128,128]{1,2,0:T(8,128)(2,1)} copy(bf16[32,128,128]{2,1,0:T(8,128)(2,1)} %slice.62) | data formatting | bytes 2097152
  80.4 0.2 dynamic-slice_reduce_fusion
  80.6 2.6 %fusion.1.src_ref = bf16[32,128,128]{2,1,0:T(8,128)(2,1)} fusion(bf16[32,128,128]{1,2,0:T(8,128)(2,1)} %copy.36, f32[32,128]{1,0:T(8,128)S(1)} %copy.29), kind=kLoop, calls=%fused_computation.7 | loop fusion | flops 1572864 | bytes 2113536 | tf_op jit(solution)/shard_map/transpose | solution.py:195
  83.2 0.0 copy-start.5
  83.2 0.0 copy-start.4
  83.2 3.6 %shard_map.113 = bf16[8,128,128]{2,1,0:T(8,128)(2,1)} custom-call(s32[1]{0:T(128)} %bitcast.21.live_ref, s32[80]{0:T(128)} %bitcast.33, s32[80]{0:T(128)} %bitcast.36, bf16[80,128,128]{2,1,0:T(8,128)(2,1)} %bitcast.24, f32[80,1,128]{2,1,0:T(1,128)} %bitcast.27, bf16[32,128,128]{2,1,0:T(8,128)(2,1)} %fusion.1.src_ref), custom_call_target="tpu_custom_call" | custom-call | flops 335544320 | bytes 3932160 | tf_op jit(solution)/shard_map/pallas_call | solution.py:122
  86.8 0.0 copy-start.2
  86.8 0.2 convert_reduce_fusion
  86.9 0.0 copy-done.5
  86.9 0.1 add_convert_fusion.1
  87.0 0.0 copy-done.4
  87.0 0.2 fusion.13
  87.2 0.0 copy-done
  87.2 0.2 fusion.12
  87.5 0.3 copy-done.2
  87.7 0.8 pad_maximum_fusion.2
  88.6 3.5 %all-to-all-start.2 = ((bf16[8,256,128]{2,1,0:T(8,128)(2,1)}), bf16[8,256,128]{2,1,0:T(8,128)(2,1)S(1)}, u32[]{:S(2)}, u32[]{:S(2)}) async-start(bf16[8,256,128]{2,1,0:T(8,128)(2,1)} %pad_maximum_fusion.2), calls=%async_computation.2 | async-start | bytes 1048576 | tf_op jit(solution)/shard_map/all_to_all | solution.py:138
  92.1 0.1 copy.31
  92.2 15.0 %all-to-all-done.2 = bf16[8,256,128]{2,1,0:T(8,128)(2,1)S(1)} async-done(((bf16[8,256,128]{2,1,0:T(8,128)(2,1)}), bf16[8,256,128]{2,1,0:T(8,128)(2,1)S(1)}, u32[]{:S(2)}, u32[]{:S(2)}) %all-to-all-start.2) | async-done | bytes 524320 | tf_op jit(solution)/shard_map/all_to_all | solution.py:138
  107.2 0.4 fusion
  107.6 0.4 fusion.8
  107.9 0.2 fusion.14
  108.2 0.1 fusion.2
  108.3 0.7 slice.63.src_ref
  109.0 3.7 %shard_map.114 = bf16[32,128,128]{2,1,0:T(8,128)(2,1)} custom-call(s32[1]{0:T(128)} %bitcast.22.live_ref, s32[80]{0:T(128)} %bitcast.34, s32[80]{0:T(128)} %bitcast.37, bf16[80,128,128]{2,1,0:T(8,128)(2,1)} %bitcast.25, f32[80,1,128]{2,1,0:T(1,128)} %bitcast.28, bf16[8,128,128]{2,1,0:T(8,128)(2,1)} %slice.63.src_ref), custom_call_target="tpu_custom_call" | custom-call | flops 335544320 | bytes 3932160 | tf_op jit(solution)/shard_map/pallas_call | solution.py:107
  112.7 1.4 pad_maximum_fusion.1
  114.1 33.5 %all_to_all.30 = bf16[32,192,128]{2,1,0:T(8,128)(2,1)S(1)} all-to-all(bf16[32,192,128]{2,1,0:T(8,128)(2,1)S(1)} %pad_maximum_fusion.1), channel_id=1, replica_groups=mesh['row'=8,'col'=32] {'col'}, dimensions={0} | all-to-all | bytes 3145728 | tf_op jit(solution)/shard_map/all_to_all | solution.py:138
  147.6 0.3 convert_element_type.91
  147.9 0.1 slice_reduce_fusion.1
  148.0 10.7 %all_to_all.31 = f32[8,32,128]{2,1,0:T(8,128)S(1)} all-to-all(f32[8,32,128]{2,1,0:T(8,128)S(1)} %broadcast_in_dim.13), channel_id=1, replica_groups=mesh['row'=8,'col'=32] {'row'}, dimensions={0} | all-to-all | bytes 262144 | tf_op jit(solution)/shard_map/all_to_all | solution.py:134
  158.7 0.9 broadcast_in_dim.14
  159.6 5.9 %all-to-all-start.5 = ((f32[32,32,128]{2,1,0:T(8,128)}), f32[32,32,128]{2,1,0:T(8,128)}, u32[]{:S(2)}, u32[]{:S(2)}) async-start(f32[32,32,128]{2,1,0:T(8,128)} %broadcast_in_dim.14), calls=%async_computation.5 | async-start | bytes 1048576 | tf_op jit(solution)/shard_map/all_to_all | solution.py:134
  165.5 0.1 slice_reduce_fusion
  165.6 0.7 add_convert_fusion
  166.3 10.8 %all-to-all-done.5 = f32[32,32,128]{2,1,0:T(8,128)} async-done(((f32[32,32,128]{2,1,0:T(8,128)}), f32[32,32,128]{2,1,0:T(8,128)}, u32[]{:S(2)}, u32[]{:S(2)}) %all-to-all-start.5) | async-done | bytes 524320 | tf_op jit(solution)/shard_map/all_to_all | solution.py:134
  177.1 1.8 fusion.10
  178.9 0.7 reshape.47
  (10 shorter events, 0.2 us)
Async XLA Ops:
  0.6 86.6 %copy-start = (bf16[512,128]{1,0:T(8,128)(2,1)S(1)}, bf16[512,128]{1,0:T(8,128)(2,1)}, u32[]{:S(2)}) copy-start(bf16[512,128]{1,0:T(8,128)(2,1)} %param.11) | copy-start | bytes 393220
  0.6 26.9 %copy-start.3 = (bf16[128,128]{1,0:T(8,128)(2,1)S(1)}, bf16[128,128]{1,0:T(8,128)(2,1)}, u32[]{:S(2)}) copy-start(bf16[128,128]{1,0:T(8,128)(2,1)} %param.17) | copy-start | bytes 98308
  2.2 19.5 %all-to-all-start = ((bf16[8,128,128]{2,1,0:T(8,128)(2,1)}), bf16[8,128,128]{2,1,0:T(8,128)(2,1)S(1)}, u32[]{:S(2)}, u32[]{:S(2)}) async-start(bf16[8,128,128]{2,1,0:T(8,128)(2,1)} %broadcast_in_dim.10), calls=%async_computation | async-start | bytes 524288 | tf_op jit(solution)/shard_map/all_to_all | solution.py:134
  21.7 0.7 copy-start.1
  30.8 45.9 %all-to-all-start.1 = ((bf16[32,320,128]{2,1,0:T(8,128)(2,1)}), bf16[32,320,128]{2,1,0:T(8,128)(2,1)S(1)}, u32[]{:S(2)}, u32[]{:S(2)}) async-start(bf16[32,320,128]{2,1,0:T(8,128)(2,1)} %pad_maximum_fusion), calls=%async_computation.1 | async-start | bytes 5242880 | tf_op jit(solution)/shard_map/all_to_all | solution.py:138
  83.2 3.7 %copy-start.5 = (bf16[128,128]{1,0:T(8,128)(2,1)S(1)}, bf16[128,128]{1,0:T(8,128)(2,1)}, u32[]{:S(2)}) copy-start(bf16[128,128]{1,0:T(8,128)(2,1)} %param.9) | copy-start | bytes 98308
  83.2 3.8 %copy-start.4 = (bf16[128,512]{1,0:T(8,128)(2,1)S(1)}, bf16[128,512]{1,0:T(8,128)(2,1)}, u32[]{:S(2)}) copy-start(bf16[128,512]{1,0:T(8,128)(2,1)} %param.10) | copy-start | bytes 393220
  86.8 0.9 copy-start.2
  88.6 18.6 %all-to-all-start.2 = ((bf16[8,256,128]{2,1,0:T(8,128)(2,1)}), bf16[8,256,128]{2,1,0:T(8,128)(2,1)S(1)}, u32[]{:S(2)}, u32[]{:S(2)}) async-start(bf16[8,256,128]{2,1,0:T(8,128)(2,1)} %pad_maximum_fusion.2), calls=%async_computation.2 | async-start | bytes 1048576 | tf_op jit(solution)/shard_map/all_to_all | solution.py:138
  159.6 17.5 %all-to-all-start.5 = ((f32[32,32,128]{2,1,0:T(8,128)}), f32[32,32,128]{2,1,0:T(8,128)}, u32[]{:S(2)}, u32[]{:S(2)}) async-start(f32[32,32,128]{2,1,0:T(8,128)} %broadcast_in_dim.14), calls=%async_computation.5 | async-start | bytes 1048576 | tf_op jit(solution)/shard_map/all_to_all | solution.py:134

commit v4 on v3

--- a/solution.py
+++ b/solution.py
@@ -25,7 +25,7 @@
     )
 
 
-UNROLL = 8
+UNROLL = 16
 
 
 def _slot(k, u, n_live, slots):
@@ -173,16 +173,14 @@
     partial_in, partial_deg = forward_aggregate(
         live, rows, cols, tiles, mask, x_panel, row_groups, with_degree=True
     )
-    deg_hi, deg_lo = split_hi_lo(partial_deg[:, 0, :])
-    shared = jnp.concatenate([deg_hi, deg_lo, cotangent], axis=0)
+    shared = jnp.concatenate([partial_deg[:, 0, :].astype(bf16), cotangent], axis=0)
     packed = jnp.concatenate(
         [partial_in, jnp.broadcast_to(shared[None], (row_groups,) + shared.shape)], axis=1
     )
     arrived = scatter_blocks(packed, "col")
     summed_in = jnp.sum(arrived[:, :BLOCK].astype(f32), axis=0)
-    degrees = jnp.sum(arrived[:, BLOCK : BLOCK + 2 * row_groups].astype(f32), axis=0)
-    degrees = degrees[:row_groups] + degrees[row_groups:]
-    group_cot = arrived[:, BLOCK + 2 * row_groups :]
+    degrees = jnp.sum(arrived[:, BLOCK : BLOCK + row_groups].astype(f32), axis=0)
+    group_cot = arrived[:, BLOCK + row_groups :]
     group_scale = 1.0 / jnp.sqrt(1.0 + degrees)
     me = lax.axis_index("col")
     row_scale = lax.dynamic_index_in_dim(group_scale, me, axis=0, keepdims=False)[:, None]
@@ -215,18 +213,15 @@
     node_scale = 1.0 / math.sqrt(node_count * n_rows_axis * n_cols_axis)
     flat = jnp.concatenate([first_term.reshape(-1), second_term.reshape(-1)]) * node_scale
     slices = flat.reshape(row_groups, -1, BLOCK)
-    slice_rows = slices.shape[1]
-    grad_hi, grad_lo = split_hi_lo(slices)
-
-    packed = jnp.concatenate([partial_y, grad_hi, grad_lo], axis=1)
+
+    packed = jnp.concatenate([partial_y, slices.astype(bf16)], axis=1)
     arrived = scatter_blocks(packed, "col").astype(f32)
     summed_y = jnp.sum(arrived[:, :BLOCK], axis=0)
     output = (projected + row_scale * summed_y).astype(bf16)
     part = jnp.sum(arrived[:, BLOCK:], axis=0)
-    part = part[:slice_rows] + part[slice_rows:]
-
-    total = jnp.sum(gather_blocks(part, "row"), axis=0)
-    everything = gather_blocks(total, "col").reshape(-1)
+
+    total = jnp.sum(gather_blocks(part.astype(bf16), "row").astype(f32), axis=0)
+    everything = gather_blocks(total.astype(bf16), "col").astype(f32).reshape(-1)
     split = first_term.size
     first_grad = everything[:split].reshape(first_term.shape)
     second_grad = everything[split:].reshape(second_term.shape)

time: 180 us -> 165 us (0.917)
  blocking collectives: 44.2 us -> 38.5 us
  waiting for transfers between devices: 68.1 us -> 63.9 us
  local copies, waits for them, and re-layouts: 11.9 us -> 9.26 us
    all_to_all x1, blocking collectives: 33.5 us -> 29 us  [scatter_blocks(): return lax.all_to_all(blocks, axis, 0, 0, tiled=False)]
    all_to_all x2, waiting for transfers between devices: 19.2 us -> 16.6 us  [gather_blocks(): lax.all_to_all(jnp.broadcast_to(block[None], (n,) + block.shape), axis, 0...]
where the time goes in v4:
time: 165 us; the launch traced here: 164 us
  waiting for transfers between devices  63.9 us (39%)
  blocking collectives  38.5 us (23%)
  starting transfers between devices  29.3 us (18%)
  other arithmetic  10.1 us (6%)
  Pallas kernels  10.1 us (6%)
  local copies, waits for them, and re-layouts  9.26 us (6%)
    all_to_all x2, waiting for transfers between devices, scatter_blocks(): return lax.all_to_all(blocks, axis, 0, 0, tiled=False)  47.3 us
    all_to_all x1, blocking collectives, scatter_blocks(): return lax.all_to_all(blocks, axis, 0, 0, tiled=False)  29 us
    all_to_all x2, waiting for transfers between devices, gather_blocks(): lax.all_to_all(jnp.broadcast_to(block[None], (n,) + block.shape), axis, 0...  16.6 us
    all_to_all x2, starting transfers between devices, scatter_blocks(): return lax.all_to_all(blocks, axis, 0, 0, tiled=False)  15.3 us
    all_to_all x2, starting transfers between devices, gather_blocks(): lax.all_to_all(jnp.broadcast_to(block[None], (n,) + block.shape), axis, 0...  14 us
    all_to_all x1, blocking collectives, gather_blocks(): lax.all_to_all(jnp.broadcast_to(block[None], (n,) + block.shape), axis, 0...  9.53 us
    pallas_call x2, Pallas kernels, forward_aggregate(): pl.pallas_call(functools.partial(_forward_kernel, with_degree), out_shape...  6.97 us
  transfers between devices with their start and end apart: 4, of which 4 were waited for; matrix products, arithmetic and copies ran while one was open for 1% of the time, Pallas kernels for 0%

profile of v4, /device:TPU:1, one launch (start us, length us, event | category | flops | bytes accessed | tf_op | source)
XLA Modules:
  0.0 164.1 jit_solution(11607430016091827212)
XLA Ops:
  0.6 0.0 copy-start
  0.6 0.0 copy-start.4
  0.7 1.5 broadcast_in_dim.10
  2.2 9.0 %all-to-all-start = ((bf16[8,128,128]{2,1,0:T(8,128)(2,1)}), bf16[8,128,128]{2,1,0:T(8,128)(2,1)S(1)}, u32[]{:S(2)}, u32[]{:S(2)}) async-start(bf16[8,128,128]{2,1,0:T(8,128)(2,1)} %broadcast_in_dim.10), calls=%async_computation | async-start | bytes 524288 | tf_op jit(solution)/shard_map/all_to_all | solution.py:134
  11.2 1.4 convert_element_type.74
  13.2 8.5 %all-to-all-done.src_ref = bf16[8,128,128]{2,1,0:T(8,128)(2,1)S(1)} async-done(((bf16[8,128,128]{2,1,0:T(8,128)(2,1)}), bf16[8,128,128]{2,1,0:T(8,128)(2,1)S(1)}, u32[]{:S(2)}, u32[]{:S(2)}) %all-to-all-start) | async-done | bytes 262176 | tf_op jit(solution)/shard_map/all_to_all | solution.py:134
  21.7 0.0 copy-start.1
  21.7 0.7 copy-done.1
  22.4 3.7 %shard_map.112 = (bf16[32,128,128]{2,1,0:T(8,128)(2,1)}, f32[32,8,128]{2,1,0:T(8,128)}) custom-call(s32[1]{0:T(128)} %bitcast.24.live_ref, s32[80]{0:T(128)} %bitcast.36, s32[80]{0:T(128)} %bitcast.39, bf16[80,128,128]{2,1,0:T(8,128)(2,1)} %bitcast.27, f32[80,1,128]{2,1,0:T(1,128)} %bitcast.30, bf16[8,128,128]{2,1,0:T(8,128)(2,1)} %copy-done.1), custom_call_target="tpu_custom_call" | custom-call | flops 356515840 | bytes 3932160 | tf_op jit(solution)/shard_map/pallas_call | solution.py:107
  26.1 0.9 slice.59
  27.0 0.0 copy-done.4
  27.0 0.2 broadcast_in_dim.11
  27.2 2.8 %pad_maximum_fusion = bf16[32,288,128]{2,1,0:T(8,128)(2,1)} fusion(bf16[32,160,128]{2,1,0:T(8,128)(2,1)S(1)} %broadcast_in_dim.11, bf16[32,128,128]{2,1,0:T(8,128)(2,1)} %get-tuple-element.5), kind=kLoop, calls=%fused_computation | loop fusion | flops 4718592 | bytes 4718592 | tf_op jit(solution)/shard_map/concatenate | solution.py:177
  30.0 11.8 %all-to-all-start.1 = ((bf16[32,288,128]{2,1,0:T(8,128)(2,1)}), bf16[32,288,128]{2,1,0:T(8,128)(2,1)S(1)}, u32[]{:S(2)}, u32[]{:S(2)}) async-start(bf16[32,288,128]{2,1,0:T(8,128)(2,1)} %pad_maximum_fusion), calls=%async_computation.1 | async-start | bytes 4718592 | tf_op jit(solution)/shard_map/all_to_all | solution.py:138
  41.8 31.5 %all-to-all-done.1 = bf16[32,288,128]{2,1,0:T(8,128)(2,1)S(1)} async-done(((bf16[32,288,128]{2,1,0:T(8,128)(2,1)}), bf16[32,288,128]{2,1,0:T(8,128)(2,1)S(1)}, u32[]{:S(2)}, u32[]{:S(2)}) %all-to-all-start.1) | async-done | bytes 2359328 | tf_op jit(solution)/shard_map/all_to_all | solution.py:138
  73.4 1.1 slice.46
  74.5 1.6 copy.43
  76.1 0.0 copy-start.3
  76.1 0.0 copy-start.2
  76.2 0.0 copy-start.6
  76.2 1.3 fusion.1.src_ref
  77.4 0.2 convert_reduce_fusion
  77.6 0.0 copy-done.3
  77.6 0.1 add_convert_fusion.1
  77.7 0.0 copy-done.2
  77.7 0.2 fusion.12
  77.9 0.0 copy-done
  77.9 0.2 fusion.11
  78.1 0.0 copy-done.6
  78.1 0.0 copy-start.5
  78.1 3.1 %shard_map.113 = bf16[8,128,128]{2,1,0:T(8,128)(2,1)} custom-call(s32[1]{0:T(128)} %bitcast.25.live_ref, s32[80]{0:T(128)} %bitcast.37, s32[80]{0:T(128)} %bitcast.40, bf16[80,128,128]{2,1,0:T(8,128)(2,1)} %bitcast.28, f32[80,1,128]{2,1,0:T(1,128)} %bitcast.31, bf16[32,128,128]{2,1,0:T(8,128)(2,1)} %fusion.1.src_ref), custom_call_target="tpu_custom_call" | custom-call | flops 335544320 | bytes 3932160 | tf_op jit(solution)/shard_map/pallas_call | solution.py:122
  81.3 1.8 %pad_maximum_fusion.2 = bf16[8,256,128]{2,1,0:T(8,128)(2,1)} fusion(bf16[8,128,128]{2,1,0:T(8,128)(2,1)} %shard_map.113, bf16[8,128,128]{2,1,0:T(8,128)(2,1)S(1)} %broadcast_in_dim.12), kind=kLoop, calls=%fused_computation.9 | loop fusion | flops 1048576 | bytes 1048576 | tf_op jit(solution)/shard_map/concatenate | solution.py:198
  83.1 3.5 %all-to-all-start.2 = ((bf16[8,256,128]{2,1,0:T(8,128)(2,1)}), bf16[8,256,128]{2,1,0:T(8,128)(2,1)S(1)}, u32[]{:S(2)}, u32[]{:S(2)}) async-start(bf16[8,256,128]{2,1,0:T(8,128)(2,1)} %pad_maximum_fusion.2), calls=%async_computation.2 | async-start | bytes 1048576 | tf_op jit(solution)/shard_map/all_to_all | solution.py:138
  86.6 0.0 copy-done.5
  86.6 0.1 copy.39
  86.7 15.8 %all-to-all-done.2 = bf16[8,256,128]{2,1,0:T(8,128)(2,1)S(1)} async-done(((bf16[8,256,128]{2,1,0:T(8,128)(2,1)}), bf16[8,256,128]{2,1,0:T(8,128)(2,1)S(1)}, u32[]{:S(2)}, u32[]{:S(2)}) %all-to-all-start.2) | async-done | bytes 524320 | tf_op jit(solution)/shard_map/all_to_all | solution.py:138
  102.5 0.4 fusion
  102.9 0.4 fusion.8
  103.3 0.2 fusion.13
  103.5 0.7 slice.47.src_ref
  104.2 3.3 %shard_map.114 = bf16[32,128,128]{2,1,0:T(8,128)(2,1)} custom-call(s32[1]{0:T(128)} %bitcast.26.live_ref, s32[80]{0:T(128)} %bitcast.38, s32[80]{0:T(128)} %bitcast.41, bf16[80,128,128]{2,1,0:T(8,128)(2,1)} %bitcast.29, f32[80,1,128]{2,1,0:T(1,128)} %bitcast.32, bf16[8,128,128]{2,1,0:T(8,128)(2,1)} %slice.47.src_ref), custom_call_target="tpu_custom_call" | custom-call | flops 335544320 | bytes 3932160 | tf_op jit(solution)/shard_map/pallas_call | solution.py:107
  107.5 0.1 fusion.2
  107.6 1.3 pad_maximum_fusion.1
  108.9 29.0 %all_to_all.30 = bf16[32,160,128]{2,1,0:T(8,128)(2,1)S(1)} all-to-all(bf16[32,160,128]{2,1,0:T(8,128)(2,1)S(1)} %pad_maximum_fusion.1), channel_id=1, replica_groups=mesh['row'=8,'col'=32] {'col'}, dimensions={0} | all-to-all | bytes 2621440 | tf_op jit(solution)/shard_map/all_to_all | solution.py:138
  137.9 0.3 convert_element_type.88
  138.2 0.0 copy-start.7
  138.3 9.5 %all_to_all.31 = bf16[8,32,128]{2,1,0:T(8,128)(2,1)S(1)} all-to-all(bf16[8,32,128]{2,1,0:T(8,128)(2,1)S(1)} %broadcast_in_dim.13), channel_id=1, replica_groups=mesh['row'=8,'col'=32] {'row'}, dimensions={0} | all-to-all | bytes 131072 | tf_op jit(solution)/shard_map/all_to_all | solution.py:134
  147.8 0.7 broadcast_in_dim.14
  148.6 5.0 %all-to-all-start.5 = ((bf16[32,32,128]{2,1,0:T(8,128)(2,1)}), bf16[32,32,128]{2,1,0:T(8,128)(2,1)S(1)}, u32[]{:S(2)}, u32[]{:S(2)}) async-start(bf16[32,32,128]{2,1,0:T(8,128)(2,1)} %broadcast_in_dim.14), calls=%async_computation.5 | async-start | bytes 524288 | tf_op jit(solution)/shard_map/all_to_all | solution.py:134
  153.6 0.1 slice_reduce_fusion
  153.7 0.0 copy-done.7
  153.7 0.7 add_convert_fusion
  154.4 8.2 %all-to-all-done.5 = bf16[32,32,128]{2,1,0:T(8,128)(2,1)S(1)} async-done(((bf16[32,32,128]{2,1,0:T(8,128)(2,1)}), bf16[32,32,128]{2,1,0:T(8,128)(2,1)S(1)}, u32[]{:S(2)}, u32[]{:S(2)}) %all-to-all-start.5) | async-done | bytes 262176 | tf_op jit(solution)/shard_map/all_to_all | solution.py:134
  162.5 0.8 fusion.10
  163.3 0.7 reshape.53
  (11 shorter events, 0.2 us)
Async XLA Ops:
  0.6 77.2 %copy-start = (bf16[512,128]{1,0:T(8,128)(2,1)S(1)}, bf16[512,128]{1,0:T(8,128)(2,1)}, u32[]{:S(2)}) copy-start(bf16[512,128]{1,0:T(8,128)(2,1)} %param.11) | copy-start | bytes 393220
  0.6 26.3 %copy-start.4 = (bf16[128,128]{1,0:T(8,128)(2,1)S(1)}, bf16[128,128]{1,0:T(8,128)(2,1)}, u32[]{:S(2)}) copy-start(bf16[128,128]{1,0:T(8,128)(2,1)} %param.17) | copy-start | bytes 98308
  2.2 19.5 %all-to-all-start = ((bf16[8,128,128]{2,1,0:T(8,128)(2,1)}), bf16[8,128,128]{2,1,0:T(8,128)(2,1)S(1)}, u32[]{:S(2)}, u32[]{:S(2)}) async-start(bf16[8,128,128]{2,1,0:T(8,128)(2,1)} %broadcast_in_dim.10), calls=%async_computation | async-start | bytes 524288 | tf_op jit(solution)/shard_map/all_to_all | solution.py:134
  21.7 0.7 copy-start.1
  30.0 43.3 %all-to-all-start.1 = ((bf16[32,288,128]{2,1,0:T(8,128)(2,1)}), bf16[32,288,128]{2,1,0:T(8,128)(2,1)S(1)}, u32[]{:S(2)}, u32[]{:S(2)}) async-start(bf16[32,288,128]{2,1,0:T(8,128)(2,1)} %pad_maximum_fusion), calls=%async_computation.1 | async-start | bytes 4718592 | tf_op jit(solution)/shard_map/all_to_all | solution.py:138
  76.1 1.5 copy-start.3
  76.1 1.6 copy-start.2
  76.2 1.9 %copy-start.6 = (f32[128]{0:T(128)}, f32[128]{0:T(128)S(1)}, u32[]{:S(2)}) copy-start(f32[128]{0:T(128)S(1)} %dynamic-slice_bitcast_fusion) | copy-start | bytes 1540
  78.1 8.5 %copy-start.5 = (bf16[128,128]{1,0:T(8,128)(2,1)S(1)}, bf16[128,128]{1,0:T(8,128)(2,1)}, u32[]{:S(2)}) copy-start(bf16[128,128]{1,0:T(8,128)(2,1)} %param.17) | copy-start | bytes 98308
  83.1 19.4 %all-to-all-start.2 = ((bf16[8,256,128]{2,1,0:T(8,128)(2,1)}), bf16[8,256,128]{2,1,0:T(8,128)(2,1)S(1)}, u32[]{:S(2)}, u32[]{:S(2)}) async-start(bf16[8,256,128]{2,1,0:T(8,128)(2,1)} %pad_maximum_fusion.2), calls=%async_computation.2 | async-start | bytes 1048576 | tf_op jit(solution)/shard_map/all_to_all | solution.py:138
  138.2 15.5 %copy-start.7 = (f32[128]{0:T(128)S(1)}, f32[128]{0:T(128)}, u32[]{:S(2)}) copy-start(f32[128]{0:T(128)} %copy-done.6) | copy-start | bytes 1540
  148.6 14.0 %all-to-all-start.5 = ((bf16[32,32,128]{2,1,0:T(8,128)(2,1)}), bf16[32,32,128]{2,1,0:T(8,128)(2,1)S(1)}, u32[]{:S(2)}, u32[]{:S(2)}) async-start(bf16[32,32,128]{2,1,0:T(8,128)(2,1)} %broadcast_in_dim.14), calls=%async_computation.5 | async-start | bytes 524288 | tf_op jit(solution)/shard_map/all_to_all | solution.py:134

commit v5 on v4

--- a/solution.py
+++ b/solution.py
@@ -37,18 +37,13 @@
     return (tiles_ref[s].astype(jnp.float32) * (mask_ref[s] * keep)).astype(jnp.bfloat16)
 
 
-def _forward_kernel(with_degree, live_ref, rows_ref, cols_ref, tiles_ref, mask_ref, src_ref, *rest):
-    if with_degree:
-        out_ref, deg_ref, acc_ref, dacc_ref = rest
-    else:
-        out_ref, acc_ref = rest
+def _forward_kernel(row_offset, live_ref, rows_ref, cols_ref, tiles_ref, mask_ref, src_ref, into_ref, out_ref,
+                    acc_ref, stage_ref, sem):
+    del into_ref
     slots = tiles_ref.shape[0]
     n_dst = acc_ref.shape[0]
     n_src = src_ref.shape[0]
     acc_ref[...] = jnp.zeros_like(acc_ref)
-    if with_degree:
-        dacc_ref[...] = jnp.zeros_like(dacc_ref)
-    ones = jnp.ones((8, BLOCK), jnp.bfloat16)
     n_live = jnp.clip(live_ref[0], 0, slots)
 
     def body(k, carry):
@@ -58,19 +53,18 @@
             c = jnp.clip(cols_ref[s], 0, n_src - 1)
             tile = _masked_tile(tiles_ref, mask_ref, s, keep)
             acc_ref[r] += jnp.dot(tile, src_ref[c], preferred_element_type=jnp.float32)
-            if with_degree:
-                dacc_ref[r] += lax.dot_general(
-                    ones, tile, (((1,), (1,)), ((), ())), preferred_element_type=jnp.float32
-                )
         return carry
 
     lax.fori_loop(0, (n_live + UNROLL - 1) // UNROLL, body, 0)
-    out_ref[...] = acc_ref[...].astype(out_ref.dtype)
-    if with_degree:
-        deg_ref[...] = dacc_ref[...]
-
-
-def _transpose_kernel(live_ref, rows_ref, cols_ref, tiles_ref, mask_ref, src_ref, out_ref, acc_ref):
+    stage_ref[...] = acc_ref[...].astype(stage_ref.dtype)
+    copy = pltpu.make_async_copy(stage_ref, out_ref.at[:, pl.ds(row_offset, BLOCK), :], sem)
+    copy.start()
+    copy.wait()
+
+
+def _transpose_kernel(row_offset, live_ref, rows_ref, cols_ref, tiles_ref, mask_ref, src_ref, into_ref, out_ref,
+                      acc_ref, stage_ref, sem):
+    del into_ref
     slots = tiles_ref.shape[0]
     n_dst = acc_ref.shape[0]
     n_src = src_ref.shape[0]
@@ -87,46 +81,44 @@
         return carry
 
     lax.fori_loop(0, (n_live + UNROLL - 1) // UNROLL, body, 0)
-    out_ref[...] = acc_ref[...].astype(out_ref.dtype)
+    stage_ref[...] = acc_ref[...].astype(stage_ref.dtype)
+    copy = pltpu.make_async_copy(stage_ref, out_ref.at[:, pl.ds(row_offset, BLOCK), :], sem)
+    copy.start()
+    copy.wait()
 
 
 _SMEM = pl.BlockSpec(memory_space=pltpu.SMEM)
 _VMEM = pl.BlockSpec(memory_space=pltpu.VMEM)
-
-
-def forward_aggregate(live, rows, cols, tiles, mask, src, n_dst, with_degree):
-    width = src.shape[-1]
+_ANY = pl.BlockSpec(memory_space=pl.ANY)
+
+
+def _aggregate_into(kernel, live, rows, cols, tiles, mask, src, into, row_offset):
+    n_dst = into.shape[0]
+    width = into.shape[2]
     slots = tiles.shape[0]
-    out_shape = [jax.ShapeDtypeStruct((n_dst, BLOCK, width), jnp.bfloat16)]
-    scratch = [pltpu.VMEM((n_dst, BLOCK, width), jnp.float32)]
-    if with_degree:
-        out_shape.append(jax.ShapeDtypeStruct((n_dst, 8, BLOCK), jnp.float32))
-        scratch.append(pltpu.VMEM((n_dst, 8, BLOCK), jnp.float32))
-    flops = 2 * slots * BLOCK * BLOCK * (width + (8 if with_degree else 0))
+    flops = 2 * slots * BLOCK * BLOCK * width
     bytes_accessed = tiles.size * 2 + src.size * 2 + n_dst * BLOCK * width * 2
     return pl.pallas_call(
-        functools.partial(_forward_kernel, with_degree),
-        out_shape=tuple(out_shape),
-        in_specs=[_SMEM, _SMEM, _SMEM, _VMEM, _VMEM, _VMEM],
-        out_specs=tuple([_VMEM] * len(out_shape)),
-        scratch_shapes=scratch,
+        functools.partial(kernel, row_offset),
+        out_shape=jax.ShapeDtypeStruct(into.shape, into.dtype),
+        in_specs=[_SMEM, _SMEM, _SMEM, _VMEM, _VMEM, _VMEM, _ANY],
+        out_specs=_ANY,
+        scratch_shapes=[
+            pltpu.VMEM((n_dst, BLOCK, width), jnp.float32),
+            pltpu.VMEM((n_dst, BLOCK, width), into.dtype),
+            pltpu.SemaphoreType.DMA(()),
+        ],
+        input_output_aliases={6: 0},
         cost_estimate=pl.CostEstimate(flops=flops, bytes_accessed=bytes_accessed, transcendentals=0),
-    )(live, rows, cols, tiles, mask, src)
-
-
-def transpose_aggregate(live, rows, cols, tiles, mask, src_t, n_dst):
-    width = src_t.shape[1]
-    slots = tiles.shape[0]
-    flops = 2 * slots * BLOCK * BLOCK * width
-    bytes_accessed = tiles.size * 2 + src_t.size * 2 + n_dst * BLOCK * width * 2
-    return pl.pallas_call(
-        _transpose_kernel,
-        out_shape=jax.ShapeDtypeStruct((n_dst, width, BLOCK), jnp.bfloat16),
-        in_specs=[_SMEM, _SMEM, _SMEM, _VMEM, _VMEM, _VMEM],
-        out_specs=_VMEM,
-        scratch_shapes=[pltpu.VMEM((n_dst, width, BLOCK), jnp.float32)],
-        cost_estimate=pl.CostEstimate(flops=flops, bytes_accessed=bytes_accessed, transcendentals=0),
-    )(live, rows, cols, tiles, mask, src_t)
+    )(live, rows, cols, tiles, mask, src, into)
+
+
+def forward_aggregate_into(live, rows, cols, tiles, mask, src, into, row_offset):
+    return _aggregate_into(_forward_kernel, live, rows, cols, tiles, mask, src, into, row_offset)
+
+
+def transpose_aggregate_into(live, rows, cols, tiles, mask, src_t, into, row_offset):
+    return _aggregate_into(_transpose_kernel, live, rows, cols, tiles, mask, src_t, into, row_offset)
 
 
 def gather_blocks(block, axis):
@@ -170,13 +162,15 @@
     mask = column_mask[0, 0].astype(f32)[:, None, :]
 
     x_panel = gather_blocks(features, "row")
-    partial_in, partial_deg = forward_aggregate(
-        live, rows, cols, tiles, mask, x_panel, row_groups, with_degree=True
-    )
-    shared = jnp.concatenate([partial_deg[:, 0, :].astype(bf16), cotangent], axis=0)
+    live_weight = (jnp.arange(tiles.shape[0]) < jnp.clip(live[0], 0, tiles.shape[0])).astype(f32)
+    row_sums = jnp.sum(tiles.astype(f32) * mask, axis=2) * live_weight[:, None]
+    partial_deg = jnp.zeros((row_groups, BLOCK), f32).at[jnp.clip(rows, 0, row_groups - 1)].add(row_sums)
+    shared = jnp.concatenate([partial_deg.astype(bf16), cotangent], axis=0)
     packed = jnp.concatenate(
-        [partial_in, jnp.broadcast_to(shared[None], (row_groups,) + shared.shape)], axis=1
-    )
+        [jnp.zeros((row_groups, BLOCK, BLOCK), bf16), jnp.broadcast_to(shared[None], (row_groups,) + shared.shape)],
+        axis=1,
+    )
+    packed = forward_aggregate_into(live, rows, cols, tiles, mask, x_panel, packed, 0)
     arrived = scatter_blocks(packed, "col")
     summed_in = jnp.sum(arrived[:, :BLOCK].astype(f32), axis=0)
     degrees = jnp.sum(arrived[:, BLOCK : BLOCK + row_groups].astype(f32), axis=0)
@@ -193,16 +187,18 @@
     grad_panel_t = jnp.swapaxes(
         (group_scale[:, :, None] * group_cot.astype(f32)).astype(bf16), 1, 2
     )
-    partial_back_t = transpose_aggregate(live, rows, cols, tiles, mask, grad_panel_t, col_groups)
 
     packed = jnp.concatenate(
-        [jnp.broadcast_to(projected.astype(bf16)[None], (col_groups, BLOCK, BLOCK)), partial_back_t],
+        [
+            jnp.broadcast_to(projected.astype(bf16)[None], (col_groups, BLOCK, BLOCK)),
+            jnp.zeros((col_groups, BLOCK, BLOCK), bf16),
+        ],
         axis=1,
     )
+    packed = transpose_aggregate_into(live, rows, cols, tiles, mask, grad_panel_t, packed, BLOCK)
     arrived = scatter_blocks(packed, "row")
     y_panel = arrived[:, :BLOCK]
     returned_t = jnp.sum(arrived[:, BLOCK:].astype(f32), axis=0)
-    (partial_y,) = forward_aggregate(live, rows, cols, tiles, mask, y_panel, row_groups, with_degree=False)
 
     hp = lax.Precision.HIGHEST
     combined = cotangent.astype(f32) + returned_t.T
@@ -214,7 +210,8 @@
     flat = jnp.concatenate([first_term.reshape(-1), second_term.reshape(-1)]) * node_scale
     slices = flat.reshape(row_groups, -1, BLOCK)
 
-    packed = jnp.concatenate([partial_y, slices.astype(bf16)], axis=1)
+    packed = jnp.concatenate([jnp.zeros((row_groups, BLOCK, BLOCK), bf16), slices.astype(bf16)], axis=1)
+    packed = forward_aggregate_into(live, rows, cols, tiles, mask, y_panel, packed, 0)
     arrived = scatter_blocks(packed, "col").astype(f32)
     summed_y = jnp.sum(arrived[:, :BLOCK], axis=0)
     output = (projected + row_scale * summed_y).astype(bf16)

time: 165 us -> 158 us (0.958)
  waiting for transfers between devices: 63.9 us -> 57.4 us
    all_to_all x2, waiting for transfers between devices: 16.6 us -> 10 us  [gather_blocks(): lax.all_to_all(jnp.broadcast_to(block[None], (n,) + block.shape), axis, 0...]
    concatenate x4 -> x1, other arithmetic: 5.91 us -> 0.01 us  [local(): shared = jnp.concatenate([partial_deg.astype(bf16), cotangent], axis=0)]
    concatenate x0 -> x3, local copies, waits for them, and re-layouts: none -> 3.73 us  [the longest x1 1.63 us: local(): jnp.concatenate([jnp.zeros((row_groups, BLOCK, BLOCK), bf16), jnp.broadca...]
    reduce_sum x0 -> x1, other arithmetic: none -> 3.16 us  [local(): row_sums = jnp.sum(tiles.astype(f32) * mask, axis=2) * live_weight[:, None]]
  transfers between devices with their start and end apart: 4 -> 4, of which waited for: 4 -> 4; matrix products, arithmetic and copies ran while one was open for 1% -> 6% of each run, Pallas kernels for 0% -> 0%
where the time goes in v5:
time: 158 us; the launch traced here: 157 us
  waiting for transfers between devices  57.4 us (36%)
  blocking collectives  38.7 us (24%)
  starting transfers between devices  28.7 us (18%)
  local copies, waits for them, and re-layouts  10.2 us (6%)
  Pallas kernels  9.98 us (6%)
  other arithmetic  8.99 us (6%)
  matrix products  1.99 us (1%)
  between operations  1.64 us (1%)
    all_to_all x2, waiting for transfers between devices, scatter_blocks(): return lax.all_to_all(blocks, axis, 0, 0, tiled=False)  47.4 us
    all_to_all x1, blocking collectives, scatter_blocks(): return lax.all_to_all(blocks, axis, 0, 0, tiled=False)  29.2 us
    all_to_all x2, starting transfers between devices, scatter_blocks(): return lax.all_to_all(blocks, axis, 0, 0, tiled=False)  14.7 us
    all_to_all x2, starting transfers between devices, gather_blocks(): lax.all_to_all(jnp.broadcast_to(block[None], (n,) + block.shape), axis, 0...  14 us
    all_to_all x2, waiting for transfers between devices, gather_blocks(): lax.all_to_all(jnp.broadcast_to(block[None], (n,) + block.shape), axis, 0...  10 us
    pallas_call x3, Pallas kernels, _aggregate_into(): pl.pallas_call(functools.partial(kernel, row_offset), out_shape=jax.Shape...  9.98 us
    all_to_all x1, blocking collectives, gather_blocks(): lax.all_to_all(jnp.broadcast_to(block[None], (n,) + block.shape), axis, 0...  9.53 us
    reduce_sum x1, other arithmetic, local(): row_sums = jnp.sum(tiles.astype(f32) * mask, axis=2) * live_weight[:, None]  3.16 us
  transfers between devices with their start and end apart: 4, of which 4 were waited for; matrix products, arithmetic and copies ran while one was open for 6% of the time, Pallas kernels for 0%

profile of v5, /device:TPU:1, one launch (start us, length us, event | category | flops | bytes accessed | tf_op | source)
XLA Modules:
  0.0 157.5 jit_solution(16810038137194333064)
XLA Ops:
  0.6 0.0 copy-start
  0.6 0.0 copy-start.8
  0.7 1.5 broadcast_in_dim.12
  2.2 9.0 %all-to-all-start = ((bf16[8,128,128]{2,1,0:T(8,128)(2,1)}), bf16[8,128,128]{2,1,0:T(8,128)(2,1)S(1)}, u32[]{:S(2)}, u32[]{:S(2)}) async-start(bf16[8,128,128]{2,1,0:T(8,128)(2,1)} %broadcast_in_dim.12), calls=%async_computation | async-start | bytes 524288 | tf_op jit(solution)/shard_map/all_to_all | solution.py:126
  11.8 1.4 convert_bitcast_fusion
  13.2 0.7 fusion.13
  13.9 3.2 %multiply_reduce_fusion = f32[80,128]{1,0:T(8,128)S(1)} fusion(f32[80,128]{1,0:T(8,128)S(1)} %get-tuple-element.5, bf16[1,1,80,128,128]{4,3,2,1,0:T(8,128)(2,1)} %param.16), kind=kLoop, calls=%fused_computation.1 | loop fusion | flops 3921920 | bytes 2703360 | tf_op jit(solution)/shard_map/reduce_sum | solution.py:166
  17.1 0.9 scatter_custom_fusion
  18.0 0.0 copy-done.8
  18.0 0.2 broadcast_in_dim.14
  18.2 1.6 %concatenate.21.into_ref = bf16[32,288,128]{2,1,0:T(8,128)(2,1)} pad(bf16[32,160,128]{2,1,0:T(8,128)(2,1)S(1)} %broadcast_in_dim.14, bf16[]{:T(256)} %constant.6.clone.1), padding=0_0x128_0x0_0 | pad | bytes 3670018 | tf_op jit(solution)/shard_map/concatenate | solution.py:169
  19.8 1.9 %all-to-all-done.src_ref = bf16[8,128,128]{2,1,0:T(8,128)(2,1)S(1)} async-done(((bf16[8,128,128]{2,1,0:T(8,128)(2,1)}), bf16[8,128,128]{2,1,0:T(8,128)(2,1)S(1)}, u32[]{:S(2)}, u32[]{:S(2)}) %all-to-all-start) | async-done | bytes 262176 | tf_op jit(solution)/shard_map/all_to_all | solution.py:126
  21.7 0.7 copy-done.1
  22.4 3.4 %shard_map.112 = bf16[32,288,128]{2,1,0:T(8,128)(2,1)} custom-call(s32[1]{0:T(128)} %bitcast.29.live_ref, s32[80]{0:T(128)} %bitcast.40, s32[80]{0:T(128)} %bitcast.43, bf16[80,128,128]{2,1,0:T(8,128)(2,1)} %bitcast.32, f32[80,1,128]{2,1,0:T(1,128)} %bitcast.35, bf16[8,128,128]{2,1,0:T(8,128)(2,1)} %copy-done.1, ...), custom_call_target="tpu_custom_call", output_to_operand_aliasing={{}: (6, {})} | custom-call | flops 335544320 | bytes 3932160 | tf_op jit(solution)/shard_map/pallas_call | solution.py:101
  25.8 0.0 copy-start.7
  25.8 0.0 copy-start.6
  25.8 10.6 %all-to-all-start.1 = ((bf16[32,288,128]{2,1,0:T(8,128)(2,1)}), bf16[32,288,128]{2,1,0:T(8,128)(2,1)S(1)}, u32[]{:S(2)}, u32[]{:S(2)}) async-start(bf16[32,288,128]{2,1,0:T(8,128)(2,1)} %shard_map.112), calls=%async_computation.1 | async-start | bytes 4718592 | tf_op jit(solution)/shard_map/all_to_all | solution.py:130
  36.4 31.5 %all-to-all-done.1 = bf16[32,288,128]{2,1,0:T(8,128)(2,1)S(1)} async-done(((bf16[32,288,128]{2,1,0:T(8,128)(2,1)}), bf16[32,288,128]{2,1,0:T(8,128)(2,1)S(1)}, u32[]{:S(2)}, u32[]{:S(2)}) %all-to-all-start.1) | async-done | bytes 2359328 | tf_op jit(solution)/shard_map/all_to_all | solution.py:130
  68.0 0.0 copy-start.11
  68.0 0.2 convert_reduce_fusion
  68.2 0.0 copy-done.7
  68.2 0.1 add_convert_fusion.1
  68.3 0.0 copy-done.6
  68.3 0.0 copy-start.2
  68.3 0.2 fusion.17
  68.5 0.0 copy-done
  68.5 0.0 copy-start.4
  68.5 0.8 fusion.16
  69.3 0.0 copy-done.2
  69.4 0.0 copy-done.4
  69.4 0.0 copy-done.11
  69.4 0.9 concatenate.22.into_ref
  70.3 0.1 slice.40
  70.4 0.7 copy.43
  71.1 1.3 fusion.1.src_ref
  72.4 3.2 %shard_map.113 = bf16[8,256,128]{2,1,0:T(8,128)(2,1)} custom-call(s32[1]{0:T(128)} %bitcast.30.live_ref, s32[80]{0:T(128)} %bitcast.41, s32[80]{0:T(128)} %bitcast.44, bf16[80,128,128]{2,1,0:T(8,128)(2,1)} %bitcast.33, f32[80,1,128]{2,1,0:T(1,128)} %bitcast.36, bf16[32,128,128]{2,1,0:T(8,128)(2,1)} %fusion.1.src_ref, ...), custom_call_target="tpu_custom_call", output_to_operand_aliasing={{}: (6, {})} | custom-call | flops 335544320 | bytes 3932160 | tf_op jit(solution)/shard_map/pallas_call | solution.py:101
  75.6 0.0 copy-start.3
  75.6 4.0 %all-to-all-start.2 = ((bf16[8,256,128]{2,1,0:T(8,128)(2,1)}), bf16[8,256,128]{2,1,0:T(8,128)(2,1)S(1)}, u32[]{:S(2)}, u32[]{:S(2)}) async-start(bf16[8,256,128]{2,1,0:T(8,128)(2,1)} %shard_map.113), calls=%async_computation.2 | async-start | bytes 1048576 | tf_op jit(solution)/shard_map/all_to_all | solution.py:130
  79.7 0.0 copy-done.9
  79.7 0.1 copy.40
  79.8 15.9 %all-to-all-done.2 = bf16[8,256,128]{2,1,0:T(8,128)(2,1)S(1)} async-done(((bf16[8,256,128]{2,1,0:T(8,128)(2,1)}), bf16[8,256,128]{2,1,0:T(8,128)(2,1)S(1)}, u32[]{:S(2)}, u32[]{:S(2)}) %all-to-all-start.2) | async-done | bytes 524320 | tf_op jit(solution)/shard_map/all_to_all | solution.py:130
  95.7 0.0 copy-done.5
  95.7 0.4 fusion
  96.1 0.4 fusion.8
  96.5 0.0 copy-done.3
  96.5 0.2 fusion.18
  96.7 0.1 fusion.2
  96.8 1.2 concatenate.26.into_ref
  98.0 0.7 slice.41.src_ref
  98.7 3.4 %shard_map.114 = bf16[32,160,128]{2,1,0:T(8,128)(2,1)} custom-call(s32[1]{0:T(128)} %bitcast.31.live_ref, s32[80]{0:T(128)} %bitcast.42, s32[80]{0:T(128)} %bitcast.45, bf16[80,128,128]{2,1,0:T(8,128)(2,1)} %bitcast.34, f32[80,1,128]{2,1,0:T(1,128)} %bitcast.37, bf16[8,128,128]{2,1,0:T(8,128)(2,1)} %slice.41.src_ref, ...), custom_call_target="tpu_custom_call", output_to_operand_aliasing={{}: (6, {})} | custom-call | flops 335544320 | bytes 3932160 | tf_op jit(solution)/shard_map/pallas_call | solution.py:101
  102.1 29.2 %all_to_all.30 = bf16[32,160,128]{2,1,0:T(8,128)(2,1)S(1)} all-to-all(bf16[32,160,128]{2,1,0:T(8,128)(2,1)} %shard_map.114), channel_id=1, replica_groups=mesh['row'=8,'col'=32] {'col'}, dimensions={0} | all-to-all | bytes 2621440 | tf_op jit(solution)/shard_map/all_to_all | solution.py:130
  131.3 0.3 convert_element_type.104
  131.6 0.0 copy-start.10
  131.6 0.0 copy-start.12
  131.7 9.5 %all_to_all.31 = bf16[8,32,128]{2,1,0:T(8,128)(2,1)S(1)} all-to-all(bf16[8,32,128]{2,1,0:T(8,128)(2,1)S(1)} %broadcast_in_dim.16), channel_id=1, replica_groups=mesh['row'=8,'col'=32] {'row'}, dimensions={0} | all-to-all | bytes 131072 | tf_op jit(solution)/shard_map/all_to_all | solution.py:126
  141.3 0.7 broadcast_in_dim.17
  142.0 5.0 %all-to-all-start.5 = ((bf16[32,32,128]{2,1,0:T(8,128)(2,1)}), bf16[32,32,128]{2,1,0:T(8,128)(2,1)S(1)}, u32[]{:S(2)}, u32[]{:S(2)}) async-start(bf16[32,32,128]{2,1,0:T(8,128)(2,1)} %broadcast_in_dim.17), calls=%async_computation.5 | async-start | bytes 524288 | tf_op jit(solution)/shard_map/all_to_all | solution.py:126
  147.0 0.1 slice_reduce_fusion
  147.1 0.0 copy-done.10
  147.1 0.0 copy-done.12
  147.1 0.7 add_convert_fusion
  147.8 8.1 %all-to-all-done.5 = bf16[32,32,128]{2,1,0:T(8,128)(2,1)S(1)} async-done(((bf16[32,32,128]{2,1,0:T(8,128)(2,1)}), bf16[32,32,128]{2,1,0:T(8,128)(2,1)S(1)}, u32[]{:S(2)}, u32[]{:S(2)}) %all-to-all-start.5) | async-done | bytes 262176 | tf_op jit(solution)/shard_map/all_to_all | solution.py:126
  156.0 0.8 fusion.15
  156.7 0.7 reshape.85
  (15 shorter events, 0.3 us)
Async XLA Ops:
  0.6 67.9 %copy-start = (bf16[512,128]{1,0:T(8,128)(2,1)S(1)}, bf16[512,128]{1,0:T(8,128)(2,1)}, u32[]{:S(2)}) copy-start(bf16[512,128]{1,0:T(8,128)(2,1)} %param.11) | copy-start | bytes 393220
  0.6 17.4 %copy-start.8 = (bf16[128,128]{1,0:T(8,128)(2,1)S(1)}, bf16[128,128]{1,0:T(8,128)(2,1)}, u32[]{:S(2)}) copy-start(bf16[128,128]{1,0:T(8,128)(2,1)} %param.17) | copy-start | bytes 98308
  2.2 19.5 %all-to-all-start = ((bf16[8,128,128]{2,1,0:T(8,128)(2,1)}), bf16[8,128,128]{2,1,0:T(8,128)(2,1)S(1)}, u32[]{:S(2)}, u32[]{:S(2)}) async-start(bf16[8,128,128]{2,1,0:T(8,128)(2,1)} %broadcast_in_dim.12), calls=%async_computation | async-start | bytes 524288 | tf_op jit(solution)/shard_map/all_to_all | solution.py:126
  21.7 0.7 copy-start.1
  25.8 42.4 %copy-start.7 = (bf16[128,128]{1,0:T(8,128)(2,1)S(1)}, bf16[128,128]{1,0:T(8,128)(2,1)}, u32[]{:S(2)}) copy-start(bf16[128,128]{1,0:T(8,128)(2,1)} %param.9) | copy-start | bytes 98308
  25.8 42.5 %copy-start.6 = (bf16[128,512]{1,0:T(8,128)(2,1)S(1)}, bf16[128,512]{1,0:T(8,128)(2,1)}, u32[]{:S(2)}) copy-start(bf16[128,512]{1,0:T(8,128)(2,1)} %param.10) | copy-start | bytes 393220
  25.8 42.2 %all-to-all-start.1 = ((bf16[32,288,128]{2,1,0:T(8,128)(2,1)}), bf16[32,288,128]{2,1,0:T(8,128)(2,1)S(1)}, u32[]{:S(2)}, u32[]{:S(2)}) async-start(bf16[32,288,128]{2,1,0:T(8,128)(2,1)} %shard_map.112), calls=%async_computation.1 | async-start | bytes 4718592 | tf_op jit(solution)/shard_map/all_to_all | solution.py:130
  68.0 1.4 copy-start.11
  68.3 1.1 copy-start.2
  68.5 0.9 copy-start.4
  72.4 7.3 %copy-start.9 = (bf16[128,128]{1,0:T(8,128)(2,1)S(1)}, bf16[128,128]{1,0:T(8,128)(2,1)}, u32[]{:S(2)}) copy-start(bf16[128,128]{1,0:T(8,128)(2,1)} %param.17) | copy-start | bytes 98308
  72.4 23.3 %copy-start.5 = (f32[128,512]{1,0:T(8,128)S(1)}, f32[128,512]{1,0:T(8,128)}, u32[]{:S(2)}) copy-start(f32[128,512]{1,0:T(8,128)} %copy-done.4) | copy-start | bytes 786436
  75.6 20.9 %copy-start.3 = (bf16[128,128]{1,0:T(8,128)(2,1)S(1)}, bf16[128,128]{1,0:T(8,128)(2,1)}, u32[]{:S(2)}) copy-start(bf16[128,128]{1,0:T(8,128)(2,1)} %copy-done.2) | copy-start | bytes 98308
  75.6 20.0 %all-to-all-start.2 = ((bf16[8,256,128]{2,1,0:T(8,128)(2,1)}), bf16[8,256,128]{2,1,0:T(8,128)(2,1)S(1)}, u32[]{:S(2)}, u32[]{:S(2)}) async-start(bf16[8,256,128]{2,1,0:T(8,128)(2,1)} %shard_map.113), calls=%async_computation.2 | async-start | bytes 1048576 | tf_op jit(solution)/shard_map/all_to_all | solution.py:130
  131.6 15.5 %copy-start.10 = (f32[128,128]{1,0:T(8,128)S(1)}, f32[128,128]{1,0:T(8,128)}, u32[]{:S(2)}) copy-start(f32[128,128]{1,0:T(8,128)} %get-tuple-element.8) | copy-start | bytes 196612
  131.6 15.5 %copy-start.12 = (f32[128]{0:T(128)S(1)}, f32[128]{0:T(128)}, u32[]{:S(2)}) copy-start(f32[128]{0:T(128)} %copy-done.11) | copy-start | bytes 1540
  142.0 14.0 %all-to-all-start.5 = ((bf16[32,32,128]{2,1,0:T(8,128)(2,1)}), bf16[32,32,128]{2,1,0:T(8,128)(2,1)S(1)}, u32[]{:S(2)}, u32[]{:S(2)}) async-start(bf16[32,32,128]{2,1,0:T(8,128)(2,1)} %broadcast_in_dim.17), calls=%async_computation.5 | async-start | bytes 524288 | tf_op jit(solution)/shard_map/all_to_all | solution.py:126

commit v6 on v5

--- a/solution.py
+++ b/solution.py
@@ -34,7 +34,8 @@
 
 
 def _masked_tile(tiles_ref, mask_ref, s, keep):
-    return (tiles_ref[s].astype(jnp.float32) * (mask_ref[s] * keep)).astype(jnp.bfloat16)
+    column = mask_ref[pl.ds(s, 1), :].astype(jnp.float32) * keep
+    return (tiles_ref[s].astype(jnp.float32) * column).astype(jnp.bfloat16)
 
 
 def _forward_kernel(row_offset, live_ref, rows_ref, cols_ref, tiles_ref, mask_ref, src_ref, into_ref, out_ref,
@@ -159,13 +160,14 @@
     rows = tile_rows[0, 0]
     cols = tile_cols[0, 0]
     tiles = edge_weight[0, 0]
-    mask = column_mask[0, 0].astype(f32)[:, None, :]
+    mask = column_mask[0, 0]
 
     x_panel = gather_blocks(features, "row")
-    live_weight = (jnp.arange(tiles.shape[0]) < jnp.clip(live[0], 0, tiles.shape[0])).astype(f32)
-    row_sums = jnp.sum(tiles.astype(f32) * mask, axis=2) * live_weight[:, None]
+    live_weight = (jnp.arange(tiles.shape[0]) < jnp.clip(live[0], 0, tiles.shape[0])).astype(jnp.int32)
+    live_mask = (mask * live_weight[:, None]).astype(bf16)
+    row_sums = jnp.einsum("sij,sj->si", tiles, live_mask, preferred_element_type=f32)
     partial_deg = jnp.zeros((row_groups, BLOCK), f32).at[jnp.clip(rows, 0, row_groups - 1)].add(row_sums)
-    shared = jnp.concatenate([partial_deg.astype(bf16), cotangent], axis=0)
+    shared = jnp.concatenate([partial_deg.astype(bf16), cotangent.T], axis=0)
     packed = jnp.concatenate(
         [jnp.zeros((row_groups, BLOCK, BLOCK), bf16), jnp.broadcast_to(shared[None], (row_groups,) + shared.shape)],
         axis=1,
@@ -174,7 +176,7 @@
     arrived = scatter_blocks(packed, "col")
     summed_in = jnp.sum(arrived[:, :BLOCK].astype(f32), axis=0)
     degrees = jnp.sum(arrived[:, BLOCK : BLOCK + row_groups].astype(f32), axis=0)
-    group_cot = arrived[:, BLOCK + row_groups :]
+    group_cot_t = arrived[:, BLOCK + row_groups :]
     group_scale = 1.0 / jnp.sqrt(1.0 + degrees)
     me = lax.axis_index("col")
     row_scale = lax.dynamic_index_in_dim(group_scale, me, axis=0, keepdims=False)[:, None]
@@ -184,10 +186,7 @@
     hidden = gelu_tanh(first_pre).astype(bf16)
     projected = jnp.dot(hidden, second_weight, preferred_element_type=f32)
 
-    grad_panel_t = jnp.swapaxes(
-        (group_scale[:, :, None] * group_cot.astype(f32)).astype(bf16), 1, 2
-    )
-
+    grad_panel_t = (group_scale[:, None, :] * group_cot_t.astype(f32)).astype(bf16)
     packed = jnp.concatenate(
         [
             jnp.broadcast_to(projected.astype(bf16)[None], (col_groups, BLOCK, BLOCK)),

time: 158 us -> 156 us (0.987)
  other arithmetic: 8.99 us -> 5.3 us
  matrix products: 1.99 us -> 4.51 us
    reduce_sum x2 -> x0, other arithmetic: 3.31 us -> none  [the longest x1 3.16 us: local(): row_sums = jnp.sum(tiles.astype(f32) * mask, axis=2) * live_weight[:, None]]
    dot_general x0 -> x1, matrix products: none -> 3.17 us  [local(): jnp.einsum('sij,sj->si', tiles, live_mask, preferred_element_type=f32)]
where the time goes in v6:
time: 156 us; the launch traced here: 155 us
  waiting for transfers between devices  57.6 us (37%)
  blocking collectives  38.4 us (25%)
  starting transfers between devices  27.7 us (18%)
  Pallas kernels  10.8 us (7%)
  local copies, waits for them, and re-layouts  9.54 us (6%)
  other arithmetic  5.3 us (3%)
  matrix products  4.51 us (3%)
    all_to_all x2, waiting for transfers between devices, scatter_blocks(): return lax.all_to_all(blocks, axis, 0, 0, tiled=False)  47.3 us
    all_to_all x1, blocking collectives, scatter_blocks(): return lax.all_to_all(blocks, axis, 0, 0, tiled=False)  28.9 us
    all_to_all x2, starting transfers between devices, gather_blocks(): lax.all_to_all(jnp.broadcast_to(block[None], (n,) + block.shape), axis, 0...  14 us
    all_to_all x2, starting transfers between devices, scatter_blocks(): return lax.all_to_all(blocks, axis, 0, 0, tiled=False)  13.7 us
    pallas_call x3, Pallas kernels, _aggregate_into(): pl.pallas_call(functools.partial(kernel, row_offset), out_shape=jax.Shape...  10.8 us
    all_to_all x2, waiting for transfers between devices, gather_blocks(): lax.all_to_all(jnp.broadcast_to(block[None], (n,) + block.shape), axis, 0...  10.3 us
    all_to_all x1, blocking collectives, gather_blocks(): lax.all_to_all(jnp.broadcast_to(block[None], (n,) + block.shape), axis, 0...  9.53 us
    dot_general x1, matrix products, local(): jnp.einsum('sij,sj->si', tiles, live_mask, preferred_element_type=f32)  3.17 us
  transfers between devices with their start and end apart: 4, of which 4 were waited for; matrix products, arithmetic and copies ran while one was open for 6% of the time, Pallas kernels for 0%

profile of v6, /device:TPU:1, one launch (start us, length us, event | category | flops | bytes accessed | tf_op | source)
XLA Modules:
  0.0 155.4 jit_solution(7448056225057647092)
XLA Ops:
  0.6 0.0 copy-start
  0.6 0.0 copy-start.4
  0.7 1.5 broadcast_in_dim.12
  2.2 9.0 %all-to-all-start = ((bf16[8,128,128]{2,1,0:T(8,128)(2,1)}), bf16[8,128,128]{2,1,0:T(8,128)(2,1)S(1)}, u32[]{:S(2)}, u32[]{:S(2)}) async-start(bf16[8,128,128]{2,1,0:T(8,128)(2,1)} %broadcast_in_dim.12), calls=%async_computation | async-start | bytes 524288 | tf_op jit(solution)/shard_map/all_to_all | solution.py:127
  11.9 0.9 fusion.10
  12.7 0.7 fusion.13
  13.4 3.2 %fusion.8 = f32[80,1,128]{2,1,0:T(1,128)S(1)} fusion(bf16[80,128,1]{1,0,2:T(8,128)(2,1)S(1)} %fusion.10, bf16[1,1,80,128,128]{4,3,2,1,0:T(8,128)(2,1)} %param.16), kind=kOutput, calls=%fused_computation.24 | convolution fusion | flops 2621440 | bytes 2682880 | tf_op jit(solution)/shard_map/sij,sj->si/dot_general | solution.py:168
  16.6 0.9 scatter_custom_fusion
  17.5 0.1 copy.21
  17.6 0.0 copy-done.4
  17.6 0.1 pad_maximum_fusion
  17.7 0.1 copy.22
  17.8 0.2 broadcast_in_dim.14
  18.0 1.6 %concatenate.21.into_ref = bf16[32,288,128]{2,1,0:T(8,128)(2,1)} pad(bf16[32,160,128]{2,1,0:T(8,128)(2,1)S(1)} %broadcast_in_dim.14, bf16[]{:T(256)} %constant.6.clone.1), padding=0_0x128_0x0_0 | pad | bytes 3670018 | tf_op jit(solution)/shard_map/concatenate | solution.py:171
  19.6 2.1 %all-to-all-done.src_ref = bf16[8,128,128]{2,1,0:T(8,128)(2,1)S(1)} async-done(((bf16[8,128,128]{2,1,0:T(8,128)(2,1)}), bf16[8,128,128]{2,1,0:T(8,128)(2,1)S(1)}, u32[]{:S(2)}, u32[]{:S(2)}) %all-to-all-start) | async-done | bytes 262176 | tf_op jit(solution)/shard_map/all_to_all | solution.py:127
  21.7 0.0 copy-start.1
  21.7 0.7 copy-done.1
  22.4 3.7 %shard_map.112 = bf16[32,288,128]{2,1,0:T(8,128)(2,1)} custom-call(s32[1]{0:T(128)} %bitcast.32.live_ref, s32[80]{0:T(128)} %bitcast.45, s32[80]{0:T(128)} %bitcast.48, bf16[80,128,128]{2,1,0:T(8,128)(2,1)} %bitcast.35, s32[80,128]{1,0:T(8,128)} %bitcast.38, bf16[8,128,128]{2,1,0:T(8,128)(2,1)} %copy-done.1, ...), custom_call_target="tpu_custom_call", output_to_operand_aliasing={{}: (6, {})} | custom-call | flops 335544320 | bytes 3932160 | tf_op jit(solution)/shard_map/pallas_call | solution.py:102
  26.1 10.2 %all-to-all-start.1 = ((bf16[32,288,128]{2,1,0:T(8,128)(2,1)}), bf16[32,288,128]{2,1,0:T(8,128)(2,1)S(1)}, u32[]{:S(2)}, u32[]{:S(2)}) async-start(bf16[32,288,128]{2,1,0:T(8,128)(2,1)} %shard_map.112), calls=%async_computation.1 | async-start | bytes 4718592 | tf_op jit(solution)/shard_map/all_to_all | solution.py:131
  36.3 0.0 copy-start.3
  36.3 0.0 copy-start.2
  36.3 31.5 %all-to-all-done.1 = bf16[32,288,128]{2,1,0:T(8,128)(2,1)S(1)} async-done(((bf16[32,288,128]{2,1,0:T(8,128)(2,1)}), bf16[32,288,128]{2,1,0:T(8,128)(2,1)S(1)}, u32[]{:S(2)}, u32[]{:S(2)}) %all-to-all-start.1) | async-done | bytes 2359328 | tf_op jit(solution)/shard_map/all_to_all | solution.py:131
  67.9 1.4 multiply_convert_fusion
  69.3 0.0 copy-done.3
  69.3 0.1 add_convert_fusion.1
  69.3 0.0 copy-done.2
  69.4 0.2 fusion.18
  69.5 0.0 copy-done
  69.5 0.2 fusion.17
  69.8 0.9 concatenate.22.into_ref
  70.7 3.5 %shard_map.113 = bf16[8,256,128]{2,1,0:T(8,128)(2,1)} custom-call(s32[1]{0:T(128)} %bitcast.33.live_ref, s32[80]{0:T(128)} %bitcast.46, s32[80]{0:T(128)} %bitcast.49, bf16[80,128,128]{2,1,0:T(8,128)(2,1)} %bitcast.36, s32[80,128]{1,0:T(8,128)} %bitcast.39, bf16[32,128,128]{2,1,0:T(8,128)(2,1)} %get-tuple-element.3.src_ref, ...), custom_call_target="tpu_custom_call", output_to_operand_aliasing={{}: (6, {})} | custom-call | flops 335544320 | bytes 3932160 | tf_op jit(solution)/shard_map/pallas_call | solution.py:102
  74.2 3.5 %all-to-all-start.2 = ((bf16[8,256,128]{2,1,0:T(8,128)(2,1)}), bf16[8,256,128]{2,1,0:T(8,128)(2,1)S(1)}, u32[]{:S(2)}, u32[]{:S(2)}) async-start(bf16[8,256,128]{2,1,0:T(8,128)(2,1)} %shard_map.113), calls=%async_computation.2 | async-start | bytes 1048576 | tf_op jit(solution)/shard_map/all_to_all | solution.py:131
  77.7 0.1 copy.23
  77.8 15.8 %all-to-all-done.2 = bf16[8,256,128]{2,1,0:T(8,128)(2,1)S(1)} async-done(((bf16[8,256,128]{2,1,0:T(8,128)(2,1)}), bf16[8,256,128]{2,1,0:T(8,128)(2,1)S(1)}, u32[]{:S(2)}, u32[]{:S(2)}) %all-to-all-start.2) | async-done | bytes 524320 | tf_op jit(solution)/shard_map/all_to_all | solution.py:131
  93.7 0.4 fusion
  94.1 0.4 fusion.7
  94.5 0.2 fusion.19
  94.7 0.1 fusion.1
  94.8 1.2 concatenate.26.into_ref
  96.0 0.7 slice.41.src_ref
  96.7 3.6 %shard_map.114 = bf16[32,160,128]{2,1,0:T(8,128)(2,1)} custom-call(s32[1]{0:T(128)} %bitcast.34.live_ref, s32[80]{0:T(128)} %bitcast.47, s32[80]{0:T(128)} %bitcast.50, bf16[80,128,128]{2,1,0:T(8,128)(2,1)} %bitcast.37, s32[80,128]{1,0:T(8,128)} %bitcast.40, bf16[8,128,128]{2,1,0:T(8,128)(2,1)} %slice.41.src_ref, ...), custom_call_target="tpu_custom_call", output_to_operand_aliasing={{}: (6, {})} | custom-call | flops 335544320 | bytes 3932160 | tf_op jit(solution)/shard_map/pallas_call | solution.py:102
  100.4 28.9 %all_to_all.30 = bf16[32,160,128]{2,1,0:T(8,128)(2,1)S(1)} all-to-all(bf16[32,160,128]{2,1,0:T(8,128)(2,1)} %shard_map.114), channel_id=1, replica_groups=mesh['row'=8,'col'=32] {'col'}, dimensions={0} | all-to-all | bytes 2621440 | tf_op jit(solution)/shard_map/all_to_all | solution.py:131
  129.3 0.3 convert_element_type.84
  129.6 9.5 %all_to_all.31 = bf16[8,32,128]{2,1,0:T(8,128)(2,1)S(1)} all-to-all(bf16[8,32,128]{2,1,0:T(8,128)(2,1)S(1)} %broadcast_in_dim.16), channel_id=1, replica_groups=mesh['row'=8,'col'=32] {'row'}, dimensions={0} | all-to-all | bytes 131072 | tf_op jit(solution)/shard_map/all_to_all | solution.py:127
  139.2 0.7 broadcast_in_dim.17
  139.9 5.0 %all-to-all-start.5 = ((bf16[32,32,128]{2,1,0:T(8,128)(2,1)}), bf16[32,32,128]{2,1,0:T(8,128)(2,1)S(1)}, u32[]{:S(2)}, u32[]{:S(2)}) async-start(bf16[32,32,128]{2,1,0:T(8,128)(2,1)} %broadcast_in_dim.17), calls=%async_computation.5 | async-start | bytes 524288 | tf_op jit(solution)/shard_map/all_to_all | solution.py:127
  144.9 0.1 slice_reduce_fusion
  145.0 0.7 add_convert_fusion
  145.7 8.2 %all-to-all-done.5 = bf16[32,32,128]{2,1,0:T(8,128)(2,1)S(1)} async-done(((bf16[32,32,128]{2,1,0:T(8,128)(2,1)}), bf16[32,32,128]{2,1,0:T(8,128)(2,1)S(1)}, u32[]{:S(2)}, u32[]{:S(2)}) %all-to-all-start.5) | async-done | bytes 262176 | tf_op jit(solution)/shard_map/all_to_all | solution.py:127
  153.9 0.8 fusion.16
  154.7 0.7 reshape.72
  (11 shorter events, 0.2 us)
Async XLA Ops:
  0.6 68.9 %copy-start = (bf16[512,128]{1,0:T(8,128)(2,1)S(1)}, bf16[512,128]{1,0:T(8,128)(2,1)}, u32[]{:S(2)}) copy-start(bf16[512,128]{1,0:T(8,128)(2,1)} %param.11) | copy-start | bytes 393220
  0.6 16.9 %copy-start.4 = (bf16[128,128]{1,0:T(8,128)(2,1)S(1)}, bf16[128,128]{1,0:T(8,128)(2,1)}, u32[]{:S(2)}) copy-start(bf16[128,128]{1,0:T(8,128)(2,1)} %param.17) | copy-start | bytes 98308
  2.2 19.5 %all-to-all-start = ((bf16[8,128,128]{2,1,0:T(8,128)(2,1)}), bf16[8,128,128]{2,1,0:T(8,128)(2,1)S(1)}, u32[]{:S(2)}, u32[]{:S(2)}) async-start(bf16[8,128,128]{2,1,0:T(8,128)(2,1)} %broadcast_in_dim.12), calls=%async_computation | async-start | bytes 524288 | tf_op jit(solution)/shard_map/all_to_all | solution.py:127
  21.7 0.7 copy-start.1
  26.1 41.7 %all-to-all-start.1 = ((bf16[32,288,128]{2,1,0:T(8,128)(2,1)}), bf16[32,288,128]{2,1,0:T(8,128)(2,1)S(1)}, u32[]{:S(2)}, u32[]{:S(2)}) async-start(bf16[32,288,128]{2,1,0:T(8,128)(2,1)} %shard_map.112), calls=%async_computation.1 | async-start | bytes 4718592 | tf_op jit(solution)/shard_map/all_to_all | solution.py:131
  36.3 33.0 %copy-start.3 = (bf16[128,128]{1,0:T(8,128)(2,1)S(1)}, bf16[128,128]{1,0:T(8,128)(2,1)}, u32[]{:S(2)}) copy-start(bf16[128,128]{1,0:T(8,128)(2,1)} %param.9) | copy-start | bytes 98308
  36.3 33.1 %copy-start.2 = (bf16[128,512]{1,0:T(8,128)(2,1)S(1)}, bf16[128,512]{1,0:T(8,128)(2,1)}, u32[]{:S(2)}) copy-start(bf16[128,512]{1,0:T(8,128)(2,1)} %param.10) | copy-start | bytes 393220
  74.2 19.5 %all-to-all-start.2 = ((bf16[8,256,128]{2,1,0:T(8,128)(2,1)}), bf16[8,256,128]{2,1,0:T(8,128)(2,1)S(1)}, u32[]{:S(2)}, u32[]{:S(2)}) async-start(bf16[8,256,128]{2,1,0:T(8,128)(2,1)} %shard_map.113), calls=%async_computation.2 | async-start | bytes 1048576 | tf_op jit(solution)/shard_map/all_to_all | solution.py:131
  139.9 14.0 %all-to-all-start.5 = ((bf16[32,32,128]{2,1,0:T(8,128)(2,1)}), bf16[32,32,128]{2,1,0:T(8,128)(2,1)S(1)}, u32[]{:S(2)}, u32[]{:S(2)}) async-start(bf16[32,32,128]{2,1,0:T(8,128)(2,1)} %broadcast_in_dim.17), calls=%async_computation.5 | async-start | bytes 524288 | tf_op jit(solution)/shard_map/all_to_all | solution.py:127

commit v7 on v6

--- a/solution.py
+++ b/solution.py
@@ -36,6 +36,11 @@
 def _masked_tile(tiles_ref, mask_ref, s, keep):
     column = mask_ref[pl.ds(s, 1), :].astype(jnp.float32) * keep
     return (tiles_ref[s].astype(jnp.float32) * column).astype(jnp.bfloat16)
+
+
+_SMEM = pl.BlockSpec(memory_space=pltpu.SMEM)
+_VMEM = pl.BlockSpec(memory_space=pltpu.VMEM)
+_ANY = pl.BlockSpec(memory_space=pl.ANY)
 
 
 def _forward_kernel(row_offset, live_ref, rows_ref, cols_ref, tiles_ref, mask_ref, src_ref, into_ref, out_ref,
@@ -63,6 +68,56 @@
     copy.wait()
 
 
+def _first_kernel(live_ref, rows_ref, cols_ref, tiles_ref, mask_ref, src_ref, shared_ref, out_ref, acc_ref, dacc_ref):
+    slots = tiles_ref.shape[0]
+    n_dst = acc_ref.shape[0]
+    n_src = src_ref.shape[0]
+    acc_ref[...] = jnp.zeros_like(acc_ref)
+    dacc_ref[...] = jnp.zeros_like(dacc_ref)
+    n_live = jnp.clip(live_ref[0], 0, slots)
+    first_row = (lax.broadcasted_iota(jnp.int32, (8, BLOCK), 0) == 0).astype(jnp.bfloat16)
+
+    def body(k, carry):
+        for u in range(UNROLL):
+            s, keep = _slot(k, u, n_live, slots)
+            r = jnp.clip(rows_ref[s], 0, n_dst - 1)
+            c = jnp.clip(cols_ref[s], 0, n_src - 1)
+            tile = _masked_tile(tiles_ref, mask_ref, s, keep)
+            acc_ref[r] += jnp.dot(tile, src_ref[c], preferred_element_type=jnp.float32)
+            dacc_ref[r] += lax.dot_general(
+                first_row, tile, (((1,), (1,)), ((), ())), preferred_element_type=jnp.float32
+            )
+        return carry
+
+    lax.fori_loop(0, (n_live + UNROLL - 1) // UNROLL, body, 0)
+    degree = jnp.sum(dacc_ref[...], axis=1).astype(out_ref.dtype)
+    shared = shared_ref[...]
+    n_deg = degree.shape[0]
+    for t in range(n_dst):
+        out_ref[t, 0:BLOCK, :] = acc_ref[t].astype(out_ref.dtype)
+        out_ref[t, BLOCK : BLOCK + n_deg, :] = degree
+        out_ref[t, BLOCK + n_deg :, :] = shared
+
+
+def first_aggregate(live, rows, cols, tiles, mask, src, shared, n_dst):
+    width = src.shape[-1]
+    slots = tiles.shape[0]
+    rows_out = BLOCK + n_dst + shared.shape[0]
+    flops = 2 * slots * BLOCK * BLOCK * (width + 8)
+    bytes_accessed = tiles.size * 2 + src.size * 2 + n_dst * rows_out * width * 2
+    return pl.pallas_call(
+        _first_kernel,
+        out_shape=jax.ShapeDtypeStruct((n_dst, rows_out, width), jnp.bfloat16),
+        in_specs=[_SMEM, _SMEM, _SMEM, _VMEM, _VMEM, _VMEM, _VMEM],
+        out_specs=_VMEM,
+        scratch_shapes=[
+            pltpu.VMEM((n_dst, BLOCK, width), jnp.float32),
+            pltpu.VMEM((n_dst, 8, BLOCK), jnp.float32),
+        ],
+        cost_estimate=pl.CostEstimate(flops=flops, bytes_accessed=bytes_accessed, transcendentals=0),
+    )(live, rows, cols, tiles, mask, src, shared)
+
+
 def _transpose_kernel(row_offset, live_ref, rows_ref, cols_ref, tiles_ref, mask_ref, src_ref, into_ref, out_ref,
                       acc_ref, stage_ref, sem):
     del into_ref
@@ -86,11 +141,6 @@
     copy = pltpu.make_async_copy(stage_ref, out_ref.at[:, pl.ds(row_offset, BLOCK), :], sem)
     copy.start()
     copy.wait()
-
-
-_SMEM = pl.BlockSpec(memory_space=pltpu.SMEM)
-_VMEM = pl.BlockSpec(memory_space=pltpu.VMEM)
-_ANY = pl.BlockSpec(memory_space=pl.ANY)
 
 
 def _aggregate_into(kernel, live, rows, cols, tiles, mask, src, into, row_offset):
@@ -163,16 +213,7 @@
     mask = column_mask[0, 0]
 
     x_panel = gather_blocks(features, "row")
-    live_weight = (jnp.arange(tiles.shape[0]) < jnp.clip(live[0], 0, tiles.shape[0])).astype(jnp.int32)
-    live_mask = (mask * live_weight[:, None]).astype(bf16)
-    row_sums = jnp.einsum("sij,sj->si", tiles, live_mask, preferred_element_type=f32)
-    partial_deg = jnp.zeros((row_groups, BLOCK), f32).at[jnp.clip(rows, 0, row_groups - 1)].add(row_sums)
-    shared = jnp.concatenate([partial_deg.astype(bf16), cotangent.T], axis=0)
-    packed = jnp.concatenate(
-        [jnp.zeros((row_groups, BLOCK, BLOCK), bf16), jnp.broadcast_to(shared[None], (row_groups,) + shared.shape)],
-        axis=1,
-    )
-    packed = forward_aggregate_into(live, rows, cols, tiles, mask, x_panel, packed, 0)
+    packed = first_aggregate(live, rows, cols, tiles, mask, x_panel, cotangent.T, row_groups)
     arrived = scatter_blocks(packed, "col")
     summed_in = jnp.sum(arrived[:, :BLOCK].astype(f32), axis=0)
     degrees = jnp.sum(arrived[:, BLOCK : BLOCK + row_groups].astype(f32), axis=0)

time: 156 us -> 158 us (1.013)
  blocking collectives: 38.4 us -> 57.5 us
  waiting for transfers between devices: 57.6 us -> 48 us
  matrix products: 4.51 us -> 1.35 us
  starting transfers between devices: 27.7 us -> 25.2 us
  other arithmetic: 5.3 us -> 2.81 us
    all_to_all x1 -> x2, blocking collectives: 28.9 us -> 47.9 us  [scatter_blocks(): return lax.all_to_all(blocks, axis, 0, 0, tiled=False)]
    all_to_all x2 -> x1, waiting for transfers between devices: 47.3 us -> 31.5 us  [scatter_blocks(): return lax.all_to_all(blocks, axis, 0, 0, tiled=False)]
    all_to_all x2, waiting for transfers between devices: 10.3 us -> 16.5 us  [gather_blocks(): lax.all_to_all(jnp.broadcast_to(block[None], (n,) + block.shape), axis, 0...]
    pallas_call x0 -> x1, Pallas kernels: none -> 4.88 us  [first_aggregate(): pl.pallas_call(_first_kernel, out_shape=jax.ShapeDtypeStruct((n_dst, rows...]
    pallas_call x3 -> x2, Pallas kernels: 10.8 us -> 7.13 us  [_aggregate_into(): pl.pallas_call(functools.partial(kernel, row_offset), out_shape=jax.Shape...]
    dot_general x1 -> x0, matrix products: 3.17 us -> none  [local(): jnp.einsum('sij,sj->si', tiles, live_mask, preferred_element_type=f32)]
    all_to_all x2 -> x1, starting transfers between devices: 13.7 us -> 11.2 us  [scatter_blocks(): return lax.all_to_all(blocks, axis, 0, 0, tiled=False)]
    concatenate x2 -> x0, local copies, waits for them, and re-layouts: 1.74 us -> none  [the longest x1 1.63 us: local(): jnp.concatenate([jnp.zeros((row_groups, BLOCK, BLOCK), bf16), jnp.broadca...]
  transfers between devices with their start and end apart: 4 -> 3, of which waited for: 4 -> 3; matrix products, arithmetic and copies ran while one was open for 6% -> 1% of each run, Pallas kernels for 0% -> 0%
where the time goes in v7:
time: 158 us; the launch traced here: 157 us
  blocking collectives  57.5 us (36%)
  waiting for transfers between devices  48 us (30%)
  starting transfers between devices  25.2 us (16%)
  Pallas kernels  12 us (8%)
  local copies, waits for them, and re-layouts  8.87 us (6%)
  other arithmetic  2.81 us (2%)
    all_to_all x2, blocking collectives, scatter_blocks(): return lax.all_to_all(blocks, axis, 0, 0, tiled=False)  47.9 us
    all_to_all x1, waiting for transfers between devices, scatter_blocks(): return lax.all_to_all(blocks, axis, 0, 0, tiled=False)  31.5 us
    all_to_all x2, waiting for transfers between devices, gather_blocks(): lax.all_to_all(jnp.broadcast_to(block[None], (n,) + block.shape), axis, 0...  16.5 us
    all_to_all x2, starting transfers between devices, gather_blocks(): lax.all_to_all(jnp.broadcast_to(block[None], (n,) + block.shape), axis, 0...  14 us
    all_to_all x1, starting transfers between devices, scatter_blocks(): return lax.all_to_all(blocks, axis, 0, 0, tiled=False)  11.2 us
    all_to_all x1, blocking collectives, gather_blocks(): lax.all_to_all(jnp.broadcast_to(block[None], (n,) + block.shape), axis, 0...  9.53 us
    pallas_call x2, Pallas kernels, _aggregate_into(): pl.pallas_call(functools.partial(kernel, row_offset), out_shape=jax.Shape...  7.13 us
    pallas_call x1, Pallas kernels, first_aggregate(): pl.pallas_call(_first_kernel, out_shape=jax.ShapeDtypeStruct((n_dst, rows...  4.88 us
  transfers between devices with their start and end apart: 3, of which 3 were waited for; matrix products, arithmetic and copies ran while one was open for 1% of the time, Pallas kernels for 0%

profile of v7, /device:TPU:1, one launch (start us, length us, event | category | flops | bytes accessed | tf_op | source)
XLA Modules:
  0.0 157.1 jit_solution(6724641050016283366)
XLA Ops:
  0.6 0.0 copy-start
  0.6 1.5 broadcast_in_dim.8
  2.2 9.0 %all-to-all-start = ((bf16[8,128,128]{2,1,0:T(8,128)(2,1)}), bf16[8,128,128]{2,1,0:T(8,128)(2,1)S(1)}, u32[]{:S(2)}, u32[]{:S(2)}) async-start(bf16[8,128,128]{2,1,0:T(8,128)(2,1)} %broadcast_in_dim.8), calls=%async_computation | async-start | bytes 524288 | tf_op jit(solution)/shard_map/all_to_all | solution.py:177
  11.2 1.5 copy.17
  13.3 8.4 %all-to-all-done.src_ref = bf16[8,128,128]{2,1,0:T(8,128)(2,1)S(1)} async-done(((bf16[8,128,128]{2,1,0:T(8,128)(2,1)}), bf16[8,128,128]{2,1,0:T(8,128)(2,1)S(1)}, u32[]{:S(2)}, u32[]{:S(2)}) %all-to-all-start) | async-done | bytes 262176 | tf_op jit(solution)/shard_map/all_to_all | solution.py:177
  21.7 0.0 copy-start.1
  21.7 0.7 copy-done.1
  22.4 4.9 %shard_map.112 = bf16[32,288,128]{2,1,0:T(8,128)(2,1)} custom-call(s32[1]{0:T(128)} %bitcast.20.live_ref, s32[80]{0:T(128)} %bitcast.32, s32[80]{0:T(128)} %bitcast.35, bf16[80,128,128]{2,1,0:T(8,128)(2,1)} %bitcast.23, s32[80,128]{1,0:T(8,128)} %bitcast.26, bf16[8,128,128]{2,1,0:T(8,128)(2,1)} %copy-done.1, bf16[128,128]{1,0:T(8,128)(2,1)} %bitcast.31), custom_call_target="tpu_custom_call" | custom-call | flops 356515840 | bytes 5242880 | tf_op jit(solution)/shard_map/pallas_call | solution.py:108
  27.3 11.2 %all-to-all-start.1 = ((bf16[32,288,128]{2,1,0:T(8,128)(2,1)}), bf16[32,288,128]{2,1,0:T(8,128)(2,1)S(1)}, u32[]{:S(2)}, u32[]{:S(2)}) async-start(bf16[32,288,128]{2,1,0:T(8,128)(2,1)} %shard_map.112), calls=%async_computation.1 | async-start | bytes 4718592 | tf_op jit(solution)/shard_map/all_to_all | solution.py:181
  38.4 0.0 copy-start.4
  38.4 0.0 copy-start.3
  38.5 31.5 %all-to-all-done.1 = bf16[32,288,128]{2,1,0:T(8,128)(2,1)S(1)} async-done(((bf16[32,288,128]{2,1,0:T(8,128)(2,1)}), bf16[32,288,128]{2,1,0:T(8,128)(2,1)S(1)}, u32[]{:S(2)}, u32[]{:S(2)}) %all-to-all-start.1) | async-done | bytes 2359328 | tf_op jit(solution)/shard_map/all_to_all | solution.py:181
  70.0 1.4 multiply_convert_fusion
  71.4 0.0 copy-done.4
  71.4 0.1 add_convert_fusion.1
  71.5 0.0 copy-done.3
  71.5 0.2 fusion.11
  71.7 0.0 copy-done
  71.7 0.2 fusion.10
  72.0 0.9 concatenate.14.into_ref
  72.8 0.0 copy-start.2
  72.8 3.5 %shard_map.113 = bf16[8,256,128]{2,1,0:T(8,128)(2,1)} custom-call(s32[1]{0:T(128)} %bitcast.21.live_ref, s32[80]{0:T(128)} %bitcast.33, s32[80]{0:T(128)} %bitcast.36, bf16[80,128,128]{2,1,0:T(8,128)(2,1)} %bitcast.24, s32[80,128]{1,0:T(8,128)} %bitcast.27, bf16[32,128,128]{2,1,0:T(8,128)(2,1)} %get-tuple-element.3.src_ref, ...), custom_call_target="tpu_custom_call", output_to_operand_aliasing={{}: (6, {})} | custom-call | flops 335544320 | bytes 3932160 | tf_op jit(solution)/shard_map/pallas_call | solution.py:152
  76.3 18.7 %all_to_all.30 = bf16[8,256,128]{2,1,0:T(8,128)(2,1)S(1)} all-to-all(bf16[8,256,128]{2,1,0:T(8,128)(2,1)} %shard_map.113), channel_id=1, replica_groups=mesh['row'=8,'col'=32] {'row'}, dimensions={0} | all-to-all | bytes 1048576 | tf_op jit(solution)/shard_map/all_to_all | solution.py:181
  95.1 0.0 copy-done.2
  95.1 0.4 fusion
  95.5 0.4 fusion.7
  95.9 0.2 fusion.12
  96.1 0.1 fusion.1
  96.2 1.2 concatenate.18.into_ref
  97.4 0.7 slice.41.src_ref
  98.1 3.6 %shard_map.114 = bf16[32,160,128]{2,1,0:T(8,128)(2,1)} custom-call(s32[1]{0:T(128)} %bitcast.22.live_ref, s32[80]{0:T(128)} %bitcast.34, s32[80]{0:T(128)} %bitcast.37, bf16[80,128,128]{2,1,0:T(8,128)(2,1)} %bitcast.25, s32[80,128]{1,0:T(8,128)} %bitcast.28, bf16[8,128,128]{2,1,0:T(8,128)(2,1)} %slice.41.src_ref, ...), custom_call_target="tpu_custom_call", output_to_operand_aliasing={{}: (6, {})} | custom-call | flops 335544320 | bytes 3932160 | tf_op jit(solution)/shard_map/pallas_call | solution.py:152
  101.8 29.2 %all_to_all.31 = bf16[32,160,128]{2,1,0:T(8,128)(2,1)S(1)} all-to-all(bf16[32,160,128]{2,1,0:T(8,128)(2,1)} %shard_map.114), channel_id=1, replica_groups=mesh['row'=8,'col'=32] {'col'}, dimensions={0} | all-to-all | bytes 2621440 | tf_op jit(solution)/shard_map/all_to_all | solution.py:181
  131.0 0.3 convert_element_type.68
  131.4 9.5 %all_to_all.32 = bf16[8,32,128]{2,1,0:T(8,128)(2,1)S(1)} all-to-all(bf16[8,32,128]{2,1,0:T(8,128)(2,1)S(1)} %broadcast_in_dim.10), channel_id=1, replica_groups=mesh['row'=8,'col'=32] {'row'}, dimensions={0} | all-to-all | bytes 131072 | tf_op jit(solution)/shard_map/all_to_all | solution.py:177
  140.9 0.7 broadcast_in_dim.11
  141.6 5.0 %all-to-all-start.5 = ((bf16[32,32,128]{2,1,0:T(8,128)(2,1)}), bf16[32,32,128]{2,1,0:T(8,128)(2,1)S(1)}, u32[]{:S(2)}, u32[]{:S(2)}) async-start(bf16[32,32,128]{2,1,0:T(8,128)(2,1)} %broadcast_in_dim.11), calls=%async_computation.5 | async-start | bytes 524288 | tf_op jit(solution)/shard_map/all_to_all | solution.py:177
  146.6 0.1 slice_reduce_fusion
  146.8 0.7 add_convert_fusion
  147.5 8.2 %all-to-all-done.5 = bf16[32,32,128]{2,1,0:T(8,128)(2,1)S(1)} async-done(((bf16[32,32,128]{2,1,0:T(8,128)(2,1)}), bf16[32,32,128]{2,1,0:T(8,128)(2,1)S(1)}, u32[]{:S(2)}, u32[]{:S(2)}) %all-to-all-start.5) | async-done | bytes 262176 | tf_op jit(solution)/shard_map/all_to_all | solution.py:177
  155.6 0.8 fusion.9
  156.4 0.7 reshape.40
  (9 shorter events, 0.2 us)
Async XLA Ops:
  0.6 71.1 %copy-start = (bf16[512,128]{1,0:T(8,128)(2,1)S(1)}, bf16[512,128]{1,0:T(8,128)(2,1)}, u32[]{:S(2)}) copy-start(bf16[512,128]{1,0:T(8,128)(2,1)} %param.11) | copy-start | bytes 393220
  2.2 19.5 %all-to-all-start = ((bf16[8,128,128]{2,1,0:T(8,128)(2,1)}), bf16[8,128,128]{2,1,0:T(8,128)(2,1)S(1)}, u32[]{:S(2)}, u32[]{:S(2)}) async-start(bf16[8,128,128]{2,1,0:T(8,128)(2,1)} %broadcast_in_dim.8), calls=%async_computation | async-start | bytes 524288 | tf_op jit(solution)/shard_map/all_to_all | solution.py:177
  21.7 0.7 copy-start.1
  27.3 42.7 %all-to-all-start.1 = ((bf16[32,288,128]{2,1,0:T(8,128)(2,1)}), bf16[32,288,128]{2,1,0:T(8,128)(2,1)S(1)}, u32[]{:S(2)}, u32[]{:S(2)}) async-start(bf16[32,288,128]{2,1,0:T(8,128)(2,1)} %shard_map.112), calls=%async_computation.1 | async-start | bytes 4718592 | tf_op jit(solution)/shard_map/all_to_all | solution.py:181
  38.4 33.0 %copy-start.4 = (bf16[128,128]{1,0:T(8,128)(2,1)S(1)}, bf16[128,128]{1,0:T(8,128)(2,1)}, u32[]{:S(2)}) copy-start(bf16[128,128]{1,0:T(8,128)(2,1)} %param.9) | copy-start | bytes 98308
  38.4 33.1 %copy-start.3 = (bf16[128,512]{1,0:T(8,128)(2,1)S(1)}, bf16[128,512]{1,0:T(8,128)(2,1)}, u32[]{:S(2)}) copy-start(bf16[128,512]{1,0:T(8,128)(2,1)} %param.10) | copy-start | bytes 393220
  72.8 22.3 %copy-start.2 = (bf16[128,128]{0,1:T(8,128)(2,1)S(1)}, bf16[128,128]{0,1:T(8,128)(2,1)}, u32[]{:S(2)}) copy-start(bf16[128,128]{0,1:T(8,128)(2,1)} %copy.17) | copy-start | bytes 98308
  141.6 14.0 %all-to-all-start.5 = ((bf16[32,32,128]{2,1,0:T(8,128)(2,1)}), bf16[32,32,128]{2,1,0:T(8,128)(2,1)S(1)}, u32[]{:S(2)}, u32[]{:S(2)}) async-start(bf16[32,32,128]{2,1,0:T(8,128)(2,1)} %broadcast_in_dim.11), calls=%async_computation.5 | async-start | bytes 524288 | tf_op jit(solution)/shard_map/all_to_all | solution.py:177

commit v8 on v6

--- a/solution.py
+++ b/solution.py
@@ -38,8 +38,8 @@
     return (tiles_ref[s].astype(jnp.float32) * column).astype(jnp.bfloat16)
 
 
-def _forward_kernel(row_offset, live_ref, rows_ref, cols_ref, tiles_ref, mask_ref, src_ref, into_ref, out_ref,
-                    acc_ref, stage_ref, sem):
+def _forward_kernel(row_offset, src_offset, live_ref, rows_ref, cols_ref, tiles_ref, mask_ref, src_ref, into_ref,
+                    out_ref, acc_ref, stage_ref, sem):
     del into_ref
     slots = tiles_ref.shape[0]
     n_dst = acc_ref.shape[0]
@@ -53,7 +53,8 @@
             r = jnp.clip(rows_ref[s], 0, n_dst - 1)
             c = jnp.clip(cols_ref[s], 0, n_src - 1)
             tile = _masked_tile(tiles_ref, mask_ref, s, keep)
-            acc_ref[r] += jnp.dot(tile, src_ref[c], preferred_element_type=jnp.float32)
+            source = src_ref[c, src_offset : src_offset + BLOCK, :]
+            acc_ref[r] += jnp.dot(tile, source, preferred_element_type=jnp.float32)
         return carry
 
     lax.fori_loop(0, (n_live + UNROLL - 1) // UNROLL, body, 0)
@@ -63,8 +64,8 @@
     copy.wait()
 
 
-def _transpose_kernel(row_offset, live_ref, rows_ref, cols_ref, tiles_ref, mask_ref, src_ref, into_ref, out_ref,
-                      acc_ref, stage_ref, sem):
+def _transpose_kernel(row_offset, src_offset, live_ref, rows_ref, cols_ref, tiles_ref, mask_ref, src_ref, scale_ref,
+                      into_ref, out_ref, acc_ref, stage_ref, sem):
     del into_ref
     slots = tiles_ref.shape[0]
     n_dst = acc_ref.shape[0]
@@ -78,7 +79,10 @@
             r = jnp.clip(rows_ref[s], 0, n_src - 1)
             c = jnp.clip(cols_ref[s], 0, n_dst - 1)
             tile = _masked_tile(tiles_ref, mask_ref, s, keep)
-            acc_ref[c] += jnp.dot(src_ref[r], tile, preferred_element_type=jnp.float32)
+            scale = scale_ref[pl.ds(r, 1), :]
+            source = src_ref[r, src_offset : src_offset + BLOCK, :].astype(jnp.float32)
+            source = (source * scale).astype(jnp.bfloat16)
+            acc_ref[c] += jnp.dot(source, tile, preferred_element_type=jnp.float32)
         return carry
 
     lax.fori_loop(0, (n_live + UNROLL - 1) // UNROLL, body, 0)
@@ -93,33 +97,41 @@
 _ANY = pl.BlockSpec(memory_space=pl.ANY)
 
 
-def _aggregate_into(kernel, live, rows, cols, tiles, mask, src, into, row_offset):
+def _aggregate_into(kernel, operands, n_vmem, into, row_offset, src_offset, tiles, src_bytes):
     n_dst = into.shape[0]
     width = into.shape[2]
     slots = tiles.shape[0]
     flops = 2 * slots * BLOCK * BLOCK * width
-    bytes_accessed = tiles.size * 2 + src.size * 2 + n_dst * BLOCK * width * 2
+    bytes_accessed = tiles.size * 2 + src_bytes + n_dst * BLOCK * width * 2
     return pl.pallas_call(
-        functools.partial(kernel, row_offset),
+        functools.partial(kernel, row_offset, src_offset),
         out_shape=jax.ShapeDtypeStruct(into.shape, into.dtype),
-        in_specs=[_SMEM, _SMEM, _SMEM, _VMEM, _VMEM, _VMEM, _ANY],
+        in_specs=[_SMEM, _SMEM, _SMEM] + [_VMEM] * n_vmem + [_ANY],
         out_specs=_ANY,
         scratch_shapes=[
             pltpu.VMEM((n_dst, BLOCK, width), jnp.float32),
             pltpu.VMEM((n_dst, BLOCK, width), into.dtype),
             pltpu.SemaphoreType.DMA(()),
         ],
-        input_output_aliases={6: 0},
+        input_output_aliases={3 + n_vmem: 0},
         cost_estimate=pl.CostEstimate(flops=flops, bytes_accessed=bytes_accessed, transcendentals=0),
-    )(live, rows, cols, tiles, mask, src, into)
-
-
-def forward_aggregate_into(live, rows, cols, tiles, mask, src, into, row_offset):
-    return _aggregate_into(_forward_kernel, live, rows, cols, tiles, mask, src, into, row_offset)
-
-
-def transpose_aggregate_into(live, rows, cols, tiles, mask, src_t, into, row_offset):
-    return _aggregate_into(_transpose_kernel, live, rows, cols, tiles, mask, src_t, into, row_offset)
+    )(*operands, into)
+
+
+def forward_aggregate_into(live, rows, cols, tiles, mask, src, src_offset, into, row_offset):
+    n_src = src.shape[0]
+    return _aggregate_into(
+        _forward_kernel, (live, rows, cols, tiles, mask, src), 3, into, row_offset, src_offset, tiles,
+        n_src * BLOCK * BLOCK * 2,
+    )
+
+
+def transpose_aggregate_into(live, rows, cols, tiles, mask, src_t, src_offset, scale, into, row_offset):
+    n_src = src_t.shape[0]
+    return _aggregate_into(
+        _transpose_kernel, (live, rows, cols, tiles, mask, src_t, scale), 4, into, row_offset, src_offset, tiles,
+        n_src * BLOCK * BLOCK * 2,
+    )
 
 
 def gather_blocks(block, axis):
@@ -172,11 +184,10 @@
         [jnp.zeros((row_groups, BLOCK, BLOCK), bf16), jnp.broadcast_to(shared[None], (row_groups,) + shared.shape)],
         axis=1,
     )
-    packed = forward_aggregate_into(live, rows, cols, tiles, mask, x_panel, packed, 0)
+    packed = forward_aggregate_into(live, rows, cols, tiles, mask, x_panel, 0, packed, 0)
     arrived = scatter_blocks(packed, "col")
     summed_in = jnp.sum(arrived[:, :BLOCK].astype(f32), axis=0)
     degrees = jnp.sum(arrived[:, BLOCK : BLOCK + row_groups].astype(f32), axis=0)
-    group_cot_t = arrived[:, BLOCK + row_groups :]
     group_scale = 1.0 / jnp.sqrt(1.0 + degrees)
     me = lax.axis_index("col")
     row_scale = lax.dynamic_index_in_dim(group_scale, me, axis=0, keepdims=False)[:, None]
@@ -186,7 +197,6 @@
     hidden = gelu_tanh(first_pre).astype(bf16)
     projected = jnp.dot(hidden, second_weight, preferred_element_type=f32)
 
-    grad_panel_t = (group_scale[:, None, :] * group_cot_t.astype(f32)).astype(bf16)
     packed = jnp.concatenate(
         [
             jnp.broadcast_to(projected.astype(bf16)[None], (col_groups, BLOCK, BLOCK)),
@@ -194,9 +204,10 @@
         ],
         axis=1,
     )
-    packed = transpose_aggregate_into(live, rows, cols, tiles, mask, grad_panel_t, packed, BLOCK)
+    packed = transpose_aggregate_into(
+        live, rows, cols, tiles, mask, arrived, BLOCK + row_groups, group_scale, packed, BLOCK
+    )
     arrived = scatter_blocks(packed, "row")
-    y_panel = arrived[:, :BLOCK]
     returned_t = jnp.sum(arrived[:, BLOCK:].astype(f32), axis=0)
 
     hp = lax.Precision.HIGHEST
@@ -210,7 +221,7 @@
     slices = flat.reshape(row_groups, -1, BLOCK)
 
     packed = jnp.concatenate([jnp.zeros((row_groups, BLOCK, BLOCK), bf16), slices.astype(bf16)], axis=1)
-    packed = forward_aggregate_into(live, rows, cols, tiles, mask, y_panel, packed, 0)
+    packed = forward_aggregate_into(live, rows, cols, tiles, mask, arrived, 0, packed, 0)
     arrived = scatter_blocks(packed, "col").astype(f32)
     summed_y = jnp.sum(arrived[:, :BLOCK], axis=0)
     output = (projected + row_scale * summed_y).astype(bf16)

time: 156 us -> 155 us (level)
  no operation moved by 1% of the time
where the time goes in v8:
time: 155 us; the launch traced here: 154 us
  waiting for transfers between devices  57.6 us (37%)
  blocking collectives  38.8 us (25%)
  starting transfers between devices  28.4 us (18%)
  Pallas kernels  10.4 us (7%)
  local copies, waits for them, and re-layouts  8.83 us (6%)
  matrix products  4.51 us (3%)
  other arithmetic  4.06 us (3%)
  between operations  1.56 us (1%)
    all_to_all x2, waiting for transfers between devices, scatter_blocks(): return lax.all_to_all(blocks, axis, 0, 0, tiled=False)  47.4 us
    all_to_all x1, blocking collectives, scatter_blocks(): return lax.all_to_all(blocks, axis, 0, 0, tiled=False)  29.3 us
    all_to_all x2, starting transfers between devices, scatter_blocks(): return lax.all_to_all(blocks, axis, 0, 0, tiled=False)  14.4 us
    all_to_all x2, starting transfers between devices, gather_blocks(): lax.all_to_all(jnp.broadcast_to(block[None], (n,) + block.shape), axis, 0...  14 us
    pallas_call x3, Pallas kernels, _aggregate_into(): pl.pallas_call(functools.partial(kernel, row_offset, src_offset), out_sha...  10.4 us
    all_to_all x2, waiting for transfers between devices, gather_blocks(): lax.all_to_all(jnp.broadcast_to(block[None], (n,) + block.shape), axis, 0...  10.3 us
    all_to_all x1, blocking collectives, gather_blocks(): lax.all_to_all(jnp.broadcast_to(block[None], (n,) + block.shape), axis, 0...  9.53 us
    dot_general x1, matrix products, local(): jnp.einsum('sij,sj->si', tiles, live_mask, preferred_element_type=f32)  3.17 us
  transfers between devices with their start and end apart: 4, of which 4 were waited for; matrix products, arithmetic and copies ran while one was open for 6% of the time, Pallas kernels for 0%

profile of v8, /device:TPU:1, one launch (start us, length us, event | category | flops | bytes accessed | tf_op | source)
XLA Modules:
  0.0 154.2 jit_solution(6856660336404471185)
XLA Ops:
  0.6 0.0 copy-start
  0.6 0.0 copy-start.6
  0.7 1.5 broadcast_in_dim.12
  2.2 9.0 %all-to-all-start = ((bf16[8,128,128]{2,1,0:T(8,128)(2,1)}), bf16[8,128,128]{2,1,0:T(8,128)(2,1)S(1)}, u32[]{:S(2)}, u32[]{:S(2)}) async-start(bf16[8,128,128]{2,1,0:T(8,128)(2,1)} %broadcast_in_dim.12), calls=%async_computation | async-start | bytes 524288 | tf_op jit(solution)/shard_map/all_to_all | solution.py:139
  11.9 0.9 fusion.10
  12.7 0.7 fusion.13
  13.4 3.2 %fusion.8 = f32[80,1,128]{2,1,0:T(1,128)S(1)} fusion(bf16[80,128,1]{1,0,2:T(8,128)(2,1)S(1)} %fusion.10, bf16[1,1,80,128,128]{4,3,2,1,0:T(8,128)(2,1)} %param.16), kind=kOutput, calls=%fused_computation.23 | convolution fusion | flops 2621440 | bytes 2682880 | tf_op jit(solution)/shard_map/sij,sj->si/dot_general | solution.py:180
  16.6 0.9 scatter_custom_fusion
  17.5 0.1 copy.21
  17.6 0.0 copy-done.6
  17.6 0.1 pad_maximum_fusion
  17.7 0.1 copy.22
  17.8 0.2 broadcast_in_dim.14
  18.0 1.6 %concatenate.21.into_ref = bf16[32,288,128]{2,1,0:T(8,128)(2,1)} pad(bf16[32,160,128]{2,1,0:T(8,128)(2,1)S(1)} %broadcast_in_dim.14, bf16[]{:T(256)} %constant.6.clone.1), padding=0_0x128_0x0_0 | pad | bytes 3670018 | tf_op jit(solution)/shard_map/concatenate | solution.py:183
  19.6 2.1 %all-to-all-done.src_ref = bf16[8,128,128]{2,1,0:T(8,128)(2,1)S(1)} async-done(((bf16[8,128,128]{2,1,0:T(8,128)(2,1)}), bf16[8,128,128]{2,1,0:T(8,128)(2,1)S(1)}, u32[]{:S(2)}, u32[]{:S(2)}) %all-to-all-start) | async-done | bytes 262176 | tf_op jit(solution)/shard_map/all_to_all | solution.py:139
  21.7 0.0 copy-start.3
  21.7 0.7 copy-done.3
  22.4 3.4 %shard_map.112 = bf16[32,288,128]{2,1,0:T(8,128)(2,1)} custom-call(s32[1]{0:T(128)} %bitcast.32.live_ref, s32[80]{0:T(128)} %bitcast.45, s32[80]{0:T(128)} %bitcast.48, bf16[80,128,128]{2,1,0:T(8,128)(2,1)} %bitcast.35, s32[80,128]{1,0:T(8,128)} %bitcast.38, bf16[8,128,128]{2,1,0:T(8,128)(2,1)} %copy-done.3, ...), custom_call_target="tpu_custom_call", output_to_operand_aliasing={{}: (6, {})} | custom-call | flops 335544320 | bytes 3932160 | tf_op jit(solution)/shard_map/pallas_call | solution.py:106
  25.8 0.0 copy-start.5
  25.8 0.0 copy-start.4
  25.8 10.6 %all-to-all-start.1 = ((bf16[32,288,128]{2,1,0:T(8,128)(2,1)}), bf16[32,288,128]{2,1,0:T(8,128)(2,1)S(1)}, u32[]{:S(2)}, u32[]{:S(2)}) async-start(bf16[32,288,128]{2,1,0:T(8,128)(2,1)} %shard_map.112), calls=%async_computation.1 | async-start | bytes 4718592 | tf_op jit(solution)/shard_map/all_to_all | solution.py:143
  36.4 31.5 %all-to-all-done.1.src_ref = bf16[32,288,128]{2,1,0:T(8,128)(2,1)S(1)} async-done(((bf16[32,288,128]{2,1,0:T(8,128)(2,1)}), bf16[32,288,128]{2,1,0:T(8,128)(2,1)S(1)}, u32[]{:S(2)}, u32[]{:S(2)}) %all-to-all-start.1) | async-done | bytes 2359328 | tf_op jit(solution)/shard_map/all_to_all | solution.py:143
  67.9 0.0 copy-start.1
  68.0 0.0 copy-start.7
  68.0 0.2 convert_reduce_fusion
  68.2 0.0 copy-done.5
  68.2 0.1 add_convert_fusion.1
  68.3 0.0 copy-done.4
  68.3 0.2 fusion.18
  68.5 0.0 copy-done
  68.5 0.2 fusion.17
  68.7 0.9 concatenate.22.into_ref
  69.6 0.0 copy-done.1
  69.6 0.0 copy-done.7
  69.6 3.6 %shard_map.113 = bf16[8,256,128]{2,1,0:T(8,128)(2,1)} custom-call(s32[1]{0:T(128)} %bitcast.33.live_ref, s32[80]{0:T(128)} %bitcast.46, s32[80]{0:T(128)} %bitcast.49, bf16[80,128,128]{2,1,0:T(8,128)(2,1)} %bitcast.36, s32[80,128]{1,0:T(8,128)} %bitcast.39, bf16[32,288,128]{2,1,0:T(8,128)(2,1)} %copy-done.1, ...), custom_call_target="tpu_custom_call", output_to_operand_aliasing={{}: (7, {})} | custom-call | flops 335544320 | bytes 3932160 | tf_op jit(solution)/shard_map/pallas_call | solution.py:106
  73.2 3.8 %all-to-all-start.2 = ((bf16[8,256,128]{2,1,0:T(8,128)(2,1)}), bf16[8,256,128]{2,1,0:T(8,128)(2,1)S(1)}, u32[]{:S(2)}, u32[]{:S(2)}) async-start(bf16[8,256,128]{2,1,0:T(8,128)(2,1)} %shard_map.113), calls=%async_computation.2 | async-start | bytes 1048576 | tf_op jit(solution)/shard_map/all_to_all | solution.py:143
  77.0 0.1 copy.23
  77.2 15.9 %all-to-all-done.2.src_ref = bf16[8,256,128]{2,1,0:T(8,128)(2,1)S(1)} async-done(((bf16[8,256,128]{2,1,0:T(8,128)(2,1)}), bf16[8,256,128]{2,1,0:T(8,128)(2,1)S(1)}, u32[]{:S(2)}, u32[]{:S(2)}) %all-to-all-start.2) | async-done | bytes 524320 | tf_op jit(solution)/shard_map/all_to_all | solution.py:143
  93.0 0.0 copy-start.2
  93.1 0.4 fusion
  93.5 0.4 fusion.7
  93.9 0.2 fusion.19
  94.1 0.1 fusion.1
  94.2 1.2 concatenate.26.into_ref
  95.4 0.0 copy-done.2
  95.4 3.4 %shard_map.114 = bf16[32,160,128]{2,1,0:T(8,128)(2,1)} custom-call(s32[1]{0:T(128)} %bitcast.34.live_ref, s32[80]{0:T(128)} %bitcast.47, s32[80]{0:T(128)} %bitcast.50, bf16[80,128,128]{2,1,0:T(8,128)(2,1)} %bitcast.37, s32[80,128]{1,0:T(8,128)} %bitcast.40, bf16[8,256,128]{2,1,0:T(8,128)(2,1)} %copy-done.2, ...), custom_call_target="tpu_custom_call", output_to_operand_aliasing={{}: (6, {})} | custom-call | flops 335544320 | bytes 3932160 | tf_op jit(solution)/shard_map/pallas_call | solution.py:106
  98.8 29.3 %all_to_all.30 = bf16[32,160,128]{2,1,0:T(8,128)(2,1)S(1)} all-to-all(bf16[32,160,128]{2,1,0:T(8,128)(2,1)} %shard_map.114), channel_id=1, replica_groups=mesh['row'=8,'col'=32] {'col'}, dimensions={0} | all-to-all | bytes 2621440 | tf_op jit(solution)/shard_map/all_to_all | solution.py:143
  128.1 0.3 convert_element_type.76
  128.4 9.5 %all_to_all.31 = bf16[8,32,128]{2,1,0:T(8,128)(2,1)S(1)} all-to-all(bf16[8,32,128]{2,1,0:T(8,128)(2,1)S(1)} %broadcast_in_dim.16), channel_id=1, replica_groups=mesh['row'=8,'col'=32] {'row'}, dimensions={0} | all-to-all | bytes 131072 | tf_op jit(solution)/shard_map/all_to_all | solution.py:139
  138.0 0.7 broadcast_in_dim.17
  138.7 5.0 %all-to-all-start.5 = ((bf16[32,32,128]{2,1,0:T(8,128)(2,1)}), bf16[32,32,128]{2,1,0:T(8,128)(2,1)S(1)}, u32[]{:S(2)}, u32[]{:S(2)}) async-start(bf16[32,32,128]{2,1,0:T(8,128)(2,1)} %broadcast_in_dim.17), calls=%async_computation.5 | async-start | bytes 524288 | tf_op jit(solution)/shard_map/all_to_all | solution.py:139
  143.7 0.1 slice_reduce_fusion
  143.8 0.7 add_convert_fusion
  144.5 8.2 %all-to-all-done.5 = bf16[32,32,128]{2,1,0:T(8,128)(2,1)S(1)} async-done(((bf16[32,32,128]{2,1,0:T(8,128)(2,1)}), bf16[32,32,128]{2,1,0:T(8,128)(2,1)S(1)}, u32[]{:S(2)}, u32[]{:S(2)}) %all-to-all-start.5) | async-done | bytes 262176 | tf_op jit(solution)/shard_map/all_to_all | solution.py:139
  152.7 0.8 fusion.16
  153.5 0.7 reshape.68
  (11 shorter events, 0.2 us)
Async XLA Ops:
  0.6 67.8 %copy-start = (bf16[512,128]{1,0:T(8,128)(2,1)S(1)}, bf16[512,128]{1,0:T(8,128)(2,1)}, u32[]{:S(2)}) copy-start(bf16[512,128]{1,0:T(8,128)(2,1)} %param.11) | copy-start | bytes 393220
  0.6 16.9 %copy-start.6 = (bf16[128,128]{1,0:T(8,128)(2,1)S(1)}, bf16[128,128]{1,0:T(8,128)(2,1)}, u32[]{:S(2)}) copy-start(bf16[128,128]{1,0:T(8,128)(2,1)} %param.17) | copy-start | bytes 98308
  2.2 19.5 %all-to-all-start = ((bf16[8,128,128]{2,1,0:T(8,128)(2,1)}), bf16[8,128,128]{2,1,0:T(8,128)(2,1)S(1)}, u32[]{:S(2)}, u32[]{:S(2)}) async-start(bf16[8,128,128]{2,1,0:T(8,128)(2,1)} %broadcast_in_dim.12), calls=%async_computation | async-start | bytes 524288 | tf_op jit(solution)/shard_map/all_to_all | solution.py:139
  21.7 0.7 copy-start.3
  25.8 42.4 %copy-start.5 = (bf16[128,128]{1,0:T(8,128)(2,1)S(1)}, bf16[128,128]{1,0:T(8,128)(2,1)}, u32[]{:S(2)}) copy-start(bf16[128,128]{1,0:T(8,128)(2,1)} %param.9) | copy-start | bytes 98308
  25.8 42.5 %copy-start.4 = (bf16[128,512]{1,0:T(8,128)(2,1)S(1)}, bf16[128,512]{1,0:T(8,128)(2,1)}, u32[]{:S(2)}) copy-start(bf16[128,512]{1,0:T(8,128)(2,1)} %param.10) | copy-start | bytes 393220
  25.8 42.1 %all-to-all-start.1 = ((bf16[32,288,128]{2,1,0:T(8,128)(2,1)}), bf16[32,288,128]{2,1,0:T(8,128)(2,1)S(1)}, u32[]{:S(2)}, u32[]{:S(2)}) async-start(bf16[32,288,128]{2,1,0:T(8,128)(2,1)} %shard_map.112), calls=%async_computation.1 | async-start | bytes 4718592 | tf_op jit(solution)/shard_map/all_to_all | solution.py:143
  67.9 1.7 %copy-start.1 = (bf16[32,288,128]{2,1,0:T(8,128)(2,1)}, bf16[32,288,128]{2,1,0:T(8,128)(2,1)S(1)}, u32[]{:S(2)}) copy-start(bf16[32,288,128]{2,1,0:T(8,128)(2,1)S(1)} %all-to-all-done.1.src_ref) | copy-start | bytes 7077892
  68.0 1.6 %copy-start.7 = (f32[32,128]{1,0:T(8,128)}, f32[32,128]{1,0:T(8,128)S(1)}, u32[]{:S(2)}) copy-start(f32[32,128]{1,0:T(8,128)S(1)} %add_rsqrt_fusion.scale_ref) | copy-start | bytes 49156
  73.2 19.8 %all-to-all-start.2 = ((bf16[8,256,128]{2,1,0:T(8,128)(2,1)}), bf16[8,256,128]{2,1,0:T(8,128)(2,1)S(1)}, u32[]{:S(2)}, u32[]{:S(2)}) async-start(bf16[8,256,128]{2,1,0:T(8,128)(2,1)} %shard_map.113), calls=%async_computation.2 | async-start | bytes 1048576 | tf_op jit(solution)/shard_map/all_to_all | solution.py:143
  93.0 2.3 %copy-start.2 = (bf16[8,256,128]{2,1,0:T(8,128)(2,1)}, bf16[8,256,128]{2,1,0:T(8,128)(2,1)S(1)}, u32[]{:S(2)}) copy-start(bf16[8,256,128]{2,1,0:T(8,128)(2,1)S(1)} %all-to-all-done.2.src_ref) | copy-start | bytes 1572868
  138.7 14.0 %all-to-all-start.5 = ((bf16[32,32,128]{2,1,0:T(8,128)(2,1)}), bf16[32,32,128]{2,1,0:T(8,128)(2,1)S(1)}, u32[]{:S(2)}, u32[]{:S(2)}) async-start(bf16[32,32,128]{2,1,0:T(8,128)(2,1)} %broadcast_in_dim.17), calls=%async_computation.5 | async-start | bytes 524288 | tf_op jit(solution)/shard_map/all_to_all | solution.py:139

commit v9 on v8

--- a/solution.py
+++ b/solution.py
@@ -214,10 +214,10 @@
     combined = cotangent.astype(f32) + returned_t.T
     hidden_grad = jnp.dot(combined, second_weight.astype(f32).T, precision=hp, preferred_element_type=f32)
     pre_grad = (hidden_grad * gelu_slope(first_pre)).astype(bf16)
-    first_term = jnp.dot(first_mix.T, pre_grad, preferred_element_type=f32)
+    first_term_t = lax.dot_general(pre_grad, first_mix, (((0,), (0,)), ((), ())), preferred_element_type=f32)
     second_term = jnp.dot(hidden.astype(f32).T, combined, precision=hp, preferred_element_type=f32)
     node_scale = 1.0 / math.sqrt(node_count * n_rows_axis * n_cols_axis)
-    flat = jnp.concatenate([first_term.reshape(-1), second_term.reshape(-1)]) * node_scale
+    flat = jnp.concatenate([first_term_t, second_term], axis=0) * node_scale
     slices = flat.reshape(row_groups, -1, BLOCK)
 
     packed = jnp.concatenate([jnp.zeros((row_groups, BLOCK, BLOCK), bf16), slices.astype(bf16)], axis=1)
@@ -228,10 +228,10 @@
     part = jnp.sum(arrived[:, BLOCK:], axis=0)
 
     total = jnp.sum(gather_blocks(part.astype(bf16), "row").astype(f32), axis=0)
-    everything = gather_blocks(total.astype(bf16), "col").astype(f32).reshape(-1)
-    split = first_term.size
-    first_grad = everything[:split].reshape(first_term.shape)
-    second_grad = everything[split:].reshape(second_term.shape)
+    everything = gather_blocks(total.astype(bf16), "col").astype(f32).reshape(-1, BLOCK)
+    split = first_term_t.shape[0]
+    first_grad = everything[:split].T
+    second_grad = everything[split:]
     return (output, first_grad, second_grad)
 
 

time: 155 us -> 155 us (level)
  no operation moved by 1% of the time
where the time goes in v9:
time: 155 us; the launch traced here: 154 us
  waiting for transfers between devices  57.6 us (37%)
  blocking collectives  38.8 us (25%)
  starting transfers between devices  28.4 us (18%)
  Pallas kernels  10.4 us (7%)
  local copies, waits for them, and re-layouts  8.9 us (6%)
  matrix products  4.52 us (3%)
  other arithmetic  4.04 us (3%)
  between operations  1.55 us (1%)
    all_to_all x2, waiting for transfers between devices, scatter_blocks(): return lax.all_to_all(blocks, axis, 0, 0, tiled=False)  47.4 us
    all_to_all x1, blocking collectives, scatter_blocks(): return lax.all_to_all(blocks, axis, 0, 0, tiled=False)  29.3 us
    all_to_all x2, starting transfers between devices, scatter_blocks(): return lax.all_to_all(blocks, axis, 0, 0, tiled=False)  14.4 us
    all_to_all x2, starting transfers between devices, gather_blocks(): lax.all_to_all(jnp.broadcast_to(block[None], (n,) + block.shape), axis, 0...  14 us
    pallas_call x3, Pallas kernels, _aggregate_into(): pl.pallas_call(functools.partial(kernel, row_offset, src_offset), out_sha...  10.4 us
    all_to_all x2, waiting for transfers between devices, gather_blocks(): lax.all_to_all(jnp.broadcast_to(block[None], (n,) + block.shape), axis, 0...  10.3 us
    all_to_all x1, blocking collectives, gather_blocks(): lax.all_to_all(jnp.broadcast_to(block[None], (n,) + block.shape), axis, 0...  9.53 us
    dot_general x1, matrix products, local(): jnp.einsum('sij,sj->si', tiles, live_mask, preferred_element_type=f32)  3.17 us
  transfers between devices with their start and end apart: 4, of which 4 were waited for; matrix products, arithmetic and copies ran while one was open for 6% of the time, Pallas kernels for 0%

profile of v9, /device:TPU:1, one launch (start us, length us, event | category | flops | bytes accessed | tf_op | source)
XLA Modules:
  0.0 154.3 jit_solution(13022588623698574088)
XLA Ops:
  0.6 0.0 copy-start
  0.6 0.0 copy-start.6
  0.7 1.5 broadcast_in_dim.12
  2.2 9.0 %all-to-all-start = ((bf16[8,128,128]{2,1,0:T(8,128)(2,1)}), bf16[8,128,128]{2,1,0:T(8,128)(2,1)S(1)}, u32[]{:S(2)}, u32[]{:S(2)}) async-start(bf16[8,128,128]{2,1,0:T(8,128)(2,1)} %broadcast_in_dim.12), calls=%async_computation | async-start | bytes 524288 | tf_op jit(solution)/shard_map/all_to_all | solution.py:139
  11.9 0.9 fusion.10
  12.7 0.7 fusion.13
  13.4 3.2 %fusion.8 = f32[80,1,128]{2,1,0:T(1,128)S(1)} fusion(bf16[80,128,1]{1,0,2:T(8,128)(2,1)S(1)} %fusion.10, bf16[1,1,80,128,128]{4,3,2,1,0:T(8,128)(2,1)} %param.16), kind=kOutput, calls=%fused_computation.23 | convolution fusion | flops 2621440 | bytes 2682880 | tf_op jit(solution)/shard_map/sij,sj->si/dot_general | solution.py:180
  16.6 0.9 scatter_custom_fusion
  17.5 0.1 copy.24
  17.6 0.0 copy-done.6
  17.6 0.1 pad_maximum_fusion
  17.7 0.1 copy.25
  17.8 0.2 broadcast_in_dim.14
  18.0 1.6 %concatenate.16.into_ref = bf16[32,288,128]{2,1,0:T(8,128)(2,1)} pad(bf16[32,160,128]{2,1,0:T(8,128)(2,1)S(1)} %broadcast_in_dim.14, bf16[]{:T(256)} %constant.6.clone.1), padding=0_0x128_0x0_0 | pad | bytes 3670018 | tf_op jit(solution)/shard_map/concatenate | solution.py:183
  19.6 2.1 %all-to-all-done.src_ref = bf16[8,128,128]{2,1,0:T(8,128)(2,1)S(1)} async-done(((bf16[8,128,128]{2,1,0:T(8,128)(2,1)}), bf16[8,128,128]{2,1,0:T(8,128)(2,1)S(1)}, u32[]{:S(2)}, u32[]{:S(2)}) %all-to-all-start) | async-done | bytes 262176 | tf_op jit(solution)/shard_map/all_to_all | solution.py:139
  21.7 0.0 copy-start.3
  21.7 0.7 copy-done.3
  22.4 3.4 %shard_map.112 = bf16[32,288,128]{2,1,0:T(8,128)(2,1)} custom-call(s32[1]{0:T(128)} %bitcast.35.live_ref, s32[80]{0:T(128)} %bitcast.49, s32[80]{0:T(128)} %bitcast.52, bf16[80,128,128]{2,1,0:T(8,128)(2,1)} %bitcast.38, s32[80,128]{1,0:T(8,128)} %bitcast.43, bf16[8,128,128]{2,1,0:T(8,128)(2,1)} %copy-done.3, ...), custom_call_target="tpu_custom_call", output_to_operand_aliasing={{}: (6, {})} | custom-call | flops 335544320 | bytes 3932160 | tf_op jit(solution)/shard_map/pallas_call | solution.py:106
  25.8 0.0 copy-start.5
  25.8 0.0 copy-start.4
  25.8 10.6 %all-to-all-start.1 = ((bf16[32,288,128]{2,1,0:T(8,128)(2,1)}), bf16[32,288,128]{2,1,0:T(8,128)(2,1)S(1)}, u32[]{:S(2)}, u32[]{:S(2)}) async-start(bf16[32,288,128]{2,1,0:T(8,128)(2,1)} %shard_map.112), calls=%async_computation.1 | async-start | bytes 4718592 | tf_op jit(solution)/shard_map/all_to_all | solution.py:143
  36.4 31.5 %all-to-all-done.1.src_ref = bf16[32,288,128]{2,1,0:T(8,128)(2,1)S(1)} async-done(((bf16[32,288,128]{2,1,0:T(8,128)(2,1)}), bf16[32,288,128]{2,1,0:T(8,128)(2,1)S(1)}, u32[]{:S(2)}, u32[]{:S(2)}) %all-to-all-start.1) | async-done | bytes 2359328 | tf_op jit(solution)/shard_map/all_to_all | solution.py:143
  67.9 0.0 copy-start.1
  68.0 0.0 copy-start.7
  68.0 0.2 convert_reduce_fusion
  68.2 0.0 copy-done.5
  68.2 0.1 add_convert_fusion.1
  68.3 0.0 copy-done.4
  68.3 0.2 fusion.18
  68.5 0.0 copy-done
  68.5 0.2 fusion.17
  68.7 0.9 concatenate.17.into_ref
  69.6 0.0 copy-done.1
  69.6 0.0 copy-done.7
  69.6 3.6 %shard_map.113 = bf16[8,256,128]{2,1,0:T(8,128)(2,1)} custom-call(s32[1]{0:T(128)} %bitcast.36.live_ref, s32[80]{0:T(128)} %bitcast.50, s32[80]{0:T(128)} %bitcast.53, bf16[80,128,128]{2,1,0:T(8,128)(2,1)} %bitcast.39, s32[80,128]{1,0:T(8,128)} %bitcast.44, bf16[32,288,128]{2,1,0:T(8,128)(2,1)} %copy-done.1, ...), custom_call_target="tpu_custom_call", output_to_operand_aliasing={{}: (7, {})} | custom-call | flops 335544320 | bytes 3932160 | tf_op jit(solution)/shard_map/pallas_call | solution.py:106
  73.2 3.8 %all-to-all-start.2 = ((bf16[8,256,128]{2,1,0:T(8,128)(2,1)}), bf16[8,256,128]{2,1,0:T(8,128)(2,1)S(1)}, u32[]{:S(2)}, u32[]{:S(2)}) async-start(bf16[8,256,128]{2,1,0:T(8,128)(2,1)} %shard_map.113), calls=%async_computation.2 | async-start | bytes 1048576 | tf_op jit(solution)/shard_map/all_to_all | solution.py:143
  77.1 0.1 copy.26
  77.2 15.9 %all-to-all-done.2.src_ref = bf16[8,256,128]{2,1,0:T(8,128)(2,1)S(1)} async-done(((bf16[8,256,128]{2,1,0:T(8,128)(2,1)}), bf16[8,256,128]{2,1,0:T(8,128)(2,1)S(1)}, u32[]{:S(2)}, u32[]{:S(2)}) %all-to-all-start.2) | async-done | bytes 524320 | tf_op jit(solution)/shard_map/all_to_all | solution.py:143
  93.0 0.0 copy-start.2
  93.1 0.4 fusion
  93.5 0.4 fusion.7
  93.9 0.2 fusion.19
  94.1 1.2 concatenate.19.into_ref
  95.3 0.0 copy-done.2
  95.3 3.4 %shard_map.114 = bf16[32,160,128]{2,1,0:T(8,128)(2,1)} custom-call(s32[1]{0:T(128)} %bitcast.37.live_ref, s32[80]{0:T(128)} %bitcast.51, s32[80]{0:T(128)} %bitcast.54, bf16[80,128,128]{2,1,0:T(8,128)(2,1)} %bitcast.40, s32[80,128]{1,0:T(8,128)} %bitcast.45, bf16[8,256,128]{2,1,0:T(8,128)(2,1)} %copy-done.2, ...), custom_call_target="tpu_custom_call", output_to_operand_aliasing={{}: (6, {})} | custom-call | flops 335544320 | bytes 3932160 | tf_op jit(solution)/shard_map/pallas_call | solution.py:106
  98.8 29.3 %all_to_all.30 = bf16[32,160,128]{2,1,0:T(8,128)(2,1)S(1)} all-to-all(bf16[32,160,128]{2,1,0:T(8,128)(2,1)} %shard_map.114), channel_id=1, replica_groups=mesh['row'=8,'col'=32] {'col'}, dimensions={0} | all-to-all | bytes 2621440 | tf_op jit(solution)/shard_map/all_to_all | solution.py:143
  128.0 0.3 convert_element_type.80
  128.4 9.5 %all_to_all.31 = bf16[8,32,128]{2,1,0:T(8,128)(2,1)S(1)} all-to-all(bf16[8,32,128]{2,1,0:T(8,128)(2,1)S(1)} %broadcast_in_dim.16), channel_id=1, replica_groups=mesh['row'=8,'col'=32] {'row'}, dimensions={0} | all-to-all | bytes 131072 | tf_op jit(solution)/shard_map/all_to_all | solution.py:139
  138.0 0.7 broadcast_in_dim.17
  138.7 5.0 %all-to-all-start.5 = ((bf16[32,32,128]{2,1,0:T(8,128)(2,1)}), bf16[32,32,128]{2,1,0:T(8,128)(2,1)S(1)}, u32[]{:S(2)}, u32[]{:S(2)}) async-start(bf16[32,32,128]{2,1,0:T(8,128)(2,1)} %broadcast_in_dim.17), calls=%async_computation.5 | async-start | bytes 524288 | tf_op jit(solution)/shard_map/all_to_all | solution.py:139
  143.7 0.1 slice_reduce_fusion
  143.8 0.7 add_convert_fusion
  144.5 8.2 %all-to-all-done.5 = bf16[32,32,128]{2,1,0:T(8,128)(2,1)S(1)} async-done(((bf16[32,32,128]{2,1,0:T(8,128)(2,1)}), bf16[32,32,128]{2,1,0:T(8,128)(2,1)S(1)}, u32[]{:S(2)}, u32[]{:S(2)}) %all-to-all-start.5) | async-done | bytes 262176 | tf_op jit(solution)/shard_map/all_to_all | solution.py:139
  152.7 0.8 fusion.16
  153.4 0.8 copy.27
  (11 shorter events, 0.3 us)
Async XLA Ops:
  0.6 67.8 %copy-start = (bf16[512,128]{1,0:T(8,128)(2,1)S(1)}, bf16[512,128]{1,0:T(8,128)(2,1)}, u32[]{:S(2)}) copy-start(bf16[512,128]{1,0:T(8,128)(2,1)} %param.11) | copy-start | bytes 393220
  0.6 16.9 %copy-start.6 = (bf16[128,128]{1,0:T(8,128)(2,1)S(1)}, bf16[128,128]{1,0:T(8,128)(2,1)}, u32[]{:S(2)}) copy-start(bf16[128,128]{1,0:T(8,128)(2,1)} %param.17) | copy-start | bytes 98308
  2.2 19.5 %all-to-all-start = ((bf16[8,128,128]{2,1,0:T(8,128)(2,1)}), bf16[8,128,128]{2,1,0:T(8,128)(2,1)S(1)}, u32[]{:S(2)}, u32[]{:S(2)}) async-start(bf16[8,128,128]{2,1,0:T(8,128)(2,1)} %broadcast_in_dim.12), calls=%async_computation | async-start | bytes 524288 | tf_op jit(solution)/shard_map/all_to_all | solution.py:139
  21.7 0.7 copy-start.3
  25.8 42.4 %copy-start.5 = (bf16[128,128]{1,0:T(8,128)(2,1)S(1)}, bf16[128,128]{1,0:T(8,128)(2,1)}, u32[]{:S(2)}) copy-start(bf16[128,128]{1,0:T(8,128)(2,1)} %param.9) | copy-start | bytes 98308
  25.8 42.5 %copy-start.4 = (bf16[128,512]{1,0:T(8,128)(2,1)S(1)}, bf16[128,512]{1,0:T(8,128)(2,1)}, u32[]{:S(2)}) copy-start(bf16[128,512]{1,0:T(8,128)(2,1)} %param.10) | copy-start | bytes 393220
  25.8 42.1 %all-to-all-start.1 = ((bf16[32,288,128]{2,1,0:T(8,128)(2,1)}), bf16[32,288,128]{2,1,0:T(8,128)(2,1)S(1)}, u32[]{:S(2)}, u32[]{:S(2)}) async-start(bf16[32,288,128]{2,1,0:T(8,128)(2,1)} %shard_map.112), calls=%async_computation.1 | async-start | bytes 4718592 | tf_op jit(solution)/shard_map/all_to_all | solution.py:143
  67.9 1.7 %copy-start.1 = (bf16[32,288,128]{2,1,0:T(8,128)(2,1)}, bf16[32,288,128]{2,1,0:T(8,128)(2,1)S(1)}, u32[]{:S(2)}) copy-start(bf16[32,288,128]{2,1,0:T(8,128)(2,1)S(1)} %all-to-all-done.1.src_ref) | copy-start | bytes 7077892
  68.0 1.6 %copy-start.7 = (f32[32,128]{1,0:T(8,128)}, f32[32,128]{1,0:T(8,128)S(1)}, u32[]{:S(2)}) copy-start(f32[32,128]{1,0:T(8,128)S(1)} %add_rsqrt_fusion.scale_ref) | copy-start | bytes 49156
  73.2 19.8 %all-to-all-start.2 = ((bf16[8,256,128]{2,1,0:T(8,128)(2,1)}), bf16[8,256,128]{2,1,0:T(8,128)(2,1)S(1)}, u32[]{:S(2)}, u32[]{:S(2)}) async-start(bf16[8,256,128]{2,1,0:T(8,128)(2,1)} %shard_map.113), calls=%async_computation.2 | async-start | bytes 1048576 | tf_op jit(solution)/shard_map/all_to_all | solution.py:143
  93.0 2.3 %copy-start.2 = (bf16[8,256,128]{2,1,0:T(8,128)(2,1)}, bf16[8,256,128]{2,1,0:T(8,128)(2,1)S(1)}, u32[]{:S(2)}) copy-start(bf16[8,256,128]{2,1,0:T(8,128)(2,1)S(1)} %all-to-all-done.2.src_ref) | copy-start | bytes 1572868
  138.7 14.0 %all-to-all-start.5 = ((bf16[32,32,128]{2,1,0:T(8,128)(2,1)}), bf16[32,32,128]{2,1,0:T(8,128)(2,1)S(1)}, u32[]{:S(2)}, u32[]{:S(2)}) async-start(bf16[32,32,128]{2,1,0:T(8,128)(2,1)} %broadcast_in_dim.17), calls=%async_computation.5 | async-start | bytes 524288 | tf_op jit(solution)/shard_map/all_to_all | solution.py:139

commit v10 on v8

--- a/solution.py
+++ b/solution.py
@@ -180,14 +180,12 @@
     row_sums = jnp.einsum("sij,sj->si", tiles, live_mask, preferred_element_type=f32)
     partial_deg = jnp.zeros((row_groups, BLOCK), f32).at[jnp.clip(rows, 0, row_groups - 1)].add(row_sums)
     shared = jnp.concatenate([partial_deg.astype(bf16), cotangent.T], axis=0)
-    packed = jnp.concatenate(
-        [jnp.zeros((row_groups, BLOCK, BLOCK), bf16), jnp.broadcast_to(shared[None], (row_groups,) + shared.shape)],
-        axis=1,
-    )
+    arrived_shared = gather_blocks(shared, "col")
+    packed = jnp.zeros((row_groups, BLOCK, BLOCK), bf16)
     packed = forward_aggregate_into(live, rows, cols, tiles, mask, x_panel, 0, packed, 0)
     arrived = scatter_blocks(packed, "col")
-    summed_in = jnp.sum(arrived[:, :BLOCK].astype(f32), axis=0)
-    degrees = jnp.sum(arrived[:, BLOCK : BLOCK + row_groups].astype(f32), axis=0)
+    summed_in = jnp.sum(arrived.astype(f32), axis=0)
+    degrees = jnp.sum(arrived_shared[:, :row_groups].astype(f32), axis=0)
     group_scale = 1.0 / jnp.sqrt(1.0 + degrees)
     me = lax.axis_index("col")
     row_scale = lax.dynamic_index_in_dim(group_scale, me, axis=0, keepdims=False)[:, None]
@@ -205,7 +203,7 @@
         axis=1,
     )
     packed = transpose_aggregate_into(
-        live, rows, cols, tiles, mask, arrived, BLOCK + row_groups, group_scale, packed, BLOCK
+        live, rows, cols, tiles, mask, arrived_shared, row_groups, group_scale, packed, BLOCK
     )
     arrived = scatter_blocks(packed, "row")
     returned_t = jnp.sum(arrived[:, BLOCK:].astype(f32), axis=0)

time: 155 us -> 160 us (1.032)
  waiting for transfers between devices: 57.6 us -> 61.6 us
  starting transfers between devices: 28.4 us -> 32 us
  blocking collectives: 38.8 us -> 36.3 us
    all_to_all x2 -> x3, waiting for transfers between devices: 10.3 us -> 26.8 us  [gather_blocks(): lax.all_to_all(jnp.broadcast_to(block[None], (n,) + block.shape), axis, 0...]
    all_to_all x2, waiting for transfers between devices: 47.4 us -> 34.8 us  [scatter_blocks(): return lax.all_to_all(blocks, axis, 0, 0, tiled=False)]
    all_to_all x2 -> x3, starting transfers between devices: 14 us -> 23.4 us  [gather_blocks(): lax.all_to_all(jnp.broadcast_to(block[None], (n,) + block.shape), axis, 0...]
    all_to_all x2, starting transfers between devices: 14.4 us -> 8.59 us  [scatter_blocks(): return lax.all_to_all(blocks, axis, 0, 0, tiled=False)]
    all_to_all x1, blocking collectives: 29.3 us -> 26.8 us  [scatter_blocks(): return lax.all_to_all(blocks, axis, 0, 0, tiled=False)]
    concatenate x1 -> x0, local copies, waits for them, and re-layouts: 1.63 us -> none  [local(): jnp.concatenate([jnp.zeros((row_groups, BLOCK, BLOCK), bf16), jnp.broadca...]
    broadcast_in_dim x3 -> x4, local copies, waits for them, and re-layouts: 2.29 us -> 3.52 us  [gather_blocks(): jnp.broadcast_to(block[None], (n,) + block.shape)]
  transfers between devices with their start and end apart: 4 -> 5, of which waited for: 4 -> 5; matrix products, arithmetic and copies ran while one was open for 6% -> 5% of each run, Pallas kernels for 0% -> 2%
where the time goes in v10:
time: 160 us; the launch traced here: 159 us
  waiting for transfers between devices  61.6 us (38%)
  blocking collectives  36.3 us (23%)
  starting transfers between devices  32 us (20%)
  Pallas kernels  10 us (6%)
  local copies, waits for them, and re-layouts  8.8 us (6%)
  matrix products  4.51 us (3%)
  other arithmetic  4.06 us (3%)
    all_to_all x2, waiting for transfers between devices, scatter_blocks(): return lax.all_to_all(blocks, axis, 0, 0, tiled=False)  34.8 us
    all_to_all x1, blocking collectives, scatter_blocks(): return lax.all_to_all(blocks, axis, 0, 0, tiled=False)  26.8 us
    all_to_all x3, waiting for transfers between devices, gather_blocks(): lax.all_to_all(jnp.broadcast_to(block[None], (n,) + block.shape), axis, 0...  26.8 us
    all_to_all x3, starting transfers between devices, gather_blocks(): lax.all_to_all(jnp.broadcast_to(block[None], (n,) + block.shape), axis, 0...  23.4 us
    pallas_call x3, Pallas kernels, _aggregate_into(): pl.pallas_call(functools.partial(kernel, row_offset, src_offset), out_sha...  10 us
    all_to_all x1, blocking collectives, gather_blocks(): lax.all_to_all(jnp.broadcast_to(block[None], (n,) + block.shape), axis, 0...  9.53 us
    all_to_all x2, starting transfers between devices, scatter_blocks(): return lax.all_to_all(blocks, axis, 0, 0, tiled=False)  8.59 us
    broadcast_in_dim x4, local copies, waits for them, and re-layouts, gather_blocks(): jnp.broadcast_to(block[None], (n,) + block.shape)  3.52 us
  transfers between devices with their start and end apart: 5, of which 5 were waited for; matrix products, arithmetic and copies ran while one was open for 5% of the time, Pallas kernels for 2%

profile of v10, /device:TPU:1, one launch (start us, length us, event | category | flops | bytes accessed | tf_op | source)
XLA Modules:
  0.0 158.8 jit_solution(17280250641966716912)
XLA Ops:
  0.6 0.0 copy-start
  0.6 0.0 copy-start.6
  0.7 1.5 broadcast_in_dim.14
  2.2 9.0 %all-to-all-start.1 = ((bf16[8,128,128]{2,1,0:T(8,128)(2,1)}), bf16[8,128,128]{2,1,0:T(8,128)(2,1)S(1)}, u32[]{:S(2)}, u32[]{:S(2)}) async-start(bf16[8,128,128]{2,1,0:T(8,128)(2,1)} %broadcast_in_dim.14), calls=%async_computation.1 | async-start | bytes 524288 | tf_op jit(solution)/shard_map/all_to_all | solution.py:139
  11.9 0.9 fusion.10
  12.7 0.7 fusion.13
  13.4 3.2 %fusion.8 = f32[80,1,128]{2,1,0:T(1,128)S(1)} fusion(bf16[80,128,1]{1,0,2:T(8,128)(2,1)S(1)} %fusion.10, bf16[1,1,80,128,128]{4,3,2,1,0:T(8,128)(2,1)} %param.16), kind=kOutput, calls=%fused_computation.23 | convolution fusion | flops 2621440 | bytes 2682880 | tf_op jit(solution)/shard_map/sij,sj->si/dot_general | solution.py:180
  16.6 0.9 scatter_custom_fusion
  17.5 0.1 copy.21
  17.6 0.0 copy-done.6
  17.6 0.1 pad_maximum_fusion
  17.7 0.1 copy.22
  17.8 3.9 %all-to-all-done.1.src_ref = bf16[8,128,128]{2,1,0:T(8,128)(2,1)S(1)} async-done(((bf16[8,128,128]{2,1,0:T(8,128)(2,1)}), bf16[8,128,128]{2,1,0:T(8,128)(2,1)S(1)}, u32[]{:S(2)}, u32[]{:S(2)}) %all-to-all-start.1) | async-done | bytes 262176 | tf_op jit(solution)/shard_map/all_to_all | solution.py:139
  21.7 0.0 copy-start.3
  21.7 1.2 broadcast_in_dim.13
  22.9 9.4 %all-to-all-start = ((bf16[32,160,128]{2,1,0:T(8,128)(2,1)}), bf16[32,160,128]{2,1,0:T(8,128)(2,1)S(1)}, u32[]{:S(2)}, u32[]{:S(2)}) async-start(bf16[32,160,128]{2,1,0:T(8,128)(2,1)} %broadcast_in_dim.13), calls=%async_computation | async-start | bytes 2621440 | tf_op jit(solution)/shard_map/all_to_all | solution.py:139
  32.4 1.2 broadcast_11_into_ref.2.into_ref
  33.6 0.0 copy-done.3
  33.6 3.3 %shard_map.112 = bf16[32,128,128]{2,1,0:T(8,128)(2,1)} custom-call(s32[1]{0:T(128)} %bitcast.32.live_ref, s32[80]{0:T(128)} %bitcast.45, s32[80]{0:T(128)} %bitcast.48, bf16[80,128,128]{2,1,0:T(8,128)(2,1)} %bitcast.35, s32[80,128]{1,0:T(8,128)} %bitcast.38, bf16[8,128,128]{2,1,0:T(8,128)(2,1)} %copy-done.3, ...), custom_call_target="tpu_custom_call", output_to_operand_aliasing={{}: (6, {})} | custom-call | flops 335544320 | bytes 3932160 | tf_op jit(solution)/shard_map/pallas_call | solution.py:106
  36.9 0.0 copy-start.5
  36.9 0.0 copy-start.4
  37.0 14.7 %all-to-all-done.src_ref = bf16[32,160,128]{2,1,0:T(8,128)(2,1)S(1)} async-done(((bf16[32,160,128]{2,1,0:T(8,128)(2,1)}), bf16[32,160,128]{2,1,0:T(8,128)(2,1)S(1)}, u32[]{:S(2)}, u32[]{:S(2)}) %all-to-all-start) | async-done | bytes 1310752 | tf_op jit(solution)/shard_map/all_to_all | solution.py:139
  51.6 0.0 copy-start.1
  51.6 5.1 %all-to-all-start.2 = ((bf16[32,128,128]{2,1,0:T(8,128)(2,1)}), bf16[32,128,128]{2,1,0:T(8,128)(2,1)S(1)}, u32[]{:S(2)}, u32[]{:S(2)}) async-start(bf16[32,128,128]{2,1,0:T(8,128)(2,1)} %shard_map.112), calls=%async_computation.2 | async-start | bytes 2097152 | tf_op jit(solution)/shard_map/all_to_all | solution.py:143
  56.8 0.0 copy-start.7
  56.8 17.1 %all-to-all-done.2 = bf16[32,128,128]{2,1,0:T(8,128)(2,1)S(1)} async-done(((bf16[32,128,128]{2,1,0:T(8,128)(2,1)}), bf16[32,128,128]{2,1,0:T(8,128)(2,1)S(1)}, u32[]{:S(2)}, u32[]{:S(2)}) %all-to-all-start.2) | async-done | bytes 1048608 | tf_op jit(solution)/shard_map/all_to_all | solution.py:143
  73.9 0.2 convert_reduce_fusion
  74.0 0.0 copy-done.5
  74.1 0.1 add_convert_fusion.1
  74.1 0.0 copy-done.4
  74.2 0.2 fusion.18
  74.3 0.0 copy-done
  74.3 0.2 fusion.17
  74.5 0.0 copy-done.1
  74.6 0.9 concatenate.18.into_ref
  75.5 0.0 copy-done.7
  75.5 3.3 %shard_map.113 = bf16[8,256,128]{2,1,0:T(8,128)(2,1)} custom-call(s32[1]{0:T(128)} %bitcast.33.live_ref, s32[80]{0:T(128)} %bitcast.46, s32[80]{0:T(128)} %bitcast.49, bf16[80,128,128]{2,1,0:T(8,128)(2,1)} %bitcast.36, s32[80,128]{1,0:T(8,128)} %bitcast.39, bf16[32,160,128]{2,1,0:T(8,128)(2,1)} %copy-done.1, ...), custom_call_target="tpu_custom_call", output_to_operand_aliasing={{}: (7, {})} | custom-call | flops 335544320 | bytes 3932160 | tf_op jit(solution)/shard_map/pallas_call | solution.py:106
  78.8 3.5 %all-to-all-start.3 = ((bf16[8,256,128]{2,1,0:T(8,128)(2,1)}), bf16[8,256,128]{2,1,0:T(8,128)(2,1)S(1)}, u32[]{:S(2)}, u32[]{:S(2)}) async-start(bf16[8,256,128]{2,1,0:T(8,128)(2,1)} %shard_map.113), calls=%async_computation.3 | async-start | bytes 1048576 | tf_op jit(solution)/shard_map/all_to_all | solution.py:143
  82.3 0.1 copy.23
  82.4 17.8 %all-to-all-done.3.src_ref = bf16[8,256,128]{2,1,0:T(8,128)(2,1)S(1)} async-done(((bf16[8,256,128]{2,1,0:T(8,128)(2,1)}), bf16[8,256,128]{2,1,0:T(8,128)(2,1)S(1)}, u32[]{:S(2)}, u32[]{:S(2)}) %all-to-all-start.3) | async-done | bytes 524320 | tf_op jit(solution)/shard_map/all_to_all | solution.py:143
  100.1 0.0 copy-start.2
  100.2 0.4 fusion
  100.6 0.4 fusion.7
  101.0 0.2 fusion.19
  101.2 0.1 fusion.1
  101.3 0.0 copy-done.2
  101.3 1.2 concatenate.22.into_ref
  102.5 3.4 %shard_map.114 = bf16[32,160,128]{2,1,0:T(8,128)(2,1)} custom-call(s32[1]{0:T(128)} %bitcast.34.live_ref, s32[80]{0:T(128)} %bitcast.47, s32[80]{0:T(128)} %bitcast.50, bf16[80,128,128]{2,1,0:T(8,128)(2,1)} %bitcast.37, s32[80,128]{1,0:T(8,128)} %bitcast.40, bf16[8,256,128]{2,1,0:T(8,128)(2,1)} %copy-done.2, ...), custom_call_target="tpu_custom_call", output_to_operand_aliasing={{}: (6, {})} | custom-call | flops 335544320 | bytes 3932160 | tf_op jit(solution)/shard_map/pallas_call | solution.py:106
  105.9 26.8 %all_to_all.35 = bf16[32,160,128]{2,1,0:T(8,128)(2,1)S(1)} all-to-all(bf16[32,160,128]{2,1,0:T(8,128)(2,1)} %shard_map.114), channel_id=1, replica_groups=mesh['row'=8,'col'=32] {'col'}, dimensions={0} | all-to-all | bytes 2621440 | tf_op jit(solution)/shard_map/all_to_all | solution.py:143
  132.7 0.3 convert_element_type.76
  133.0 9.5 %all_to_all.36 = bf16[8,32,128]{2,1,0:T(8,128)(2,1)S(1)} all-to-all(bf16[8,32,128]{2,1,0:T(8,128)(2,1)S(1)} %broadcast_in_dim.16), channel_id=1, replica_groups=mesh['row'=8,'col'=32] {'row'}, dimensions={0} | all-to-all | bytes 131072 | tf_op jit(solution)/shard_map/all_to_all | solution.py:139
  142.6 0.7 broadcast_in_dim.17
  143.3 5.0 %all-to-all-start.6 = ((bf16[32,32,128]{2,1,0:T(8,128)(2,1)}), bf16[32,32,128]{2,1,0:T(8,128)(2,1)S(1)}, u32[]{:S(2)}, u32[]{:S(2)}) async-start(bf16[32,32,128]{2,1,0:T(8,128)(2,1)} %broadcast_in_dim.17), calls=%async_computation.6 | async-start | bytes 524288 | tf_op jit(solution)/shard_map/all_to_all | solution.py:139
  148.3 0.1 slice_reduce_fusion
  148.4 0.7 add_convert_fusion
  149.1 8.2 %all-to-all-done.6 = bf16[32,32,128]{2,1,0:T(8,128)(2,1)S(1)} async-done(((bf16[32,32,128]{2,1,0:T(8,128)(2,1)}), bf16[32,32,128]{2,1,0:T(8,128)(2,1)S(1)}, u32[]{:S(2)}, u32[]{:S(2)}) %all-to-all-start.6) | async-done | bytes 262176 | tf_op jit(solution)/shard_map/all_to_all | solution.py:139
  157.3 0.8 fusion.16
  158.1 0.7 reshape.68
  (11 shorter events, 0.2 us)
Async XLA Ops:
  0.6 73.7 %copy-start = (bf16[512,128]{1,0:T(8,128)(2,1)S(1)}, bf16[512,128]{1,0:T(8,128)(2,1)}, u32[]{:S(2)}) copy-start(bf16[512,128]{1,0:T(8,128)(2,1)} %param.11) | copy-start | bytes 393220
  0.6 16.9 %copy-start.6 = (bf16[128,128]{1,0:T(8,128)(2,1)S(1)}, bf16[128,128]{1,0:T(8,128)(2,1)}, u32[]{:S(2)}) copy-start(bf16[128,128]{1,0:T(8,128)(2,1)} %param.17) | copy-start | bytes 98308
  2.2 19.5 %all-to-all-start.1 = ((bf16[8,128,128]{2,1,0:T(8,128)(2,1)}), bf16[8,128,128]{2,1,0:T(8,128)(2,1)S(1)}, u32[]{:S(2)}, u32[]{:S(2)}) async-start(bf16[8,128,128]{2,1,0:T(8,128)(2,1)} %broadcast_in_dim.14), calls=%async_computation.1 | async-start | bytes 524288 | tf_op jit(solution)/shard_map/all_to_all | solution.py:139
  21.7 11.9 %copy-start.3 = (bf16[8,128,128]{2,1,0:T(8,128)(2,1)}, bf16[8,128,128]{2,1,0:T(8,128)(2,1)S(1)}, u32[]{:S(2)}) copy-start(bf16[8,128,128]{2,1,0:T(8,128)(2,1)S(1)} %all-to-all-done.1.src_ref) | copy-start | bytes 786436
  22.9 28.7 %all-to-all-start = ((bf16[32,160,128]{2,1,0:T(8,128)(2,1)}), bf16[32,160,128]{2,1,0:T(8,128)(2,1)S(1)}, u32[]{:S(2)}, u32[]{:S(2)}) async-start(bf16[32,160,128]{2,1,0:T(8,128)(2,1)} %broadcast_in_dim.13), calls=%async_computation | async-start | bytes 2621440 | tf_op jit(solution)/shard_map/all_to_all | solution.py:139
  36.9 37.1 %copy-start.5 = (bf16[128,128]{1,0:T(8,128)(2,1)S(1)}, bf16[128,128]{1,0:T(8,128)(2,1)}, u32[]{:S(2)}) copy-start(bf16[128,128]{1,0:T(8,128)(2,1)} %param.9) | copy-start | bytes 98308
  36.9 37.2 %copy-start.4 = (bf16[128,512]{1,0:T(8,128)(2,1)S(1)}, bf16[128,512]{1,0:T(8,128)(2,1)}, u32[]{:S(2)}) copy-start(bf16[128,512]{1,0:T(8,128)(2,1)} %param.10) | copy-start | bytes 393220
  51.6 22.9 %copy-start.1 = (bf16[32,160,128]{2,1,0:T(8,128)(2,1)}, bf16[32,160,128]{2,1,0:T(8,128)(2,1)S(1)}, u32[]{:S(2)}) copy-start(bf16[32,160,128]{2,1,0:T(8,128)(2,1)S(1)} %all-to-all-done.src_ref) | copy-start | bytes 3932164
  51.6 22.3 %all-to-all-start.2 = ((bf16[32,128,128]{2,1,0:T(8,128)(2,1)}), bf16[32,128,128]{2,1,0:T(8,128)(2,1)S(1)}, u32[]{:S(2)}, u32[]{:S(2)}) async-start(bf16[32,128,128]{2,1,0:T(8,128)(2,1)} %shard_map.112), calls=%async_computation.2 | async-start | bytes 2097152 | tf_op jit(solution)/shard_map/all_to_all | solution.py:143
  56.8 18.7 %copy-start.7 = (f32[32,128]{1,0:T(8,128)}, f32[32,128]{1,0:T(8,128)S(1)}, u32[]{:S(2)}) copy-start(f32[32,128]{1,0:T(8,128)S(1)} %add_rsqrt_fusion.scale_ref) | copy-start | bytes 49156
  78.8 21.4 %all-to-all-start.3 = ((bf16[8,256,128]{2,1,0:T(8,128)(2,1)}), bf16[8,256,128]{2,1,0:T(8,128)(2,1)S(1)}, u32[]{:S(2)}, u32[]{:S(2)}) async-start(bf16[8,256,128]{2,1,0:T(8,128)(2,1)} %shard_map.113), calls=%async_computation.3 | async-start | bytes 1048576 | tf_op jit(solution)/shard_map/all_to_all | solution.py:143
  100.1 1.1 copy-start.2
  143.3 14.0 %all-to-all-start.6 = ((bf16[32,32,128]{2,1,0:T(8,128)(2,1)}), bf16[32,32,128]{2,1,0:T(8,128)(2,1)S(1)}, u32[]{:S(2)}, u32[]{:S(2)}) async-start(bf16[32,32,128]{2,1,0:T(8,128)(2,1)} %broadcast_in_dim.17), calls=%async_computation.6 | async-start | bytes 524288 | tf_op jit(solution)/shard_map/all_to_all | solution.py:139

commit v11 on v8

--- a/solution.py
+++ b/solution.py
@@ -38,9 +38,13 @@
     return (tiles_ref[s].astype(jnp.float32) * column).astype(jnp.bfloat16)
 
 
-def _forward_kernel(row_offset, src_offset, live_ref, rows_ref, cols_ref, tiles_ref, mask_ref, src_ref, into_ref,
-                    out_ref, acc_ref, stage_ref, sem):
+def _forward_kernel(row_offset, src_offset, extra_offset, live_ref, rows_ref, cols_ref, tiles_ref, mask_ref, src_ref,
+                    extra_ref, into_ref, out_ref, acc_ref, stage_ref, sem, extra_sem):
     del into_ref
+    extra_copy = pltpu.make_async_copy(
+        extra_ref, out_ref.at[:, pl.ds(extra_offset, extra_ref.shape[1]), :], extra_sem
+    )
+    extra_copy.start()
     slots = tiles_ref.shape[0]
     n_dst = acc_ref.shape[0]
     n_src = src_ref.shape[0]
@@ -62,11 +66,16 @@
     copy = pltpu.make_async_copy(stage_ref, out_ref.at[:, pl.ds(row_offset, BLOCK), :], sem)
     copy.start()
     copy.wait()
-
-
-def _transpose_kernel(row_offset, src_offset, live_ref, rows_ref, cols_ref, tiles_ref, mask_ref, src_ref, scale_ref,
-                      into_ref, out_ref, acc_ref, stage_ref, sem):
+    extra_copy.wait()
+
+
+def _transpose_kernel(row_offset, src_offset, extra_offset, live_ref, rows_ref, cols_ref, tiles_ref, mask_ref,
+                      src_ref, scale_ref, extra_ref, into_ref, out_ref, acc_ref, stage_ref, sem, extra_sem):
     del into_ref
+    extra_copy = pltpu.make_async_copy(
+        extra_ref, out_ref.at[:, pl.ds(extra_offset, extra_ref.shape[1]), :], extra_sem
+    )
+    extra_copy.start()
     slots = tiles_ref.shape[0]
     n_dst = acc_ref.shape[0]
     n_src = src_ref.shape[0]
@@ -90,6 +99,7 @@
     copy = pltpu.make_async_copy(stage_ref, out_ref.at[:, pl.ds(row_offset, BLOCK), :], sem)
     copy.start()
     copy.wait()
+    extra_copy.wait()
 
 
 _SMEM = pl.BlockSpec(memory_space=pltpu.SMEM)
@@ -97,14 +107,14 @@
 _ANY = pl.BlockSpec(memory_space=pl.ANY)
 
 
-def _aggregate_into(kernel, operands, n_vmem, into, row_offset, src_offset, tiles, src_bytes):
+def _aggregate_into(kernel, operands, n_vmem, into, row_offset, src_offset, extra_offset, tiles, src_bytes):
     n_dst = into.shape[0]
     width = into.shape[2]
     slots = tiles.shape[0]
     flops = 2 * slots * BLOCK * BLOCK * width
     bytes_accessed = tiles.size * 2 + src_bytes + n_dst * BLOCK * width * 2
     return pl.pallas_call(
-        functools.partial(kernel, row_offset, src_offset),
+        functools.partial(kernel, row_offset, src_offset, extra_offset),
         out_shape=jax.ShapeDtypeStruct(into.shape, into.dtype),
         in_specs=[_SMEM, _SMEM, _SMEM] + [_VMEM] * n_vmem + [_ANY],
         out_specs=_ANY,
@@ -112,25 +122,27 @@
             pltpu.VMEM((n_dst, BLOCK, width), jnp.float32),
             pltpu.VMEM((n_dst, BLOCK, width), into.dtype),
             pltpu.SemaphoreType.DMA(()),
+            pltpu.SemaphoreType.DMA(()),
         ],
         input_output_aliases={3 + n_vmem: 0},
         cost_estimate=pl.CostEstimate(flops=flops, bytes_accessed=bytes_accessed, transcendentals=0),
     )(*operands, into)
 
 
-def forward_aggregate_into(live, rows, cols, tiles, mask, src, src_offset, into, row_offset):
+def forward_aggregate_into(live, rows, cols, tiles, mask, src, src_offset, extra, extra_offset, into, row_offset):
     n_src = src.shape[0]
     return _aggregate_into(
-        _forward_kernel, (live, rows, cols, tiles, mask, src), 3, into, row_offset, src_offset, tiles,
-        n_src * BLOCK * BLOCK * 2,
-    )
-
-
-def transpose_aggregate_into(live, rows, cols, tiles, mask, src_t, src_offset, scale, into, row_offset):
+        _forward_kernel, (live, rows, cols, tiles, mask, src, extra), 4, into, row_offset, src_offset,
+        extra_offset, tiles, n_src * BLOCK * BLOCK * 2,
+    )
+
+
+def transpose_aggregate_into(live, rows, cols, tiles, mask, src_t, src_offset, scale, extra, extra_offset, into,
+                             row_offset):
     n_src = src_t.shape[0]
     return _aggregate_into(
-        _transpose_kernel, (live, rows, cols, tiles, mask, src_t, scale), 4, into, row_offset, src_offset, tiles,
-        n_src * BLOCK * BLOCK * 2,
+        _transpose_kernel, (live, rows, cols, tiles, mask, src_t, scale, extra), 5, into, row_offset, src_offset,
+        extra_offset, tiles, n_src * BLOCK * BLOCK * 2,
     )
 
 
@@ -180,11 +192,11 @@
     row_sums = jnp.einsum("sij,sj->si", tiles, live_mask, preferred_element_type=f32)
     partial_deg = jnp.zeros((row_groups, BLOCK), f32).at[jnp.clip(rows, 0, row_groups - 1)].add(row_sums)
     shared = jnp.concatenate([partial_deg.astype(bf16), cotangent.T], axis=0)
-    packed = jnp.concatenate(
-        [jnp.zeros((row_groups, BLOCK, BLOCK), bf16), jnp.broadcast_to(shared[None], (row_groups,) + shared.shape)],
-        axis=1,
-    )
-    packed = forward_aggregate_into(live, rows, cols, tiles, mask, x_panel, 0, packed, 0)
+    packed = jnp.zeros((row_groups, BLOCK + shared.shape[0], BLOCK), bf16)
+    packed = forward_aggregate_into(
+        live, rows, cols, tiles, mask, x_panel, 0,
+        jnp.broadcast_to(shared[None], (row_groups,) + shared.shape), BLOCK, packed, 0,
+    )
     arrived = scatter_blocks(packed, "col")
     summed_in = jnp.sum(arrived[:, :BLOCK].astype(f32), axis=0)
     degrees = jnp.sum(arrived[:, BLOCK : BLOCK + row_groups].astype(f32), axis=0)
@@ -197,15 +209,10 @@
     hidden = gelu_tanh(first_pre).astype(bf16)
     projected = jnp.dot(hidden, second_weight, preferred_element_type=f32)
 
-    packed = jnp.concatenate(
-        [
-            jnp.broadcast_to(projected.astype(bf16)[None], (col_groups, BLOCK, BLOCK)),
-            jnp.zeros((col_groups, BLOCK, BLOCK), bf16),
-        ],
-        axis=1,
-    )
+    packed = jnp.zeros((col_groups, 2 * BLOCK, BLOCK), bf16)
     packed = transpose_aggregate_into(
-        live, rows, cols, tiles, mask, arrived, BLOCK + row_groups, group_scale, packed, BLOCK
+        live, rows, cols, tiles, mask, arrived, BLOCK + row_groups, group_scale,
+        jnp.broadcast_to(projected.astype(bf16)[None], (col_groups, BLOCK, BLOCK)), 0, packed, BLOCK,
     )
     arrived = scatter_blocks(packed, "row")
     returned_t = jnp.sum(arrived[:, BLOCK:].astype(f32), axis=0)
@@ -220,8 +227,8 @@
     flat = jnp.concatenate([first_term.reshape(-1), second_term.reshape(-1)]) * node_scale
     slices = flat.reshape(row_groups, -1, BLOCK)
 
-    packed = jnp.concatenate([jnp.zeros((row_groups, BLOCK, BLOCK), bf16), slices.astype(bf16)], axis=1)
-    packed = forward_aggregate_into(live, rows, cols, tiles, mask, arrived, 0, packed, 0)
+    packed = jnp.zeros((row_groups, BLOCK + slices.shape[1], BLOCK), bf16)
+    packed = forward_aggregate_into(live, rows, cols, tiles, mask, arrived, 0, slices.astype(bf16), BLOCK, packed, 0)
     arrived = scatter_blocks(packed, "col").astype(f32)
     summed_y = jnp.sum(arrived[:, :BLOCK], axis=0)
     output = (projected + row_scale * summed_y).astype(bf16)

time: 155 us -> 159 us (1.026)
  waiting for transfers between devices: 57.6 us -> 59.3 us
    broadcast_in_dim x0 -> x3, local copies, waits for them, and re-layouts: none -> 3.82 us  [the longest x1 1.72 us: local(): packed = jnp.zeros((row_groups, BLOCK + shared.shape[0], BLOCK), bf16)]
    concatenate x3 -> x0, local copies, waits for them, and re-layouts: 3.72 us -> none  [the longest x1 1.63 us: local(): jnp.concatenate([jnp.zeros((row_groups, BLOCK, BLOCK), bf16), jnp.broadca...]
    all_to_all x2, waiting for transfers between devices: 10.3 us -> 12.1 us  [gather_blocks(): lax.all_to_all(jnp.broadcast_to(block[None], (n,) + block.shape), axis, 0...]
  transfers between devices with their start and end apart: 4 -> 4, of which waited for: 4 -> 4; matrix products, arithmetic and copies ran while one was open for 6% -> 4% of each run, Pallas kernels for 0% -> 0%
where the time goes in v11:
time: 159 us; the launch traced here: 158 us
  waiting for transfers between devices  59.3 us (37%)
  blocking collectives  38.8 us (24%)
  starting transfers between devices  28.1 us (18%)
  Pallas kernels  11 us (7%)
  local copies, waits for them, and re-layouts  10 us (6%)
  other arithmetic  4.76 us (3%)
  matrix products  4.51 us (3%)
    all_to_all x2, waiting for transfers between devices, scatter_blocks(): return lax.all_to_all(blocks, axis, 0, 0, tiled=False)  47.3 us
    all_to_all x1, blocking collectives, scatter_blocks(): return lax.all_to_all(blocks, axis, 0, 0, tiled=False)  29.3 us
    all_to_all x2, starting transfers between devices, scatter_blocks(): return lax.all_to_all(blocks, axis, 0, 0, tiled=False)  14.1 us
    all_to_all x2, starting transfers between devices, gather_blocks(): lax.all_to_all(jnp.broadcast_to(block[None], (n,) + block.shape), axis, 0...  14 us
    all_to_all x2, waiting for transfers between devices, gather_blocks(): lax.all_to_all(jnp.broadcast_to(block[None], (n,) + block.shape), axis, 0...  12.1 us
    pallas_call x3, Pallas kernels, _aggregate_into(): pl.pallas_call(functools.partial(kernel, row_offset, src_offset, extra_of...  11 us
    all_to_all x1, blocking collectives, gather_blocks(): lax.all_to_all(jnp.broadcast_to(block[None], (n,) + block.shape), axis, 0...  9.53 us
  transfers between devices with their start and end apart: 4, of which 4 were waited for; matrix products, arithmetic and copies ran while one was open for 4% of the time, Pallas kernels for 0%

profile of v11, /device:TPU:1, one launch (start us, length us, event | category | flops | bytes accessed | tf_op | source)
XLA Modules:
  0.0 158.0 jit_solution(16455642719680968644)
XLA Ops:
  0.6 0.0 copy-start
  0.6 0.0 copy-start.6
  0.7 1.5 broadcast_in_dim.18
  2.2 9.0 %all-to-all-start = ((bf16[8,128,128]{2,1,0:T(8,128)(2,1)}), bf16[8,128,128]{2,1,0:T(8,128)(2,1)S(1)}, u32[]{:S(2)}, u32[]{:S(2)}) async-start(bf16[8,128,128]{2,1,0:T(8,128)(2,1)} %broadcast_in_dim.18), calls=%async_computation | async-start | bytes 524288 | tf_op jit(solution)/shard_map/all_to_all | solution.py:151
  11.9 0.9 fusion.10
  12.7 0.7 fusion.13
  13.4 3.2 %fusion.8 = f32[80,1,128]{2,1,0:T(1,128)S(1)} fusion(bf16[80,128,1]{1,0,2:T(8,128)(2,1)S(1)} %fusion.10, bf16[1,1,80,128,128]{4,3,2,1,0:T(8,128)(2,1)} %param.16), kind=kOutput, calls=%fused_computation.23 | convolution fusion | flops 2621440 | bytes 2682880 | tf_op jit(solution)/shard_map/sij,sj->si/dot_general | solution.py:192
  16.6 0.9 scatter_custom_fusion
  17.5 0.1 copy.21
  17.6 0.0 copy-done.6
  17.6 0.1 pad_maximum_fusion
  17.7 0.1 copy.22
  17.8 3.9 %all-to-all-done.src_ref = bf16[8,128,128]{2,1,0:T(8,128)(2,1)S(1)} async-done(((bf16[8,128,128]{2,1,0:T(8,128)(2,1)}), bf16[8,128,128]{2,1,0:T(8,128)(2,1)S(1)}, u32[]{:S(2)}, u32[]{:S(2)}) %all-to-all-start) | async-done | bytes 262176 | tf_op jit(solution)/shard_map/all_to_all | solution.py:151
  21.7 0.0 copy-start.3
  21.7 1.2 broadcast_in_dim.20.extra_ref
  22.9 1.7 %broadcast_in_dim.21.into_ref = bf16[32,288,128]{2,1,0:T(8,128)(2,1)} broadcast(bf16[]{:T(256)} %constant.20.clone.1), dimensions={} | broadcast | bytes 2359298 | tf_op jit(solution)/shard_map/broadcast_in_dim | solution.py:195
  24.7 0.0 copy-done.3
  24.7 3.8 %shard_map.112 = bf16[32,288,128]{2,1,0:T(8,128)(2,1)} custom-call(s32[1]{0:T(128)} %bitcast.32.live_ref, s32[80]{0:T(128)} %bitcast.45, s32[80]{0:T(128)} %bitcast.48, bf16[80,128,128]{2,1,0:T(8,128)(2,1)} %bitcast.35, s32[80,128]{1,0:T(8,128)} %bitcast.38, bf16[8,128,128]{2,1,0:T(8,128)(2,1)} %copy-done.3, ...), custom_call_target="tpu_custom_call", output_to_operand_aliasing={{}: (7, {})} | custom-call | flops 335544320 | bytes 3932160 | tf_op jit(solution)/shard_map/pallas_call | solution.py:116
  28.5 0.0 copy-start.5
  28.5 0.0 copy-start.4
  28.5 10.6 %all-to-all-start.1 = ((bf16[32,288,128]{2,1,0:T(8,128)(2,1)}), bf16[32,288,128]{2,1,0:T(8,128)(2,1)S(1)}, u32[]{:S(2)}, u32[]{:S(2)}) async-start(bf16[32,288,128]{2,1,0:T(8,128)(2,1)} %shard_map.112), calls=%async_computation.1 | async-start | bytes 4718592 | tf_op jit(solution)/shard_map/all_to_all | solution.py:155
  39.1 31.5 %all-to-all-done.1.src_ref = bf16[32,288,128]{2,1,0:T(8,128)(2,1)S(1)} async-done(((bf16[32,288,128]{2,1,0:T(8,128)(2,1)}), bf16[32,288,128]{2,1,0:T(8,128)(2,1)S(1)}, u32[]{:S(2)}, u32[]{:S(2)}) %all-to-all-start.1) | async-done | bytes 2359328 | tf_op jit(solution)/shard_map/all_to_all | solution.py:155
  70.6 0.0 copy-start.1
  70.7 0.0 copy-start.7
  70.7 0.2 convert_reduce_fusion
  70.9 0.0 copy-done.5
  70.9 0.1 add_convert_fusion.1
  71.0 0.0 copy-done.4
  71.0 0.2 fusion.18
  71.2 0.0 copy-done
  71.2 0.2 fusion.17
  71.4 0.7 broadcast_in_dim.22.extra_ref
  72.1 0.9 broadcast_in_dim.23.into_ref
  73.0 0.0 copy-done.1
  73.0 0.0 copy-done.7
  73.0 3.6 %shard_map.113 = bf16[8,256,128]{2,1,0:T(8,128)(2,1)} custom-call(s32[1]{0:T(128)} %bitcast.33.live_ref, s32[80]{0:T(128)} %bitcast.46, s32[80]{0:T(128)} %bitcast.49, bf16[80,128,128]{2,1,0:T(8,128)(2,1)} %bitcast.36, s32[80,128]{1,0:T(8,128)} %bitcast.39, bf16[32,288,128]{2,1,0:T(8,128)(2,1)} %copy-done.1, ...), custom_call_target="tpu_custom_call", output_to_operand_aliasing={{}: (8, {})} | custom-call | flops 335544320 | bytes 3932160 | tf_op jit(solution)/shard_map/pallas_call | solution.py:116
  76.7 3.5 %all-to-all-start.2 = ((bf16[8,256,128]{2,1,0:T(8,128)(2,1)}), bf16[8,256,128]{2,1,0:T(8,128)(2,1)S(1)}, u32[]{:S(2)}, u32[]{:S(2)}) async-start(bf16[8,256,128]{2,1,0:T(8,128)(2,1)} %shard_map.113), calls=%async_computation.2 | async-start | bytes 1048576 | tf_op jit(solution)/shard_map/all_to_all | solution.py:155
  80.2 0.1 copy.23
  80.3 15.8 %all-to-all-done.2.src_ref = bf16[8,256,128]{2,1,0:T(8,128)(2,1)S(1)} async-done(((bf16[8,256,128]{2,1,0:T(8,128)(2,1)}), bf16[8,256,128]{2,1,0:T(8,128)(2,1)S(1)}, u32[]{:S(2)}, u32[]{:S(2)}) %all-to-all-start.2) | async-done | bytes 524320 | tf_op jit(solution)/shard_map/all_to_all | solution.py:155
  96.1 0.0 copy-start.2
  96.1 0.4 fusion
  96.5 0.4 fusion.7
  96.9 0.2 fusion.19
  97.1 0.8 fusion.1.extra_ref
  97.9 1.2 broadcast_in_dim.24.into_ref
  99.1 0.0 copy-done.2
  99.1 3.5 %shard_map.114 = bf16[32,160,128]{2,1,0:T(8,128)(2,1)} custom-call(s32[1]{0:T(128)} %bitcast.34.live_ref, s32[80]{0:T(128)} %bitcast.47, s32[80]{0:T(128)} %bitcast.50, bf16[80,128,128]{2,1,0:T(8,128)(2,1)} %bitcast.37, s32[80,128]{1,0:T(8,128)} %bitcast.40, bf16[8,256,128]{2,1,0:T(8,128)(2,1)} %copy-done.2, ...), custom_call_target="tpu_custom_call", output_to_operand_aliasing={{}: (7, {})} | custom-call | flops 335544320 | bytes 3932160 | tf_op jit(solution)/shard_map/pallas_call | solution.py:116
  102.6 29.3 %all_to_all.30 = bf16[32,160,128]{2,1,0:T(8,128)(2,1)S(1)} all-to-all(bf16[32,160,128]{2,1,0:T(8,128)(2,1)} %shard_map.114), channel_id=1, replica_groups=mesh['row'=8,'col'=32] {'col'}, dimensions={0} | all-to-all | bytes 2621440 | tf_op jit(solution)/shard_map/all_to_all | solution.py:155
  131.9 0.3 convert_element_type.76
  132.3 9.5 %all_to_all.31 = bf16[8,32,128]{2,1,0:T(8,128)(2,1)S(1)} all-to-all(bf16[8,32,128]{2,1,0:T(8,128)(2,1)S(1)} %broadcast_in_dim.25), channel_id=1, replica_groups=mesh['row'=8,'col'=32] {'row'}, dimensions={0} | all-to-all | bytes 131072 | tf_op jit(solution)/shard_map/all_to_all | solution.py:151
  141.8 0.7 broadcast_in_dim.26
  142.5 5.0 %all-to-all-start.5 = ((bf16[32,32,128]{2,1,0:T(8,128)(2,1)}), bf16[32,32,128]{2,1,0:T(8,128)(2,1)S(1)}, u32[]{:S(2)}, u32[]{:S(2)}) async-start(bf16[32,32,128]{2,1,0:T(8,128)(2,1)} %broadcast_in_dim.26), calls=%async_computation.5 | async-start | bytes 524288 | tf_op jit(solution)/shard_map/all_to_all | solution.py:151
  147.5 0.1 slice_reduce_fusion
  147.7 0.7 add_convert_fusion
  148.4 8.2 %all-to-all-done.5 = bf16[32,32,128]{2,1,0:T(8,128)(2,1)S(1)} async-done(((bf16[32,32,128]{2,1,0:T(8,128)(2,1)}), bf16[32,32,128]{2,1,0:T(8,128)(2,1)S(1)}, u32[]{:S(2)}, u32[]{:S(2)}) %all-to-all-start.5) | async-done | bytes 262176 | tf_op jit(solution)/shard_map/all_to_all | solution.py:151
  156.5 0.8 fusion.16
  157.3 0.7 reshape.68
  (10 shorter events, 0.2 us)
Async XLA Ops:
  0.6 70.5 %copy-start = (bf16[512,128]{1,0:T(8,128)(2,1)S(1)}, bf16[512,128]{1,0:T(8,128)(2,1)}, u32[]{:S(2)}) copy-start(bf16[512,128]{1,0:T(8,128)(2,1)} %param.11) | copy-start | bytes 393220
  0.6 16.9 %copy-start.6 = (bf16[128,128]{1,0:T(8,128)(2,1)S(1)}, bf16[128,128]{1,0:T(8,128)(2,1)}, u32[]{:S(2)}) copy-start(bf16[128,128]{1,0:T(8,128)(2,1)} %param.17) | copy-start | bytes 98308
  2.2 19.5 %all-to-all-start = ((bf16[8,128,128]{2,1,0:T(8,128)(2,1)}), bf16[8,128,128]{2,1,0:T(8,128)(2,1)S(1)}, u32[]{:S(2)}, u32[]{:S(2)}) async-start(bf16[8,128,128]{2,1,0:T(8,128)(2,1)} %broadcast_in_dim.18), calls=%async_computation | async-start | bytes 524288 | tf_op jit(solution)/shard_map/all_to_all | solution.py:151
  21.7 3.0 %copy-start.3 = (bf16[8,128,128]{2,1,0:T(8,128)(2,1)}, bf16[8,128,128]{2,1,0:T(8,128)(2,1)S(1)}, u32[]{:S(2)}) copy-start(bf16[8,128,128]{2,1,0:T(8,128)(2,1)S(1)} %all-to-all-done.src_ref) | copy-start | bytes 786436
  28.5 42.4 %copy-start.5 = (bf16[128,128]{1,0:T(8,128)(2,1)S(1)}, bf16[128,128]{1,0:T(8,128)(2,1)}, u32[]{:S(2)}) copy-start(bf16[128,128]{1,0:T(8,128)(2,1)} %param.9) | copy-start | bytes 98308
  28.5 42.5 %copy-start.4 = (bf16[128,512]{1,0:T(8,128)(2,1)S(1)}, bf16[128,512]{1,0:T(8,128)(2,1)}, u32[]{:S(2)}) copy-start(bf16[128,512]{1,0:T(8,128)(2,1)} %param.10) | copy-start | bytes 393220
  28.5 42.1 %all-to-all-start.1 = ((bf16[32,288,128]{2,1,0:T(8,128)(2,1)}), bf16[32,288,128]{2,1,0:T(8,128)(2,1)S(1)}, u32[]{:S(2)}, u32[]{:S(2)}) async-start(bf16[32,288,128]{2,1,0:T(8,128)(2,1)} %shard_map.112), calls=%async_computation.1 | async-start | bytes 4718592 | tf_op jit(solution)/shard_map/all_to_all | solution.py:155
  70.6 2.4 %copy-start.1 = (bf16[32,288,128]{2,1,0:T(8,128)(2,1)}, bf16[32,288,128]{2,1,0:T(8,128)(2,1)S(1)}, u32[]{:S(2)}) copy-start(bf16[32,288,128]{2,1,0:T(8,128)(2,1)S(1)} %all-to-all-done.1.src_ref) | copy-start | bytes 7077892
  70.7 2.3 %copy-start.7 = (f32[32,128]{1,0:T(8,128)}, f32[32,128]{1,0:T(8,128)S(1)}, u32[]{:S(2)}) copy-start(f32[32,128]{1,0:T(8,128)S(1)} %add_rsqrt_fusion.scale_ref) | copy-start | bytes 49156
  76.7 19.4 %all-to-all-start.2 = ((bf16[8,256,128]{2,1,0:T(8,128)(2,1)}), bf16[8,256,128]{2,1,0:T(8,128)(2,1)S(1)}, u32[]{:S(2)}, u32[]{:S(2)}) async-start(bf16[8,256,128]{2,1,0:T(8,128)(2,1)} %shard_map.113), calls=%async_computation.2 | async-start | bytes 1048576 | tf_op jit(solution)/shard_map/all_to_all | solution.py:155
  96.1 3.1 %copy-start.2 = (bf16[8,256,128]{2,1,0:T(8,128)(2,1)}, bf16[8,256,128]{2,1,0:T(8,128)(2,1)S(1)}, u32[]{:S(2)}) copy-start(bf16[8,256,128]{2,1,0:T(8,128)(2,1)S(1)} %all-to-all-done.2.src_ref) | copy-start | bytes 1572868
  142.5 14.0 %all-to-all-start.5 = ((bf16[32,32,128]{2,1,0:T(8,128)(2,1)}), bf16[32,32,128]{2,1,0:T(8,128)(2,1)S(1)}, u32[]{:S(2)}, u32[]{:S(2)}) async-start(bf16[32,32,128]{2,1,0:T(8,128)(2,1)} %broadcast_in_dim.26), calls=%async_computation.5 | async-start | bytes 524288 | tf_op jit(solution)/shard_map/all_to_all | solution.py:151

commit v12 on v8

--- a/solution.py
+++ b/solution.py
@@ -210,12 +210,11 @@
     arrived = scatter_blocks(packed, "row")
     returned_t = jnp.sum(arrived[:, BLOCK:].astype(f32), axis=0)
 
-    hp = lax.Precision.HIGHEST
     combined = cotangent.astype(f32) + returned_t.T
-    hidden_grad = jnp.dot(combined, second_weight.astype(f32).T, precision=hp, preferred_element_type=f32)
+    hidden_grad = jnp.dot(combined.astype(bf16), second_weight.T, preferred_element_type=f32)
     pre_grad = (hidden_grad * gelu_slope(first_pre)).astype(bf16)
     first_term = jnp.dot(first_mix.T, pre_grad, preferred_element_type=f32)
-    second_term = jnp.dot(hidden.astype(f32).T, combined, precision=hp, preferred_element_type=f32)
+    second_term = jnp.dot(hidden.T, combined.astype(bf16), preferred_element_type=f32)
     node_scale = 1.0 / math.sqrt(node_count * n_rows_axis * n_cols_axis)
     flat = jnp.concatenate([first_term.reshape(-1), second_term.reshape(-1)]) * node_scale
     slices = flat.reshape(row_groups, -1, BLOCK)

time: 155 us -> 155 us (level)
  no operation moved by 1% of the time
where the time goes in v12:
time: 155 us; the launch traced here: 154 us
  waiting for transfers between devices  57.6 us (37%)
  blocking collectives  38.5 us (25%)
  starting transfers between devices  27.8 us (18%)
  Pallas kernels  11.4 us (7%)
  local copies, waits for them, and re-layouts  8.83 us (6%)
  matrix products  4.23 us (3%)
  other arithmetic  4.06 us (3%)
  between operations  1.56 us (1%)
    all_to_all x2, waiting for transfers between devices, scatter_blocks(): return lax.all_to_all(blocks, axis, 0, 0, tiled=False)  47.4 us
    all_to_all x1, blocking collectives, scatter_blocks(): return lax.all_to_all(blocks, axis, 0, 0, tiled=False)  28.9 us
    all_to_all x2, starting transfers between devices, gather_blocks(): lax.all_to_all(jnp.broadcast_to(block[None], (n,) + block.shape), axis, 0...  14 us
    all_to_all x2, starting transfers between devices, scatter_blocks(): return lax.all_to_all(blocks, axis, 0, 0, tiled=False)  13.8 us
    pallas_call x3, Pallas kernels, _aggregate_into(): pl.pallas_call(functools.partial(kernel, row_offset, src_offset), out_sha...  11.4 us
    all_to_all x2, waiting for transfers between devices, gather_blocks(): lax.all_to_all(jnp.broadcast_to(block[None], (n,) + block.shape), axis, 0...  10.3 us
    all_to_all x1, blocking collectives, gather_blocks(): lax.all_to_all(jnp.broadcast_to(block[None], (n,) + block.shape), axis, 0...  9.53 us
    dot_general x1, matrix products, local(): jnp.einsum('sij,sj->si', tiles, live_mask, preferred_element_type=f32)  3.17 us
  transfers between devices with their start and end apart: 4, of which 4 were waited for; matrix products, arithmetic and copies ran while one was open for 6% of the time, Pallas kernels for 0%

profile of v12, /device:TPU:1, one launch (start us, length us, event | category | flops | bytes accessed | tf_op | source)
XLA Modules:
  0.0 153.9 jit_solution(7726579717179349794)
XLA Ops:
  0.6 0.0 copy-start
  0.6 0.0 copy-start.6
  0.7 1.5 broadcast_in_dim.12
  2.2 9.0 %all-to-all-start = ((bf16[8,128,128]{2,1,0:T(8,128)(2,1)}), bf16[8,128,128]{2,1,0:T(8,128)(2,1)S(1)}, u32[]{:S(2)}, u32[]{:S(2)}) async-start(bf16[8,128,128]{2,1,0:T(8,128)(2,1)} %broadcast_in_dim.12), calls=%async_computation | async-start | bytes 524288 | tf_op jit(solution)/shard_map/all_to_all | solution.py:139
  11.9 0.9 fusion.25
  12.7 0.7 fusion.28
  13.4 3.2 %fusion.23 = f32[80,1,128]{2,1,0:T(1,128)S(1)} fusion(bf16[80,128,1]{1,0,2:T(8,128)(2,1)S(1)} %fusion.25, bf16[1,1,80,128,128]{4,3,2,1,0:T(8,128)(2,1)} %param.16), kind=kOutput, calls=%fused_computation.36 | convolution fusion | flops 2621440 | bytes 2682880 | tf_op jit(solution)/shard_map/sij,sj->si/dot_general | solution.py:180
  16.6 0.9 scatter_custom_fusion
  17.5 0.1 copy.21
  17.6 0.0 copy-done.6
  17.6 0.1 pad_maximum_fusion
  17.7 0.1 copy.22
  17.8 0.2 broadcast_in_dim.14
  18.0 1.6 %concatenate.21.into_ref = bf16[32,288,128]{2,1,0:T(8,128)(2,1)} pad(bf16[32,160,128]{2,1,0:T(8,128)(2,1)S(1)} %broadcast_in_dim.14, bf16[]{:T(256)} %constant.6.clone.1), padding=0_0x128_0x0_0 | pad | bytes 3670018 | tf_op jit(solution)/shard_map/concatenate | solution.py:183
  19.6 2.1 %all-to-all-done.src_ref = bf16[8,128,128]{2,1,0:T(8,128)(2,1)S(1)} async-done(((bf16[8,128,128]{2,1,0:T(8,128)(2,1)}), bf16[8,128,128]{2,1,0:T(8,128)(2,1)S(1)}, u32[]{:S(2)}, u32[]{:S(2)}) %all-to-all-start) | async-done | bytes 262176 | tf_op jit(solution)/shard_map/all_to_all | solution.py:139
  21.7 0.0 copy-start.3
  21.7 0.7 copy-done.3
  22.4 3.7 %shard_map.112 = bf16[32,288,128]{2,1,0:T(8,128)(2,1)} custom-call(s32[1]{0:T(128)} %bitcast.34.live_ref, s32[80]{0:T(128)} %bitcast.47, s32[80]{0:T(128)} %bitcast.50, bf16[80,128,128]{2,1,0:T(8,128)(2,1)} %bitcast.37, s32[80,128]{1,0:T(8,128)} %bitcast.40, bf16[8,128,128]{2,1,0:T(8,128)(2,1)} %copy-done.3, ...), custom_call_target="tpu_custom_call", output_to_operand_aliasing={{}: (6, {})} | custom-call | flops 335544320 | bytes 3932160 | tf_op jit(solution)/shard_map/pallas_call | solution.py:106
  26.1 0.0 copy-start.5
  26.1 0.0 copy-start.4
  26.1 10.3 %all-to-all-start.1 = ((bf16[32,288,128]{2,1,0:T(8,128)(2,1)}), bf16[32,288,128]{2,1,0:T(8,128)(2,1)S(1)}, u32[]{:S(2)}, u32[]{:S(2)}) async-start(bf16[32,288,128]{2,1,0:T(8,128)(2,1)} %shard_map.112), calls=%async_computation.1 | async-start | bytes 4718592 | tf_op jit(solution)/shard_map/all_to_all | solution.py:143
  36.4 31.5 %all-to-all-done.1.src_ref = bf16[32,288,128]{2,1,0:T(8,128)(2,1)S(1)} async-done(((bf16[32,288,128]{2,1,0:T(8,128)(2,1)}), bf16[32,288,128]{2,1,0:T(8,128)(2,1)S(1)}, u32[]{:S(2)}, u32[]{:S(2)}) %all-to-all-start.1) | async-done | bytes 2359328 | tf_op jit(solution)/shard_map/all_to_all | solution.py:143
  67.9 0.0 copy-start.1
  68.0 0.0 copy-start.7
  68.0 0.2 convert_reduce_fusion
  68.2 0.0 copy-done.5
  68.2 0.1 add_convert_fusion.1
  68.3 0.0 copy-done.4
  68.3 0.2 fusion.42
  68.5 0.0 copy-done
  68.5 0.2 fusion.41
  68.7 0.9 concatenate.22.into_ref
  69.6 0.0 copy-done.1
  69.6 0.0 copy-done.7
  69.6 3.9 %shard_map.113 = bf16[8,256,128]{2,1,0:T(8,128)(2,1)} custom-call(s32[1]{0:T(128)} %bitcast.35.live_ref, s32[80]{0:T(128)} %bitcast.48, s32[80]{0:T(128)} %bitcast.51, bf16[80,128,128]{2,1,0:T(8,128)(2,1)} %bitcast.38, s32[80,128]{1,0:T(8,128)} %bitcast.41, bf16[32,288,128]{2,1,0:T(8,128)(2,1)} %copy-done.1, ...), custom_call_target="tpu_custom_call", output_to_operand_aliasing={{}: (7, {})} | custom-call | flops 335544320 | bytes 3932160 | tf_op jit(solution)/shard_map/pallas_call | solution.py:106
  73.6 3.5 %all-to-all-start.2 = ((bf16[8,256,128]{2,1,0:T(8,128)(2,1)}), bf16[8,256,128]{2,1,0:T(8,128)(2,1)S(1)}, u32[]{:S(2)}, u32[]{:S(2)}) async-start(bf16[8,256,128]{2,1,0:T(8,128)(2,1)} %shard_map.113), calls=%async_computation.2 | async-start | bytes 1048576 | tf_op jit(solution)/shard_map/all_to_all | solution.py:143
  77.1 0.1 copy.23
  77.2 15.9 %all-to-all-done.2.src_ref = bf16[8,256,128]{2,1,0:T(8,128)(2,1)S(1)} async-done(((bf16[8,256,128]{2,1,0:T(8,128)(2,1)}), bf16[8,256,128]{2,1,0:T(8,128)(2,1)S(1)}, u32[]{:S(2)}, u32[]{:S(2)}) %all-to-all-start.2) | async-done | bytes 524320 | tf_op jit(solution)/shard_map/all_to_all | solution.py:143
  93.0 0.0 copy-start.2
  93.1 0.4 fusion.1
  93.5 0.3 fusion.35
  93.8 0.1 fusion.2
  93.9 1.2 concatenate.26.into_ref
  95.1 0.0 copy-done.2
  95.1 3.7 %shard_map.114 = bf16[32,160,128]{2,1,0:T(8,128)(2,1)} custom-call(s32[1]{0:T(128)} %bitcast.36.live_ref, s32[80]{0:T(128)} %bitcast.49, s32[80]{0:T(128)} %bitcast.52, bf16[80,128,128]{2,1,0:T(8,128)(2,1)} %bitcast.39, s32[80,128]{1,0:T(8,128)} %bitcast.42, bf16[8,256,128]{2,1,0:T(8,128)(2,1)} %copy-done.2, ...), custom_call_target="tpu_custom_call", output_to_operand_aliasing={{}: (6, {})} | custom-call | flops 335544320 | bytes 3932160 | tf_op jit(solution)/shard_map/pallas_call | solution.py:106
  98.8 28.9 %all_to_all.30 = bf16[32,160,128]{2,1,0:T(8,128)(2,1)S(1)} all-to-all(bf16[32,160,128]{2,1,0:T(8,128)(2,1)} %shard_map.114), channel_id=1, replica_groups=mesh['row'=8,'col'=32] {'col'}, dimensions={0} | all-to-all | bytes 2621440 | tf_op jit(solution)/shard_map/all_to_all | solution.py:143
  127.8 0.3 convert_element_type.79
  128.2 9.5 %all_to_all.31 = bf16[8,32,128]{2,1,0:T(8,128)(2,1)S(1)} all-to-all(bf16[8,32,128]{2,1,0:T(8,128)(2,1)S(1)} %broadcast_in_dim.16), channel_id=1, replica_groups=mesh['row'=8,'col'=32] {'row'}, dimensions={0} | all-to-all | bytes 131072 | tf_op jit(solution)/shard_map/all_to_all | solution.py:139
  137.7 0.7 broadcast_in_dim.17
  138.4 5.0 %all-to-all-start.5 = ((bf16[32,32,128]{2,1,0:T(8,128)(2,1)}), bf16[32,32,128]{2,1,0:T(8,128)(2,1)S(1)}, u32[]{:S(2)}, u32[]{:S(2)}) async-start(bf16[32,32,128]{2,1,0:T(8,128)(2,1)} %broadcast_in_dim.17), calls=%async_computation.5 | async-start | bytes 524288 | tf_op jit(solution)/shard_map/all_to_all | solution.py:139
  143.4 0.1 slice_reduce_fusion
  143.5 0.7 add_convert_fusion
  144.3 8.2 %all-to-all-done.5 = bf16[32,32,128]{2,1,0:T(8,128)(2,1)S(1)} async-done(((bf16[32,32,128]{2,1,0:T(8,128)(2,1)}), bf16[32,32,128]{2,1,0:T(8,128)(2,1)S(1)}, u32[]{:S(2)}, u32[]{:S(2)}) %all-to-all-start.5) | async-done | bytes 262176 | tf_op jit(solution)/shard_map/all_to_all | solution.py:139
  152.4 0.8 fusion.40
  153.2 0.7 reshape.68
  (11 shorter events, 0.2 us)
Async XLA Ops:
  0.6 67.8 %copy-start = (bf16[512,128]{1,0:T(8,128)(2,1)S(1)}, bf16[512,128]{1,0:T(8,128)(2,1)}, u32[]{:S(2)}) copy-start(bf16[512,128]{1,0:T(8,128)(2,1)} %param.11) | copy-start | bytes 393220
  0.6 16.9 %copy-start.6 = (bf16[128,128]{1,0:T(8,128)(2,1)S(1)}, bf16[128,128]{1,0:T(8,128)(2,1)}, u32[]{:S(2)}) copy-start(bf16[128,128]{1,0:T(8,128)(2,1)} %param.17) | copy-start | bytes 98308
  2.2 19.5 %all-to-all-start = ((bf16[8,128,128]{2,1,0:T(8,128)(2,1)}), bf16[8,128,128]{2,1,0:T(8,128)(2,1)S(1)}, u32[]{:S(2)}, u32[]{:S(2)}) async-start(bf16[8,128,128]{2,1,0:T(8,128)(2,1)} %broadcast_in_dim.12), calls=%async_computation | async-start | bytes 524288 | tf_op jit(solution)/shard_map/all_to_all | solution.py:139
  21.7 0.7 copy-start.3
  26.1 42.1 %copy-start.5 = (bf16[128,128]{1,0:T(8,128)(2,1)S(1)}, bf16[128,128]{1,0:T(8,128)(2,1)}, u32[]{:S(2)}) copy-start(bf16[128,128]{1,0:T(8,128)(2,1)} %param.9) | copy-start | bytes 98308
  26.1 42.2 %copy-start.4 = (bf16[128,512]{1,0:T(8,128)(2,1)S(1)}, bf16[128,512]{1,0:T(8,128)(2,1)}, u32[]{:S(2)}) copy-start(bf16[128,512]{1,0:T(8,128)(2,1)} %param.10) | copy-start | bytes 393220
  26.1 41.8 %all-to-all-start.1 = ((bf16[32,288,128]{2,1,0:T(8,128)(2,1)}), bf16[32,288,128]{2,1,0:T(8,128)(2,1)S(1)}, u32[]{:S(2)}, u32[]{:S(2)}) async-start(bf16[32,288,128]{2,1,0:T(8,128)(2,1)} %shard_map.112), calls=%async_computation.1 | async-start | bytes 4718592 | tf_op jit(solution)/shard_map/all_to_all | solution.py:143
  67.9 1.7 %copy-start.1 = (bf16[32,288,128]{2,1,0:T(8,128)(2,1)}, bf16[32,288,128]{2,1,0:T(8,128)(2,1)S(1)}, u32[]{:S(2)}) copy-start(bf16[32,288,128]{2,1,0:T(8,128)(2,1)S(1)} %all-to-all-done.1.src_ref) | copy-start | bytes 7077892
  68.0 1.6 %copy-start.7 = (f32[32,128]{1,0:T(8,128)}, f32[32,128]{1,0:T(8,128)S(1)}, u32[]{:S(2)}) copy-start(f32[32,128]{1,0:T(8,128)S(1)} %add_rsqrt_fusion.scale_ref) | copy-start | bytes 49156
  73.6 19.5 %all-to-all-start.2 = ((bf16[8,256,128]{2,1,0:T(8,128)(2,1)}), bf16[8,256,128]{2,1,0:T(8,128)(2,1)S(1)}, u32[]{:S(2)}, u32[]{:S(2)}) async-start(bf16[8,256,128]{2,1,0:T(8,128)(2,1)} %shard_map.113), calls=%async_computation.2 | async-start | bytes 1048576 | tf_op jit(solution)/shard_map/all_to_all | solution.py:143
  93.0 2.1 %copy-start.2 = (bf16[8,256,128]{2,1,0:T(8,128)(2,1)}, bf16[8,256,128]{2,1,0:T(8,128)(2,1)S(1)}, u32[]{:S(2)}) copy-start(bf16[8,256,128]{2,1,0:T(8,128)(2,1)S(1)} %all-to-all-done.2.src_ref) | copy-start | bytes 1572868
  138.4 14.0 %all-to-all-start.5 = ((bf16[32,32,128]{2,1,0:T(8,128)(2,1)}), bf16[32,32,128]{2,1,0:T(8,128)(2,1)S(1)}, u32[]{:S(2)}, u32[]{:S(2)}) async-start(bf16[32,32,128]{2,1,0:T(8,128)(2,1)} %broadcast_in_dim.17), calls=%async_computation.5 | async-start | bytes 524288 | tf_op jit(solution)/shard_map/all_to_all | solution.py:139

commit v13 on v12

--- a/solution.py
+++ b/solution.py
@@ -25,7 +25,7 @@
     )
 
 
-UNROLL = 16
+UNROLL = 20
 
 
 def _slot(k, u, n_live, slots):

time: 155 us -> 154 us (level)
  no operation moved by 1% of the time
where the time goes in v13:
time: 154 us
  waiting for transfers between devices  57.2 us (37%)
  blocking collectives  39.1 us (25%)
  starting transfers between devices  27.9 us (18%)
  Pallas kernels  10.5 us (7%)
  local copies, waits for them, and re-layouts  8.83 us (6%)
  matrix products  4.23 us (3%)
  other arithmetic  4.06 us (3%)
  between operations  1.56 us (1%)
    all_to_all x2, waiting for transfers between devices, scatter_blocks(): return lax.all_to_all(blocks, axis, 0, 0, tiled=False)  47 us
    all_to_all x1, blocking collectives, scatter_blocks(): return lax.all_to_all(blocks, axis, 0, 0, tiled=False)  29.6 us
    all_to_all x2, starting transfers between devices, gather_blocks(): lax.all_to_all(jnp.broadcast_to(block[None], (n,) + block.shape), axis, 0...  14 us
    all_to_all x2, starting transfers between devices, scatter_blocks(): return lax.all_to_all(blocks, axis, 0, 0, tiled=False)  13.9 us
    pallas_call x3, Pallas kernels, _aggregate_into(): pl.pallas_call(functools.partial(kernel, row_offset, src_offset), out_sha...  10.5 us
    all_to_all x2, waiting for transfers between devices, gather_blocks(): lax.all_to_all(jnp.broadcast_to(block[None], (n,) + block.shape), axis, 0...  10.3 us
    all_to_all x1, blocking collectives, gather_blocks(): lax.all_to_all(jnp.broadcast_to(block[None], (n,) + block.shape), axis, 0...  9.53 us
    dot_general x1, matrix products, local(): jnp.einsum('sij,sj->si', tiles, live_mask, preferred_element_type=f32)  3.17 us
  transfers between devices with their start and end apart: 4, of which 4 were waited for; matrix products, arithmetic and copies ran while one was open for 6% of the time, Pallas kernels for 0%

profile of v13, /device:TPU:1, one launch (start us, length us, event | category | flops | bytes accessed | tf_op | source)
XLA Modules:
  0.0 153.5 jit_solution(13038637315314293820)
XLA Ops:
  0.6 0.0 copy-start
  0.6 0.0 copy-start.6
  0.7 1.5 broadcast_in_dim.12
  2.2 9.0 %all-to-all-start = ((bf16[8,128,128]{2,1,0:T(8,128)(2,1)}), bf16[8,128,128]{2,1,0:T(8,128)(2,1)S(1)}, u32[]{:S(2)}, u32[]{:S(2)}) async-start(bf16[8,128,128]{2,1,0:T(8,128)(2,1)} %broadcast_in_dim.12), calls=%async_computation | async-start | bytes 524288 | tf_op jit(solution)/shard_map/all_to_all | solution.py:139
  11.9 0.9 fusion.25
  12.7 0.7 fusion.28
  13.4 3.2 %fusion.23 = f32[80,1,128]{2,1,0:T(1,128)S(1)} fusion(bf16[80,128,1]{1,0,2:T(8,128)(2,1)S(1)} %fusion.25, bf16[1,1,80,128,128]{4,3,2,1,0:T(8,128)(2,1)} %param.16), kind=kOutput, calls=%fused_computation.36 | convolution fusion | flops 2621440 | bytes 2682880 | tf_op jit(solution)/shard_map/sij,sj->si/dot_general | solution.py:180
  16.6 0.9 scatter_custom_fusion
  17.5 0.1 copy.21
  17.6 0.0 copy-done.6
  17.6 0.1 pad_maximum_fusion
  17.7 0.1 copy.22
  17.8 0.2 broadcast_in_dim.14
  18.0 1.6 %concatenate.21.into_ref = bf16[32,288,128]{2,1,0:T(8,128)(2,1)} pad(bf16[32,160,128]{2,1,0:T(8,128)(2,1)S(1)} %broadcast_in_dim.14, bf16[]{:T(256)} %constant.6.clone.1), padding=0_0x128_0x0_0 | pad | bytes 3670018 | tf_op jit(solution)/shard_map/concatenate | solution.py:183
  19.6 2.1 %all-to-all-done.src_ref = bf16[8,128,128]{2,1,0:T(8,128)(2,1)S(1)} async-done(((bf16[8,128,128]{2,1,0:T(8,128)(2,1)}), bf16[8,128,128]{2,1,0:T(8,128)(2,1)S(1)}, u32[]{:S(2)}, u32[]{:S(2)}) %all-to-all-start) | async-done | bytes 262176 | tf_op jit(solution)/shard_map/all_to_all | solution.py:139
  21.7 0.0 copy-start.3
  21.7 0.7 copy-done.3
  22.4 3.4 %shard_map.112 = bf16[32,288,128]{2,1,0:T(8,128)(2,1)} custom-call(s32[1]{0:T(128)} %bitcast.34.live_ref, s32[80]{0:T(128)} %bitcast.47, s32[80]{0:T(128)} %bitcast.50, bf16[80,128,128]{2,1,0:T(8,128)(2,1)} %bitcast.37, s32[80,128]{1,0:T(8,128)} %bitcast.40, bf16[8,128,128]{2,1,0:T(8,128)(2,1)} %copy-done.3, ...), custom_call_target="tpu_custom_call", output_to_operand_aliasing={{}: (6, {})} | custom-call | flops 335544320 | bytes 3932160 | tf_op jit(solution)/shard_map/pallas_call | solution.py:106
  25.8 0.0 copy-start.5
  25.8 0.0 copy-start.4
  25.8 10.4 %all-to-all-start.1 = ((bf16[32,288,128]{2,1,0:T(8,128)(2,1)}), bf16[32,288,128]{2,1,0:T(8,128)(2,1)S(1)}, u32[]{:S(2)}, u32[]{:S(2)}) async-start(bf16[32,288,128]{2,1,0:T(8,128)(2,1)} %shard_map.112), calls=%async_computation.1 | async-start | bytes 4718592 | tf_op jit(solution)/shard_map/all_to_all | solution.py:143
  36.3 31.5 %all-to-all-done.1.src_ref = bf16[32,288,128]{2,1,0:T(8,128)(2,1)S(1)} async-done(((bf16[32,288,128]{2,1,0:T(8,128)(2,1)}), bf16[32,288,128]{2,1,0:T(8,128)(2,1)S(1)}, u32[]{:S(2)}, u32[]{:S(2)}) %all-to-all-start.1) | async-done | bytes 2359328 | tf_op jit(solution)/shard_map/all_to_all | solution.py:143
  67.8 0.0 copy-start.1
  67.9 0.0 copy-start.7
  67.9 0.2 convert_reduce_fusion
  68.0 0.0 copy-done.5
  68.1 0.1 add_convert_fusion.1
  68.1 0.0 copy-done.4
  68.2 0.2 fusion.42
  68.3 0.0 copy-done
  68.3 0.2 fusion.41
  68.6 0.9 concatenate.22.into_ref
  69.5 0.0 copy-done.1
  69.5 0.0 copy-done.7
  69.5 3.7 %shard_map.113 = bf16[8,256,128]{2,1,0:T(8,128)(2,1)} custom-call(s32[1]{0:T(128)} %bitcast.35.live_ref, s32[80]{0:T(128)} %bitcast.48, s32[80]{0:T(128)} %bitcast.51, bf16[80,128,128]{2,1,0:T(8,128)(2,1)} %bitcast.38, s32[80,128]{1,0:T(8,128)} %bitcast.41, bf16[32,288,128]{2,1,0:T(8,128)(2,1)} %copy-done.1, ...), custom_call_target="tpu_custom_call", output_to_operand_aliasing={{}: (7, {})} | custom-call | flops 335544320 | bytes 3932160 | tf_op jit(solution)/shard_map/pallas_call | solution.py:106
  73.1 3.5 %all-to-all-start.2 = ((bf16[8,256,128]{2,1,0:T(8,128)(2,1)}), bf16[8,256,128]{2,1,0:T(8,128)(2,1)S(1)}, u32[]{:S(2)}, u32[]{:S(2)}) async-start(bf16[8,256,128]{2,1,0:T(8,128)(2,1)} %shard_map.113), calls=%async_computation.2 | async-start | bytes 1048576 | tf_op jit(solution)/shard_map/all_to_all | solution.py:143
  76.7 0.1 copy.23
  76.8 15.5 %all-to-all-done.2.src_ref = bf16[8,256,128]{2,1,0:T(8,128)(2,1)S(1)} async-done(((bf16[8,256,128]{2,1,0:T(8,128)(2,1)}), bf16[8,256,128]{2,1,0:T(8,128)(2,1)S(1)}, u32[]{:S(2)}, u32[]{:S(2)}) %all-to-all-start.2) | async-done | bytes 524320 | tf_op jit(solution)/shard_map/all_to_all | solution.py:143
  92.3 0.0 copy-start.2
  92.3 0.4 fusion.1
  92.7 0.3 fusion.35
  93.0 0.1 fusion.2
  93.1 1.2 concatenate.26.into_ref
  94.3 0.0 copy-done.2
  94.3 3.5 %shard_map.114 = bf16[32,160,128]{2,1,0:T(8,128)(2,1)} custom-call(s32[1]{0:T(128)} %bitcast.36.live_ref, s32[80]{0:T(128)} %bitcast.49, s32[80]{0:T(128)} %bitcast.52, bf16[80,128,128]{2,1,0:T(8,128)(2,1)} %bitcast.39, s32[80,128]{1,0:T(8,128)} %bitcast.42, bf16[8,256,128]{2,1,0:T(8,128)(2,1)} %copy-done.2, ...), custom_call_target="tpu_custom_call", output_to_operand_aliasing={{}: (6, {})} | custom-call | flops 335544320 | bytes 3932160 | tf_op jit(solution)/shard_map/pallas_call | solution.py:106
  97.8 29.6 %all_to_all.30 = bf16[32,160,128]{2,1,0:T(8,128)(2,1)S(1)} all-to-all(bf16[32,160,128]{2,1,0:T(8,128)(2,1)} %shard_map.114), channel_id=1, replica_groups=mesh['row'=8,'col'=32] {'col'}, dimensions={0} | all-to-all | bytes 2621440 | tf_op jit(solution)/shard_map/all_to_all | solution.py:143
  127.4 0.3 convert_element_type.79
  127.8 9.5 %all_to_all.31 = bf16[8,32,128]{2,1,0:T(8,128)(2,1)S(1)} all-to-all(bf16[8,32,128]{2,1,0:T(8,128)(2,1)S(1)} %broadcast_in_dim.16), channel_id=1, replica_groups=mesh['row'=8,'col'=32] {'row'}, dimensions={0} | all-to-all | bytes 131072 | tf_op jit(solution)/shard_map/all_to_all | solution.py:139
  137.3 0.7 broadcast_in_dim.17
  138.0 5.0 %all-to-all-start.5 = ((bf16[32,32,128]{2,1,0:T(8,128)(2,1)}), bf16[32,32,128]{2,1,0:T(8,128)(2,1)S(1)}, u32[]{:S(2)}, u32[]{:S(2)}) async-start(bf16[32,32,128]{2,1,0:T(8,128)(2,1)} %broadcast_in_dim.17), calls=%async_computation.5 | async-start | bytes 524288 | tf_op jit(solution)/shard_map/all_to_all | solution.py:139
  143.0 0.1 slice_reduce_fusion
  143.2 0.7 add_convert_fusion
  143.9 8.2 %all-to-all-done.5 = bf16[32,32,128]{2,1,0:T(8,128)(2,1)S(1)} async-done(((bf16[32,32,128]{2,1,0:T(8,128)(2,1)}), bf16[32,32,128]{2,1,0:T(8,128)(2,1)S(1)}, u32[]{:S(2)}, u32[]{:S(2)}) %all-to-all-start.5) | async-done | bytes 262176 | tf_op jit(solution)/shard_map/all_to_all | solution.py:139
  152.0 0.8 fusion.40
  152.8 0.7 reshape.68
  (11 shorter events, 0.2 us)
Async XLA Ops:
  0.6 67.7 %copy-start = (bf16[512,128]{1,0:T(8,128)(2,1)S(1)}, bf16[512,128]{1,0:T(8,128)(2,1)}, u32[]{:S(2)}) copy-start(bf16[512,128]{1,0:T(8,128)(2,1)} %param.11) | copy-start | bytes 393220
  0.6 16.9 %copy-start.6 = (bf16[128,128]{1,0:T(8,128)(2,1)S(1)}, bf16[128,128]{1,0:T(8,128)(2,1)}, u32[]{:S(2)}) copy-start(bf16[128,128]{1,0:T(8,128)(2,1)} %param.17) | copy-start | bytes 98308
  2.2 19.5 %all-to-all-start = ((bf16[8,128,128]{2,1,0:T(8,128)(2,1)}), bf16[8,128,128]{2,1,0:T(8,128)(2,1)S(1)}, u32[]{:S(2)}, u32[]{:S(2)}) async-start(bf16[8,128,128]{2,1,0:T(8,128)(2,1)} %broadcast_in_dim.12), calls=%async_computation | async-start | bytes 524288 | tf_op jit(solution)/shard_map/all_to_all | solution.py:139
  21.7 0.7 copy-start.3
  25.8 42.2 %copy-start.5 = (bf16[128,128]{1,0:T(8,128)(2,1)S(1)}, bf16[128,128]{1,0:T(8,128)(2,1)}, u32[]{:S(2)}) copy-start(bf16[128,128]{1,0:T(8,128)(2,1)} %param.9) | copy-start | bytes 98308
  25.8 42.3 %copy-start.4 = (bf16[128,512]{1,0:T(8,128)(2,1)S(1)}, bf16[128,512]{1,0:T(8,128)(2,1)}, u32[]{:S(2)}) copy-start(bf16[128,512]{1,0:T(8,128)(2,1)} %param.10) | copy-start | bytes 393220
  25.8 42.0 %all-to-all-start.1 = ((bf16[32,288,128]{2,1,0:T(8,128)(2,1)}), bf16[32,288,128]{2,1,0:T(8,128)(2,1)S(1)}, u32[]{:S(2)}, u32[]{:S(2)}) async-start(bf16[32,288,128]{2,1,0:T(8,128)(2,1)} %shard_map.112), calls=%async_computation.1 | async-start | bytes 4718592 | tf_op jit(solution)/shard_map/all_to_all | solution.py:143
  67.8 1.7 %copy-start.1 = (bf16[32,288,128]{2,1,0:T(8,128)(2,1)}, bf16[32,288,128]{2,1,0:T(8,128)(2,1)S(1)}, u32[]{:S(2)}) copy-start(bf16[32,288,128]{2,1,0:T(8,128)(2,1)S(1)} %all-to-all-done.1.src_ref) | copy-start | bytes 7077892
  67.9 1.6 %copy-start.7 = (f32[32,128]{1,0:T(8,128)}, f32[32,128]{1,0:T(8,128)S(1)}, u32[]{:S(2)}) copy-start(f32[32,128]{1,0:T(8,128)S(1)} %add_rsqrt_fusion.scale_ref) | copy-start | bytes 49156
  73.1 19.1 %all-to-all-start.2 = ((bf16[8,256,128]{2,1,0:T(8,128)(2,1)}), bf16[8,256,128]{2,1,0:T(8,128)(2,1)S(1)}, u32[]{:S(2)}, u32[]{:S(2)}) async-start(bf16[8,256,128]{2,1,0:T(8,128)(2,1)} %shard_map.113), calls=%async_computation.2 | async-start | bytes 1048576 | tf_op jit(solution)/shard_map/all_to_all | solution.py:143
  92.3 2.1 %copy-start.2 = (bf16[8,256,128]{2,1,0:T(8,128)(2,1)}, bf16[8,256,128]{2,1,0:T(8,128)(2,1)S(1)}, u32[]{:S(2)}) copy-start(bf16[8,256,128]{2,1,0:T(8,128)(2,1)S(1)} %all-to-all-done.2.src_ref) | copy-start | bytes 1572868
  138.0 14.0 %all-to-all-start.5 = ((bf16[32,32,128]{2,1,0:T(8,128)(2,1)}), bf16[32,32,128]{2,1,0:T(8,128)(2,1)S(1)}, u32[]{:S(2)}, u32[]{:S(2)}) async-start(bf16[32,32,128]{2,1,0:T(8,128)(2,1)} %broadcast_in_dim.17), calls=%async_computation.5 | async-start | bytes 524288 | tf_op jit(solution)/shard_map/all_to_all | solution.py:139
